TPU v7x, 512 devices: a whole 4x8x8 slice. The times are simulated.
512 devices in a mesh: seq: 16 (over z, core), expert: 32 (over x, y).
Axes of the slice: x: 4, y: 8, z: 8, core: 2. Of those that a mesh axis runs over, the one named last changes fastest.
Arguments:
- hidden: bfloat16 [32, 1024, 2048], P('expert', 'seq'), may hold values from -6 to 6
- queries: bfloat16 [32, 1024, 4608], P('expert', 'seq'), may hold values from -5 to 5
- suffix_latent: bfloat16 [32, 1024, 576], P('expert', 'seq'), may hold values from -6 to 6
- prefix_latent: bfloat16 [2, 1024, 576], P(None, 'seq'), may hold values from -6 to 6
- lengths: int32 [32, 4], P('expert'), may hold values from 1 to 512, 1024 in all within a row
- prefix_of: int32 [32, 4], P('expert'), may hold values from 0 to 1
- value_up: bfloat16 [8, 512, 128], replicated, may hold values from -1 to 1
- out_proj: bfloat16 [1024, 2048], P(None, 'expert'), may hold values from -0.1875 to 0.1875
- norm_gain: float32 [2048], replicated, may hold values from 0.5 to 1.5
- router: bfloat16 [2048, 32], replicated, may hold values from -0.0625 to 0.0625
- routes: int32 [32, 1024, 6], P('expert', 'seq'), may hold values from 0 to 31, all different within a row; in each aligned block of 64 rows (0 to 63, 64 to 127, ..., all dimensions but the last counted through in order) at most 16 rows name the same one
- expert_in: bfloat16 [32, 2048, 1408], P('expert', 'seq'), may hold values from -0.125 to 0.125
- expert_out: bfloat16 [32, 2048, 704], P('expert', 'seq'), may hold values from -1.25 to 1.25
Outputs:
- layer_out: bfloat16 [32, 1024, 2048], P('expert', 'seq')
Inputs may be any that keep to these rules, and one draw needn't show every extreme that they name: `routes`: among the rows of one device (aligned blocks of 64 tokens) no expert is named more than 16 times, a bound that some block reaches; a token's 6 experts differ. `lengths`: each row sums to 1024; its longest request has exactly 512 tokens.
All inputs are finite; a program needn't handle non-finite values.
Results may differ from a plain program's by a relative error of at most 0.013.
Values may be sent and summed in bfloat16 or wider, within the bound.
No kernel may reach another device: no remote copies, remote signals or barrier semaphores. Data moves between devices by JAX's collectives and lax.ppermute only.
A program may use at most 128 MiB of HBM per device.

v0:
```python
import jax
import jax.numpy as jnp
from jax import lax
from jax.sharding import PartitionSpec as P

qk_scale = 192.0 ** (-0.5)
big_negative = -1e30


def request_of(positions, request_ends):
    return jnp.sum((positions[:, None] >= request_ends[None, :]).astype(jnp.int32), axis=1)


def merge_scores(running, scores, allowed, values):
    running_max, running_sum, running_acc = running
    new_max = jnp.maximum(running_max, jnp.max(jnp.where(allowed, scores, big_negative), axis=2))
    weights = jnp.where(allowed, jnp.exp(scores - new_max[:, :, None]), 0.0)
    new_sum = jnp.sum(weights, axis=2)
    new_acc = jnp.einsum(
        "thn,nl->thl", weights.astype(jnp.bfloat16), values, preferred_element_type=jnp.float32
    )
    return (new_max, new_sum, new_acc)


def local(
    hidden,
    queries,
    suffix_latent,
    prefix_latent,
    lengths,
    prefix_of,
    value_up,
    out_proj,
    norm_gain,
    router,
    routes,
    expert_in,
    expert_out,
):
    local_tokens = hidden.shape[1]
    model_width = hidden.shape[2]
    key_width = suffix_latent.shape[2]
    head_count = value_up.shape[0]
    latent_width = value_up.shape[1]
    expert_count = router.shape[1]
    top_count = routes.shape[2]
    capacity = 4 * local_tokens * top_count // (3 * expert_count)
    request_count = lengths.shape[1]
    request_ends = jnp.cumsum(lengths[0])
    my_positions = lax.axis_index("seq") * local_tokens + jnp.arange(local_tokens, dtype=jnp.int32)
    my_requests = request_of(my_positions, request_ends)
    request_ids = jnp.arange(request_count, dtype=jnp.int32)
    chosen = jnp.sum(
        jnp.where(my_requests[:, None] == request_ids[None, :], prefix_of[0][None, :], 0), axis=1
    )
    prefix_pick = chosen[:, None] == jnp.arange(2, dtype=jnp.int32)[None, :]
    single_prefix = jnp.all(chosen == chosen[0])
    my_prefix = chosen[0]
    query_rows = queries[0].reshape(local_tokens, head_count, key_width)
    start_state = (
        jnp.full((local_tokens, head_count), big_negative, jnp.float32),
        jnp.zeros((local_tokens, head_count), jnp.float32),
        jnp.zeros((local_tokens, head_count, latent_width), jnp.float32),
    )
    suffix_piece = lax.all_gather(suffix_latent, "seq", axis=1, tiled=True)
    prefix_piece = lax.all_gather(prefix_latent, "seq", axis=1, tiled=True)
    piece_rows = suffix_piece.shape[1]
    suffix_keys = suffix_piece[0]
    key_positions = jnp.arange(piece_rows, dtype=jnp.int32)
    key_requests = request_of(key_positions, request_ends)
    suffix_allowed = (key_requests[None, :] == my_requests[:, None]) & (
        key_positions[None, :] <= my_positions[:, None]
    )
    suffix_scores = (
        jnp.einsum("thk,nk->thn", query_rows, suffix_keys, preferred_element_type=jnp.float32)
        * qk_scale
    )

    def one_prefix(running_state):
        chosen_keys = lax.dynamic_index_in_dim(prefix_piece, my_prefix, 0, keepdims=False)
        prefix_scores = (
            jnp.einsum("thk,nk->thn", query_rows, chosen_keys, preferred_element_type=jnp.float32)
            * qk_scale
        )
        scores = jnp.concatenate([suffix_scores, prefix_scores], axis=2)
        every_key = jnp.ones((local_tokens, piece_rows), dtype=bool)
        allowed = jnp.concatenate([suffix_allowed, every_key], axis=1)[:, None, :]
        values = jnp.concatenate(
            [suffix_keys[:, :latent_width], chosen_keys[:, :latent_width]], axis=0
        )
        return merge_scores(running_state, scores, allowed, values)

    def two_prefixes(running_state):
        prefix_scores = (
            jnp.einsum(
                "thk,pnk->thpn", query_rows, prefix_piece, preferred_element_type=jnp.float32
            )
            * qk_scale
        )
        scores = jnp.concatenate(
            [suffix_scores, prefix_scores.reshape(local_tokens, head_count, 2 * piece_rows)], axis=2
        )
        prefix_allowed = jnp.broadcast_to(
            prefix_pick[:, :, None], (local_tokens, 2, piece_rows)
        ).reshape(local_tokens, 2 * piece_rows)
        allowed = jnp.concatenate([suffix_allowed, prefix_allowed], axis=1)[:, None, :]
        values = jnp.concatenate(
            [
                suffix_keys[:, :latent_width],
                prefix_piece[:, :, :latent_width].reshape(2 * piece_rows, latent_width),
            ],
            axis=0,
        )
        return merge_scores(running_state, scores, allowed, values)

    final_max, final_sum, final_acc = lax.cond(single_prefix, one_prefix, two_prefixes, start_state)
    latent_out = (final_acc / final_sum[:, :, None]).astype(jnp.bfloat16)
    value_out = jnp.einsum(
        "thl,hlv->thv", latent_out, value_up, preferred_element_type=jnp.float32
    ).astype(jnp.bfloat16)
    value_out = value_out.reshape(local_tokens, head_count * value_up.shape[2])
    projected = jnp.dot(
        value_out,
        lax.all_gather(out_proj, "expert", axis=1, tiled=True),
        preferred_element_type=jnp.float32,
    )
    residual = hidden[0].astype(jnp.float32) + projected
    normed = (
        residual
        * lax.rsqrt(jnp.mean(residual * residual, axis=1, keepdims=True) + 1e-06)
        * norm_gain
    ).astype(jnp.bfloat16)
    logits = jnp.dot(normed, router, preferred_element_type=jnp.float32)
    expert_probs = jax.nn.softmax(logits, axis=1)
    expert_ids = jnp.arange(expert_count, dtype=jnp.int32)
    my_routes = routes[0]
    matches = my_routes[:, :, None] == expert_ids[None, None, :]
    gate_values = jnp.sum(jnp.where(matches, expert_probs[:, None, :], 0.0), axis=2)
    flat_hits = matches.reshape(local_tokens * top_count, expert_count).astype(jnp.int32)
    earlier = jnp.cumsum(flat_hits, axis=0) - flat_hits
    slot_index = jnp.sum(earlier * flat_hits, axis=1).reshape(local_tokens, top_count)
    cell_index = my_routes * capacity + slot_index
    cell_ids = jnp.arange(expert_count * capacity, dtype=jnp.int32)
    placing = jnp.sum(
        (cell_ids[:, None, None] == cell_index[None, :, :]).astype(jnp.int32), axis=2
    ).astype(jnp.bfloat16)
    outgoing = jnp.dot(placing, normed, preferred_element_type=jnp.float32).astype(jnp.bfloat16)
    outgoing = outgoing.reshape(expert_count, capacity, model_width)
    incoming = lax.all_to_all(outgoing, "expert", split_axis=0, concat_axis=0, tiled=True)
    full_in, full_out = (
        lax.all_gather(expert_in, "seq", axis=1, tiled=True),
        lax.all_gather(expert_out, "seq", axis=1, tiled=True),
    )
    all_rows = incoming.reshape(-1, model_width)
    gate_up = jnp.dot(all_rows, full_in[0], preferred_element_type=jnp.float32)
    hidden_units = gate_up.shape[1] // 2
    active = (jax.nn.silu(gate_up[:, :hidden_units]) * gate_up[:, hidden_units:]).astype(
        jnp.bfloat16
    )
    produced = lax.dot_general(
        active, full_out[0], (((1,), (1,)), ((), ())), preferred_element_type=jnp.float32
    ).astype(jnp.bfloat16)
    returned = lax.all_to_all(
        produced.reshape(-1, capacity, model_width),
        "expert",
        split_axis=0,
        concat_axis=0,
        tiled=True,
    )
    returned_rows = returned.reshape(-1, model_width)
    picked = returned_rows[cell_index]
    routed_sum = jnp.sum(gate_values[:, :, None] * picked.astype(jnp.float32), axis=1)
    layer_out = (residual + routed_sum).astype(jnp.bfloat16)
    return layer_out[None]


def solution(mesh):
    in_specs = (
        P("expert", "seq", None),
        P("expert", "seq", None),
        P("expert", "seq", None),
        P(None, "seq", None),
        P("expert", None),
        P("expert", None),
        P(),
        P(None, "expert"),
        P(),
        P(),
        P("expert", "seq", None),
        P("expert", "seq", None),
        P("expert", "seq", None),
    )
    out_specs = P("expert", "seq", None)
    return jax.shard_map(local, mesh=mesh, in_specs=in_specs, out_specs=out_specs, check_vma=False)
```

profile of v0, /device:TPU:8, one launch (start us, length us, event | category | flops | bytes accessed | tf_op | source)
XLA Modules:
  0.0 367.6 jit_solution(16596417180253832410)
XLA Ops:
  6.5 0.7 all-gather.8.cloned.1.call-update
  7.3 0.0 all-gather.6.cloned.1.call-start
  7.3 1.8 copy.86
  9.1 0.0 all-gather.10.cloned.1.call-start
  9.1 0.7 all-gather.10.cloned.1.call-update
  9.8 0.0 all-gather.12.cloned.1.call-start
  9.9 0.5 all-gather.12.cloned.1.call-update
  10.4 0.0 all-gather.14.cloned.1.call-start
  10.4 0.5 all-gather.14.cloned.1.call-update
  11.0 0.8 copy.97
  11.8 0.1 eq.114
  11.9 0.1 eq.110
  12.1 0.8 reduce-window.18
  12.9 0.1 convert_reduce_fusion.1
  13.0 0.1 convert_reduce_fusion.2
  13.1 0.1 fusion.38
  13.2 0.7 select_reduce_fusion.3
  13.9 2.4 reshape_squeeze.3
  16.4 0.7 compare_reduce_fusion
  17.7 0.9 reduce-window.19
  18.6 0.2 slice_reduce_fusion
  18.9 0.1 fusion.44
  19.0 0.1 reshape.139
  19.1 0.1 copy.101
  19.2 0.8 convert_reduce_fusion
  20.0 36.4 %all-gather.8.cloned.1.call-done = bf16[1,1024,576]{2,1,0:T(8,128)(2,1)} async-done(((bf16[1,64,576]{2,1,0:T(8,128)(2,1)}), bf16[1,1024,576]{2,1,0:T(8,128)(2,1)}) %all-gather.8.cloned.1.call-update) | async-done | bytes 1179664 | tf_op jit(solution)/shard_map/all_gather | solution.py:65
  56.4 2.4 copy.87
  58.8 2.5 convolution_multiply_fusion
  61.3 39.0 %all-gather.6.cloned.1.call-done = bf16[2,1024,576]{2,0,1:T(2,128)(2,1)} async-done(((bf16[2,64,576]{2,0,1:T(2,128)(2,1)}), bf16[2,1024,576]{2,0,1:T(2,128)(2,1)}) %all-gather.6.cloned.1.call-update) | async-done | bytes 2359312 | tf_op jit(solution)/shard_map/all_gather | solution.py:66
  100.3 16.9 %conditional.1 = (f32[64,8,512]{2,1,0:T(8,128)}, f32[64,8]{1,0:T(8,128)S(1)}) conditional(s32[]{:T(128)} %convert_element_type.64, (s32[64]{0:T(128)S(1)}, s32[64,2]{1,0:T(8,128)S(1)}, pred[64,1024]{1,0:T(8,128)(4,1)S(1)}, bf16[64,8,576]{2,1,0:T(8,128)(2,1)}, bf16[2,1024,576]{2,0,1:T(2,128)(2,1)}, /*index=5*/f32[64,8,1024]{2,1,0:T(8,128)S(1)}, ...), branch_computations={%region_5.8_spmd, %region_8.11_spmd} | conditional | flops 2843409920 | bytes 92157032 | solution.py:116
  100.5 7.4 %copy.90 = bf16[2,1024,576]{1,2,0:T(8,128)(2,1)} copy(bf16[2,1024,576]{2,0,1:T(2,128)(2,1)} %get-tuple-element.115) | data formatting | bytes 4718592 | tf_op jit(solution)/shard_map
  107.8 2.4 multiply_bitcast_fusion
  110.3 1.2 copy.92
  111.5 0.5 select_reduce_fusion.1
  112.1 1.0 fusion.18
  113.1 0.6 copy-done.7
  113.7 0.1 dynamic-slice_bitcast_fusion
  113.8 0.1 slice.37
  113.9 0.7 copy-done.3
  114.5 0.1 slice.21
  114.6 2.6 fusion.19
  117.2 0.1 copy.106
  117.3 1.4 divide_convert_fusion
  118.7 0.4 fusion.33
  119.1 69.8 %all-gather.10.cloned.1.call-done = bf16[1024,2048]{0,1:T(8,128)(2,1)} async-done(((bf16[1024,64]{0,1:T(8,128)(2,1)}), bf16[1024,2048]{0,1:T(8,128)(2,1)}) %all-gather.10.cloned.1.call-update) | async-done | bytes 4194320 | tf_op jit(solution)/shard_map/all_gather | solution.py:124
  189.0 3.7 %multiply_reduce_fusion.1 = (f32[64]{0:T(128)S(1)}, f32[64,2048]{1,0:T(8,128)S(1)}) fusion(bf16[1024,2048]{0,1:T(8,128)(2,1)} %all-gather.10.cloned.1.call-done, bf16[8,8,8,128]{3,2,1,0:T(8,128)(2,1)S(1)} %fusion.33, bf16[1,64,2048]{2,1,0:T(8,128)(2,1)S(1)} %copy-done.9), kind=kOutput, calls=%fused_computation.60 | convolution fusion | flops 268959680 | bytes 5112064 | tf_op jit(solution)/shard_map/dot_general | solution.py:122
  192.7 0.8 copy-done.5
  193.5 2.1 convolution_convert_fusion.1
  195.6 5.8 %all-to-all-start = ((bf16[32,16,2048]{2,1,0:T(8,128)(2,1)}), bf16[32,16,2048]{2,1,0:T(8,128)(2,1)S(1)}, u32[]{:S(2)}, u32[]{:S(2)}) async-start(bf16[32,16,2048]{2,1,0:T(8,128)(2,1)} %bitcast.20), calls=%async_computation | async-start | bytes 4194304 | tf_op jit(solution)/shard_map/all_to_all | solution.py:149
  201.4 34.9 %all-gather.12.cloned.1.call-done = bf16[1,2048,1408]{2,1,0:T(8,128)(2,1)} async-done(((bf16[1,128,1408]{2,1,0:T(8,128)(2,1)}), bf16[1,2048,1408]{2,1,0:T(8,128)(2,1)}) %all-gather.12.cloned.1.call-update) | async-done | bytes 5767184 | tf_op jit(solution)/shard_map/all_gather | solution.py:151
  236.3 12.3 %all-to-all-done = bf16[32,16,2048]{2,1,0:T(8,128)(2,1)S(1)} async-done(((bf16[32,16,2048]{2,1,0:T(8,128)(2,1)}), bf16[32,16,2048]{2,1,0:T(8,128)(2,1)S(1)}, u32[]{:S(2)}, u32[]{:S(2)}) %all-to-all-start) | async-done | bytes 2097184 | tf_op jit(solution)/shard_map/all_to_all | solution.py:149
  248.6 7.7 %fusion.28 = f32[512,1408]{1,0:T(8,128)} fusion(bf16[512,2048]{1,0:T(8,128)(2,1)S(1)} %bitcast.103, bf16[1,2048,1408]{2,1,0:T(8,128)(2,1)} %all-gather.12.cloned.1.call-done), kind=kOutput, calls=%fused_computation.40 | convolution fusion | flops 2952790016 | bytes 10747904 | tf_op jit(solution)/shard_map/dot_general | solution.py:155
  256.3 27.2 %all-gather.14.cloned.1.call-done = bf16[1,2048,704]{1,2,0:T(8,128)(2,1)} async-done(((bf16[1,128,704]{1,2,0:T(8,128)(2,1)}), bf16[1,2048,704]{1,2,0:T(8,128)(2,1)}) %all-gather.14.cloned.1.call-update) | async-done | bytes 2883600 | tf_op jit(solution)/shard_map/all_gather | solution.py:152
  283.5 6.0 %convolution_convert_fusion = bf16[512,2048]{1,0:T(8,128)(2,1)} fusion(bf16[1,2048,704]{1,2,0:T(8,128)(2,1)} %all-gather.14.cloned.1.call-done, f32[512,1408]{1,0:T(8,128)} %fusion.28), kind=kOutput, calls=%fused_computation.43 | convolution fusion | flops 1479606272 | bytes 8126464 | tf_op jit(solution)/shard_map/dot_general | solution.py:160
  289.5 10.0 %all-to-all-start.1 = ((bf16[32,16,2048]{2,1,0:T(8,128)(2,1)}), bf16[32,16,2048]{2,1,0:T(8,128)(2,1)S(1)}, u32[]{:S(2)}, u32[]{:S(2)}) async-start(bf16[32,16,2048]{2,1,0:T(8,128)(2,1)} %bitcast.102), calls=%async_computation.1 | async-start | bytes 4194304 | tf_op jit(solution)/shard_map/all_to_all | solution.py:163
  299.6 0.1 reshape.144
  299.7 0.1 reshape.148
  299.9 1.3 fusion.50
  301.3 0.1 copy.96
  301.4 48.1 %all-to-all-done.1 = bf16[32,16,2048]{2,1,0:T(8,128)(2,1)S(1)} async-done(((bf16[32,16,2048]{2,1,0:T(8,128)(2,1)}), bf16[32,16,2048]{2,1,0:T(8,128)(2,1)S(1)}, u32[]{:S(2)}, u32[]{:S(2)}) %all-to-all-start.1) | async-done | bytes 2097184 | tf_op jit(solution)/shard_map/all_to_all | solution.py:163
  349.5 3.1 gather_fusion
  352.6 3.9 %reshape.155 = f32[64,6,2048]{2,1,0:T(8,128)} reshape(bf16[384,2048]{1,0:T(8,128)(2,1)} %gather_fusion) | data formatting | bytes 4718592 | tf_op jit(solution)/shard_map/convert_element_type | solution.py:172
  356.5 3.8 %multiply_reduce_fusion = f32[64,2048]{1,0:T(8,128)S(1)} fusion(f32[64,6,2048]{2,1,0:T(8,128)} %reshape.155, f32[64,6]{1,0:T(8,128)S(1)} %copy.96), kind=kLoop, calls=%fused_computation.42 | loop fusion | flops 1441792 | bytes 3671552 | tf_op jit(solution)/shard_map/reduce_sum | solution.py:172
  360.3 0.8 fusion.37
  (33 shorter events, 0.2 us)
Async XLA Ops:
  6.5 112.2 %copy-start = (bf16[8,512,128]{2,1,0:T(8,128)(2,1)S(1)}, bf16[8,512,128]{2,1,0:T(8,128)(2,1)}, u32[]{:S(2)}) copy-start(bf16[8,512,128]{2,1,0:T(8,128)(2,1)} %param.21) | copy-start | bytes 3145732
  6.5 49.8 %all-gather.8.cloned.1.call-start = ((), (), s32[]{:S(2)}) async-start(), calls=%async_computation.3 | async-start | bytes 1392640 | tf_op jit(solution)/shard_map/all_gather | solution.py:65
  7.3 93.1 %all-gather.6.cloned.1.call-start = ((), (), s32[]{:S(2)}) async-start(), calls=%async_computation.2 | async-start | bytes 2785280 | tf_op jit(solution)/shard_map/all_gather | solution.py:66
  9.1 179.9 %all-gather.10.cloned.1.call-start = ((), (), s32[]{:S(2)}) async-start(), calls=%async_computation.4 | async-start | bytes 4325376 | tf_op jit(solution)/shard_map/all_gather | solution.py:124
  9.8 226.5 %all-gather.12.cloned.1.call-start = ((), (), s32[]{:S(2)}) async-start(), calls=%async_computation.5 | async-start | bytes 6127616 | tf_op jit(solution)/shard_map/all_gather | solution.py:151
  10.4 273.1 %all-gather.14.cloned.1.call-start = ((), (), s32[]{:S(2)}) async-start(), calls=%async_computation.6 | async-start | bytes 3063808 | tf_op jit(solution)/shard_map/all_gather | solution.py:152
  112.1 1.7 copy-start.7
  113.1 1.4 copy-start.3
  117.3 71.7 %copy-start.9 = (bf16[1,64,2048]{2,1,0:T(8,128)(2,1)S(1)}, bf16[1,64,2048]{2,1,0:T(8,128)(2,1)}, u32[]{:S(2)}) copy-start(bf16[1,64,2048]{2,1,0:T(8,128)(2,1)} %param.15) | copy-start | bytes 786436
  119.1 74.4 %copy-start.8 = (s32[512,64]{0,1:T(8,128)S(1)}, s32[512,64]{0,1:T(8,128)}, u32[]{:S(2)}) copy-start(s32[512,64]{0,1:T(8,128)} %convert_reduce_fusion) | copy-start | bytes 393220
  119.1 74.4 %copy-start.11 = (f32[2048]{0:T(1024)S(1)}, f32[2048]{0:T(1024)}, u32[]{:S(2)}) copy-start(f32[2048]{0:T(1024)} %param.23) | copy-start | bytes 24580
  192.7 0.8 copy-start.5
  195.6 53.0 %all-to-all-start = ((bf16[32,16,2048]{2,1,0:T(8,128)(2,1)}), bf16[32,16,2048]{2,1,0:T(8,128)(2,1)S(1)}, u32[]{:S(2)}, u32[]{:S(2)}) async-start(bf16[32,16,2048]{2,1,0:T(8,128)(2,1)} %bitcast.20), calls=%async_computation | async-start | bytes 4194304 | tf_op jit(solution)/shard_map/all_to_all | solution.py:149
  289.5 10.0 %copy-start.12 = (s32[1,64,6]{1,0,2:T(1,128)S(1)}, s32[1,64,6]{1,0,2:T(1,128)}, u32[]{:S(2)}) copy-start(s32[1,64,6]{1,0,2:T(1,128)} %param.25) | copy-start | bytes 4612
  289.5 10.3 %copy-start.10 = (bf16[2048,32]{0,1:T(8,128)(2,1)S(1)}, bf16[2048,32]{0,1:T(8,128)(2,1)}, u32[]{:S(2)}) copy-start(bf16[2048,32]{0,1:T(8,128)(2,1)} %param.24) | copy-start | bytes 393220
  289.5 59.9 %all-to-all-start.1 = ((bf16[32,16,2048]{2,1,0:T(8,128)(2,1)}), bf16[32,16,2048]{2,1,0:T(8,128)(2,1)S(1)}, u32[]{:S(2)}, u32[]{:S(2)}) async-start(bf16[32,16,2048]{2,1,0:T(8,128)(2,1)} %bitcast.102), calls=%async_computation.1 | async-start | bytes 4194304 | tf_op jit(solution)/shard_map/all_to_all | solution.py:163
  356.5 3.8 %copy-start.6 = (f32[64,2048]{1,0:T(8,128)S(1)}, f32[64,2048]{1,0:T(8,128)}, u32[]{:S(2)}) copy-start(f32[64,2048]{1,0:T(8,128)} %copy-done.5) | copy-start | bytes 1572868
Sparse Core Ops, SparseCore 0:
  9.5 46.8 all-gather.7
  58.5 41.7 all-gather.5
  103.5 85.3 all-gather.9
  190.9 45.2 all-gather.11
  238.2 45.3 all-gather.13
where the time goes:
time: 369 us; the launch traced here: 368 us
  waiting for transfers between devices  270 us (73%)
  matrix products  28.7 us (8%)
  local copies, waits for them, and re-layouts  26.5 us (7%)
  starting transfers between devices  16 us (4%)
  between operations  14 us (4%)
  other arithmetic  12.1 us (3%)
    all_gather x1, waiting for transfers between devices, local(): lax.all_gather(out_proj, 'expert', axis=1, tiled=True)  69.8 us
    all_to_all x1, waiting for transfers between devices, local(): lax.all_to_all(produced.reshape(-1, capacity, model_width), 'expert', spl...  48.1 us
    all_gather x1, waiting for transfers between devices, local(): prefix_piece = lax.all_gather(prefix_latent, 'seq', axis=1, tiled=True)  39 us
    all_gather x1, waiting for transfers between devices, local(): suffix_piece = lax.all_gather(suffix_latent, 'seq', axis=1, tiled=True)  36.4 us
    all_gather x1, waiting for transfers between devices, local(): lax.all_gather(expert_in, 'seq', axis=1, tiled=True)  34.9 us
    all_gather x1, waiting for transfers between devices, local(): lax.all_gather(expert_out, 'seq', axis=1, tiled=True)  27.2 us
    all_to_all x1, waiting for transfers between devices, local(): lax.all_to_all(outgoing, 'expert', split_axis=0, concat_axis=0, tiled=True)  12.3 us
    all_to_all x1, starting transfers between devices, local(): lax.all_to_all(produced.reshape(-1, capacity, model_width), 'expert', spl...  9.98 us
  transfers between devices with their start and end apart: 7, of which 7 were waited for; matrix products, arithmetic and copies ran while one was open for 13% of the time, Pallas kernels for 0%

commit v1 on v0

--- a/solution.py
+++ b/solution.py
@@ -62,8 +62,10 @@
         jnp.zeros((local_tokens, head_count), jnp.float32),
         jnp.zeros((local_tokens, head_count, latent_width), jnp.float32),
     )
-    suffix_piece = lax.all_gather(suffix_latent, "seq", axis=1, tiled=True)
-    prefix_piece = lax.all_gather(prefix_latent, "seq", axis=1, tiled=True)
+    key_stack = jnp.concatenate([suffix_latent, prefix_latent], axis=0)
+    key_stack = lax.all_gather(key_stack, "seq", axis=1, tiled=True)
+    suffix_piece = key_stack[:1]
+    prefix_piece = key_stack[1:]
     piece_rows = suffix_piece.shape[1]
     suffix_keys = suffix_piece[0]
     key_positions = jnp.arange(piece_rows, dtype=jnp.int32)
@@ -119,11 +121,17 @@
         "thl,hlv->thv", latent_out, value_up, preferred_element_type=jnp.float32
     ).astype(jnp.bfloat16)
     value_out = value_out.reshape(local_tokens, head_count * value_up.shape[2])
-    projected = jnp.dot(
-        value_out,
-        lax.all_gather(out_proj, "expert", axis=1, tiled=True),
-        preferred_element_type=jnp.float32,
-    )
+    expert_devices = model_width // out_proj.shape[1]
+    column_blocks = lax.all_to_all(
+        jnp.broadcast_to(out_proj[None], (expert_devices,) + out_proj.shape),
+        "expert",
+        split_axis=0,
+        concat_axis=0,
+        tiled=True,
+    )
+    projected = jnp.einsum(
+        "tr,jrc->tjc", value_out, column_blocks, preferred_element_type=jnp.float32
+    ).reshape(local_tokens, model_width)
     residual = hidden[0].astype(jnp.float32) + projected
     normed = (
         residual
@@ -147,10 +155,11 @@
     outgoing = jnp.dot(placing, normed, preferred_element_type=jnp.float32).astype(jnp.bfloat16)
     outgoing = outgoing.reshape(expert_count, capacity, model_width)
     incoming = lax.all_to_all(outgoing, "expert", split_axis=0, concat_axis=0, tiled=True)
-    full_in, full_out = (
-        lax.all_gather(expert_in, "seq", axis=1, tiled=True),
-        lax.all_gather(expert_out, "seq", axis=1, tiled=True),
-    )
+    in_width = expert_in.shape[2]
+    full_both = lax.all_gather(
+        jnp.concatenate([expert_in, expert_out], axis=2), "seq", axis=1, tiled=True
+    )
+    full_in, full_out = full_both[:, :, :in_width], full_both[:, :, in_width:]
     all_rows = incoming.reshape(-1, model_width)
     gate_up = jnp.dot(all_rows, full_in[0], preferred_element_type=jnp.float32)
     hidden_units = gate_up.shape[1] // 2

time: 369 us -> 268 us (0.73)
  the two profiles are of different devices: /device:TPU:8 before, /device:TPU:16 now
where the time goes in v1:
time: 268 us; the launch traced here: 267 us
  waiting for transfers between devices  111 us (41%)
  blocking collectives  56.9 us (21%)
  matrix products  24.9 us (9%)
  local copies, waits for them, and re-layouts  24.8 us (9%)
  other arithmetic  17.7 us (7%)
  starting transfers between devices  17.5 us (7%)
  between operations  14.3 us (5%)
    all_to_all x1, blocking collectives, local(): lax.all_to_all(outgoing, 'expert', split_axis=0, concat_axis=0, tiled=True)  56.9 us
    all_to_all x1, waiting for transfers between devices, local(): lax.all_to_all(produced.reshape(-1, capacity, model_width), 'expert', spl...  48.7 us
    all_to_all x1, waiting for transfers between devices, local(): lax.all_to_all(jnp.broadcast_to(out_proj[None], (expert_devices,) + out_p...  32.6 us
    all_gather x1, waiting for transfers between devices, local(): key_stack = lax.all_gather(key_stack, 'seq', axis=1, tiled=True)  29.3 us
    all_to_all x1, starting transfers between devices, local(): lax.all_to_all(jnp.broadcast_to(out_proj[None], (expert_devices,) + out_p...  10.3 us
    all_to_all x1, starting transfers between devices, local(): lax.all_to_all(produced.reshape(-1, capacity, model_width), 'expert', spl...  7.19 us
    dot_general x1, matrix products, local(): gate_up = jnp.dot(all_rows, full_in[0], preferred_element_type=jnp.float32)  5.74 us
  transfers between devices with their start and end apart: 4, of which 3 were waited for; matrix products, arithmetic and copies ran while one was open for 15% of the time, Pallas kernels for 0%

profile of v1, /device:TPU:16, one launch (start us, length us, event | category | flops | bytes accessed | tf_op | source)
XLA Modules:
  0.0 266.8 jit_solution(5147941125471809802)
XLA Ops:
  6.5 0.0 all-gather.3.cloned.1.call-start
  6.5 1.8 pad_maximum_fusion.3
  8.3 0.0 all-gather.3.cloned.1.call-update
  8.3 0.0 all-gather.5.cloned.1.call-start
  8.4 1.1 copy.107
  9.5 1.8 pad_maximum_fusion.2
  11.3 0.0 all-gather.5.cloned.1.call-update
  11.3 3.4 %broadcast_in_dim.113 = bf16[32,1024,64]{1,2,0:T(8,128)(2,1)} broadcast(bf16[1024,64]{0,1:T(8,128)(2,1)} %param.22), dimensions={1,2} | broadcast | bytes 4325376 | tf_op jit(solution)/shard_map/broadcast_in_dim | solution.py:126
  14.7 10.3 %all-to-all-start = ((bf16[32,1024,64]{1,2,0:T(8,128)(2,1)}), bf16[32,1024,64]{1,2,0:T(8,128)(2,1)}, u32[]{:S(2)}, u32[]{:S(2)}) async-start(bf16[32,1024,64]{1,2,0:T(8,128)(2,1)} %broadcast_in_dim.113), calls=%async_computation | async-start | bytes 8388608 | tf_op jit(solution)/shard_map/all_to_all | solution.py:125
  25.0 0.1 copy.102
  25.1 0.1 eq.114
  25.3 0.1 eq.110
  25.4 0.0 copy-done.10
  25.4 0.5 reshape_squeeze.3
  25.9 0.2 reduce-window.18
  26.1 0.1 convert_reduce_fusion.2
  26.2 0.1 select_reduce_fusion.3
  26.3 0.7 compare_reduce_fusion
  27.6 0.9 reduce-window.19
  28.4 0.2 slice_reduce_fusion
  28.7 0.1 fusion.45
  28.8 0.1 reshape.142
  29.0 0.1 copy.106
  29.0 0.1 convert_reduce_fusion.1
  29.1 0.8 convert_reduce_fusion
  29.9 0.1 fusion.39
  30.0 29.3 %all-gather.3.cloned.1.call-done = bf16[3,1024,576]{2,1,0:T(8,128)(2,1)} async-done(((bf16[3,64,576]{2,1,0:T(8,128)(2,1)}), bf16[3,1024,576]{2,1,0:T(8,128)(2,1)}) %all-gather.3.cloned.1.call-update) | async-done | bytes 3538960 | tf_op jit(solution)/shard_map/all_gather | solution.py:66
  59.4 1.4 slice.55
  60.8 1.5 copy.115
  62.3 3.5 %slice.54 = bf16[2,1024,576]{2,1,0:T(8,128)(2,1)} slice(bf16[3,1024,576]{2,1,0:T(8,128)(2,1)} %all-gather.3.cloned.1.call-done), slice={[1:3], [0:1024], [0:576]} | slice | bytes 4718592 | tf_op jit(solution)/shard_map/slice | solution.py:68
  65.8 3.7 %multiply_bitcast_fusion.1 = f32[64,8,1024]{2,0,1:T(8,128)} fusion(bf16[64,8,576]{2,1,0:T(8,128)(2,1)S(1)} %reshape_squeeze.3, bf16[3,1024,576]{2,1,0:T(8,128)(2,1)} %all-gather.3.cloned.1.call-done), kind=kOutput, calls=%fused_computation.48 | convolution fusion | flops 604504064 | bytes 3997696 | tf_op jit(solution)/shard_map/thk,nk->thn/dot_general | solution.py:77
  69.4 15.4 %conditional.1 = (f32[64,8,512]{2,1,0:T(8,128)}, f32[64,8]{1,0:T(8,128)S(1)}) conditional(s32[]{:T(128)} %convert_element_type.64, (s32[64]{0:T(128)S(1)}, s32[64,2]{1,0:T(8,128)S(1)}, pred[64,1024]{1,0:T(8,128)(4,1)S(1)}, bf16[64,8,576]{2,1,0:T(8,128)(2,1)S(1)}, bf16[2,1024,576]{2,1,0:T(8,128)(2,1)}, /*index=5*/f32[64,8,1024]{2,0,1:T(8,128)}, ...), branch_computations={%region_5.8_spmd, %region_8.11_spmd} | conditional | flops 2843409920 | bytes 86914120 | solution.py:118
  69.6 0.7 copy-done.9
  70.3 2.9 %copy.96 = bf16[2,1024,576]{1,2,0:T(8,128)(2,1)S(1)} copy(bf16[2,1024,576]{2,1,0:T(8,128)(2,1)} %get-tuple-element.109) | data formatting | bytes 4718592 | tf_op jit(solution)/shard_map
  73.2 2.6 multiply_bitcast_fusion
  75.9 2.2 select_reduce_fusion.1
  78.0 0.0 copy-done.7
  78.0 2.8 %fusion.18 = (f32[64,8]{0,1:T(8,128)S(1)}, bf16[64,8,2048]{2,0,1:T(8,128)(2,1)S(1)}) fusion(f32[64,8,1024]{2,0,1:T(8,128)S(1)} %multiply_bitcast_fusion, f32[64,8,1024]{2,0,1:T(8,128)} %get-tuple-element.41, f32[64,8]{0,1:T(8,128)S(1)} %broadcast_maximum_fusion.1, pred[64,2048]{1,0:T(8,128)(4,1)S(1)} %concatenate.19), kind=kLoop, calls=%fused_computation.26 | loop fusion | flops 5242368 | bytes 6426624 | tf_op jit(solution)/shard_map/cond/branch_1_fun/reduce_sum | solution.py:18
  80.8 0.1 dynamic-slice_bitcast_fusion
  80.9 0.1 slice.53
  81.0 1.1 copy-done.4
  82.1 0.1 slice.29
  82.2 2.6 fusion.19
  84.7 0.1 copy.113
  84.8 1.4 divide_convert_fusion
  86.3 0.4 fusion.33
  86.7 0.0 copy-start.14
  86.7 32.6 %all-to-all-done = bf16[32,1024,64]{1,2,0:T(8,128)(2,1)} async-done(((bf16[32,1024,64]{1,2,0:T(8,128)(2,1)}), bf16[32,1024,64]{1,2,0:T(8,128)(2,1)}, u32[]{:S(2)}, u32[]{:S(2)}) %all-to-all-start) | async-done | bytes 4194336 | tf_op jit(solution)/shard_map/all_to_all | solution.py:125
  119.3 3.7 %multiply_reduce_fusion.1 = (f32[64]{0:T(128)S(1)}, f32[64,2048]{1,0:T(8,128)S(1)}) fusion(bf16[2048,1024]{1,0:T(8,128)(2,1)} %bitcast.20, bf16[8,8,8,128]{3,2,1,0:T(8,128)(2,1)S(1)} %fusion.33, bf16[1,64,2048]{2,1,0:T(8,128)(2,1)S(1)} %copy-done.12), kind=kOutput, calls=%fused_computation.63 | convolution fusion | flops 268959680 | bytes 5112064 | tf_op jit(solution)/shard_map/tr,jrc->tjc/dot_general | solution.py:132
  123.0 0.8 convolution_convert_fusion
  123.8 56.9 %all_to_all.15 = bf16[32,16,2048]{2,1,0:T(8,128)(2,1)S(1)} all-to-all(bf16[32,16,2048]{2,1,0:T(8,128)(2,1)S(1)} %bitcast.109), channel_id=1, replica_groups=mesh['seq'=16,'expert'=32] {'expert'}, dimensions={0} | all-to-all | bytes 4194304 | tf_op jit(solution)/shard_map/all_to_all | solution.py:157
  180.7 5.7 %fusion.28 = f32[512,1408]{1,0:T(8,128)S(1)} fusion(bf16[512,2048]{1,0:T(8,128)(2,1)S(1)} %bitcast.111, bf16[1,2048,2112]{2,1,0:T(8,128)(2,1)} %all-gather.5.cloned.1.call-done), kind=kOutput, calls=%fused_computation.41 | convolution fusion | flops 2952790016 | bytes 10747904 | tf_op jit(solution)/shard_map/dot_general | solution.py:164
  186.4 5.2 %fusion.30 = bf16[512,2048]{1,0:T(8,128)(2,1)} fusion(bf16[1,2048,2112]{2,1,0:T(8,128)(2,1)} %all-gather.5.cloned.1.call-done, f32[512,1408]{1,0:T(8,128)S(1)} %fusion.28), kind=kOutput, calls=%fused_computation.45 | convolution fusion | flops 1479606272 | bytes 8388608 | tf_op jit(solution)/shard_map/dot_general | solution.py:169
  191.6 7.2 %all-to-all-start.2 = ((bf16[32,16,2048]{2,1,0:T(8,128)(2,1)}), bf16[32,16,2048]{2,1,0:T(8,128)(2,1)S(1)}, u32[]{:S(2)}, u32[]{:S(2)}) async-start(bf16[32,16,2048]{2,1,0:T(8,128)(2,1)} %bitcast.110), calls=%async_computation.2 | async-start | bytes 4194304 | tf_op jit(solution)/shard_map/all_to_all | solution.py:172
  198.8 0.1 reshape.147
  199.0 0.1 reshape.151
  199.1 0.3 fusion.52
  199.5 0.1 copy.101
  199.6 48.7 %all-to-all-done.2 = bf16[32,16,2048]{2,1,0:T(8,128)(2,1)S(1)} async-done(((bf16[32,16,2048]{2,1,0:T(8,128)(2,1)}), bf16[32,16,2048]{2,1,0:T(8,128)(2,1)S(1)}, u32[]{:S(2)}, u32[]{:S(2)}) %all-to-all-start.2) | async-done | bytes 2097184 | tf_op jit(solution)/shard_map/all_to_all | solution.py:172
  248.3 3.1 %gather_fusion = bf16[384,2048]{1,0:T(8,128)(2,1)} fusion(bf16[512,2048]{1,0:T(8,128)(2,1)S(1)} %bitcast.103, s32[1024]{0:T(1024)S(1)} %pad_clamp_fusion), kind=kCustom, calls=%fused_computation | custom fusion | bytes 3147264 | tf_op jit(solution)/shard_map/gather | solution.py:180
  251.4 4.0 %reshape.158 = f32[64,6,2048]{2,1,0:T(8,128)} reshape(bf16[384,2048]{1,0:T(8,128)(2,1)} %gather_fusion) | data formatting | bytes 4718592 | tf_op jit(solution)/shard_map/convert_element_type | solution.py:181
  255.4 3.8 %multiply_reduce_fusion = f32[64,2048]{1,0:T(8,128)S(1)} fusion(f32[64,6,2048]{2,1,0:T(8,128)} %reshape.158, f32[64,6]{1,0:T(8,128)S(1)} %copy.101), kind=kLoop, calls=%fused_computation.42 | loop fusion | flops 1441792 | bytes 3671552 | tf_op jit(solution)/shard_map/reduce_sum | solution.py:181
  259.2 0.0 copy-done.6
  259.2 0.8 fusion.38
  (41 shorter events, 0.2 us)
Async XLA Ops:
  6.5 79.7 %copy-start = (bf16[8,512,128]{2,1,0:T(8,128)(2,1)S(1)}, bf16[8,512,128]{2,1,0:T(8,128)(2,1)}, u32[]{:S(2)}) copy-start(bf16[8,512,128]{2,1,0:T(8,128)(2,1)} %param.21) | copy-start | bytes 3145732
  6.5 52.9 %all-gather.3.cloned.1.call-start = ((), (), s32[]{:S(2)}) async-start(), calls=%async_computation.3 | async-start | bytes 4177920 | tf_op jit(solution)/shard_map/all_gather | solution.py:66
  8.3 172.3 %all-gather.5.cloned.1.call-start = ((), (), s32[]{:S(2)}) async-start(), calls=%async_computation.4 | async-start | bytes 9469952 | tf_op jit(solution)/shard_map/all_gather | solution.py:159
  14.7 10.3 %copy-start.15 = (s32[1,64,6]{1,0,2:T(1,128)S(1)}, s32[1,64,6]{1,0,2:T(1,128)}, u32[]{:S(2)}) copy-start(s32[1,64,6]{1,0,2:T(1,128)} %param.25) | copy-start | bytes 4612
  14.7 10.7 %copy-start.10 = (bf16[1,64,4608]{2,1,0:T(8,128)(2,1)S(1)}, bf16[1,64,4608]{2,1,0:T(8,128)(2,1)}, u32[]{:S(2)}) copy-start(bf16[1,64,4608]{2,1,0:T(8,128)(2,1)} %param.16) | copy-start | bytes 1769476
  14.7 11.2 %copy-start.16 = (s32[1,4]{1,0:T(1,128)S(1)}, s32[1,4]{1,0:T(1,128)}, u32[]{:S(2)}) copy-start(s32[1,4]{1,0:T(1,128)} %param.19) | copy-start | bytes 52
  14.7 11.5 %copy-start.17 = (s32[1,4]{1,0:T(1,128)S(1)}, s32[1,4]{1,0:T(1,128)}, u32[]{:S(2)}) copy-start(s32[1,4]{1,0:T(1,128)} %param.20) | copy-start | bytes 52
  14.7 104.5 %all-to-all-start = ((bf16[32,1024,64]{1,2,0:T(8,128)(2,1)}), bf16[32,1024,64]{1,2,0:T(8,128)(2,1)}, u32[]{:S(2)}, u32[]{:S(2)}) async-start(bf16[32,1024,64]{1,2,0:T(8,128)(2,1)} %broadcast_in_dim.113), calls=%async_computation | async-start | bytes 8388608 | tf_op jit(solution)/shard_map/all_to_all | solution.py:125
  69.4 0.8 copy-start.9
  73.2 4.8 %copy-start.7 = (bf16[2,1024,576]{1,2,0:T(8,128)(2,1)}, bf16[2,1024,576]{1,2,0:T(8,128)(2,1)S(1)}, u32[]{:S(2)}) copy-start(bf16[2,1024,576]{1,2,0:T(8,128)(2,1)S(1)} %copy.96) | copy-start | bytes 7077892 | tf_op jit(solution)/shard_map/cond
  78.0 2.8 %copy-start.8 = (bf16[2,1024,576]{1,2,0:T(8,128)(2,1)S(1)}, bf16[2,1024,576]{1,2,0:T(8,128)(2,1)}, u32[]{:S(2)}) copy-start(bf16[2,1024,576]{1,2,0:T(8,128)(2,1)} %copy-done.7) | copy-start | bytes 7077892 | tf_op jit(solution)/shard_map/cond
  80.8 1.3 copy-start.4
  84.8 34.4 %copy-start.12 = (bf16[1,64,2048]{2,1,0:T(8,128)(2,1)S(1)}, bf16[1,64,2048]{2,1,0:T(8,128)(2,1)}, u32[]{:S(2)}) copy-start(bf16[1,64,2048]{2,1,0:T(8,128)(2,1)} %param.15) | copy-start | bytes 786436
  86.7 36.4 %copy-start.11 = (s32[512,64]{0,1:T(8,128)S(1)}, s32[512,64]{0,1:T(8,128)}, u32[]{:S(2)}) copy-start(s32[512,64]{0,1:T(8,128)} %convert_reduce_fusion) | copy-start | bytes 393220
  86.7 36.4 %copy-start.14 = (f32[2048]{0:T(1024)S(1)}, f32[2048]{0:T(1024)}, u32[]{:S(2)}) copy-start(f32[2048]{0:T(1024)} %param.23) | copy-start | bytes 24580
  123.0 76.1 %copy-start.5 = (f32[64,2048]{1,0:T(8,128)}, f32[64,2048]{1,0:T(8,128)S(1)}, u32[]{:S(2)}) copy-start(f32[64,2048]{1,0:T(8,128)S(1)} %get-tuple-element.117) | copy-start | bytes 1572868
  191.6 7.5 %copy-start.13 = (bf16[2048,32]{0,1:T(8,128)(2,1)S(1)}, bf16[2048,32]{0,1:T(8,128)(2,1)}, u32[]{:S(2)}) copy-start(bf16[2048,32]{0,1:T(8,128)(2,1)} %param.24) | copy-start | bytes 393220
  191.6 56.7 %all-to-all-start.2 = ((bf16[32,16,2048]{2,1,0:T(8,128)(2,1)}), bf16[32,16,2048]{2,1,0:T(8,128)(2,1)S(1)}, u32[]{:S(2)}, u32[]{:S(2)}) async-start(bf16[32,16,2048]{2,1,0:T(8,128)(2,1)} %bitcast.110), calls=%async_computation.2 | async-start | bytes 4194304 | tf_op jit(solution)/shard_map/all_to_all | solution.py:172
  251.4 8.6 %copy-start.1 = (bf16[8,512,128]{2,1,0:T(8,128)(2,1)S(1)}, bf16[8,512,128]{2,1,0:T(8,128)(2,1)}, u32[]{:S(2)}) copy-start(bf16[8,512,128]{2,1,0:T(8,128)(2,1)} %param.21) | copy-start | bytes 3145732
  255.4 3.8 %copy-start.6 = (f32[64,2048]{1,0:T(8,128)S(1)}, f32[64,2048]{1,0:T(8,128)}, u32[]{:S(2)}) copy-start(f32[64,2048]{1,0:T(8,128)} %copy-done.5) | copy-start | bytes 1572868
Sparse Core Ops, SparseCore 0:
  9.5 49.8 all-gather.2
  61.5 59.6 all-gather.4

commit v2 on v1

--- a/solution.py
+++ b/solution.py
@@ -1,3 +1,5 @@
+import functools
+
 import jax
 import jax.numpy as jnp
 from jax import lax
@@ -36,6 +38,7 @@
     routes,
     expert_in,
     expert_out,
+    seq_count=1,
 ):
     local_tokens = hidden.shape[1]
     model_width = hidden.shape[2]
@@ -122,15 +125,24 @@
     ).astype(jnp.bfloat16)
     value_out = value_out.reshape(local_tokens, head_count * value_up.shape[2])
     expert_devices = model_width // out_proj.shape[1]
-    column_blocks = lax.all_to_all(
-        jnp.broadcast_to(out_proj[None], (expert_devices,) + out_proj.shape),
+    half_rows = out_proj.shape[0] // 2
+    core = lax.axis_index("seq") % 2
+    my_rows = lax.dynamic_slice_in_dim(out_proj, core * half_rows, half_rows, axis=0)
+    my_blocks = lax.all_to_all(
+        jnp.broadcast_to(my_rows[None], (expert_devices,) + my_rows.shape),
         "expert",
         split_axis=0,
         concat_axis=0,
         tiled=True,
     )
-    projected = jnp.einsum(
-        "tr,jrc->tjc", value_out, column_blocks, preferred_element_type=jnp.float32
+    other_blocks = lax.ppermute(
+        my_blocks, "seq", perm=[(i, i ^ 1) for i in range(seq_count)]
+    )
+    my_part = lax.dynamic_slice_in_dim(value_out, core * half_rows, half_rows, axis=1)
+    other_part = lax.dynamic_slice_in_dim(value_out, (1 - core) * half_rows, half_rows, axis=1)
+    projected = (
+        jnp.einsum("tr,jrc->tjc", my_part, my_blocks, preferred_element_type=jnp.float32)
+        + jnp.einsum("tr,jrc->tjc", other_part, other_blocks, preferred_element_type=jnp.float32)
     ).reshape(local_tokens, model_width)
     residual = hidden[0].astype(jnp.float32) + projected
     normed = (
@@ -200,4 +212,4 @@
         P("expert", "seq", None),
     )
     out_specs = P("expert", "seq", None)
-    return jax.shard_map(local, mesh=mesh, in_specs=in_specs, out_specs=out_specs, check_vma=False)
+    return jax.shard_map(functools.partial(local, seq_count=mesh.shape["seq"]), mesh=mesh, in_specs=in_specs, out_specs=out_specs, check_vma=False)

time: 268 us -> 274 us (1.022)
  the two profiles are of different devices: /device:TPU:16 before, /device:TPU:80 now
where the time goes in v2:
time: 274 us; the launch traced here: 273 us
  waiting for transfers between devices  96.3 us (35%)
  blocking collectives  72 us (26%)
  matrix products  26.3 us (10%)
  local copies, waits for them, and re-layouts  26.1 us (10%)
  starting transfers between devices  20.3 us (7%)
  other arithmetic  17.7 us (6%)
  between operations  14.3 us (5%)
    all_to_all x1, blocking collectives, local(): lax.all_to_all(outgoing, 'expert', split_axis=0, concat_axis=0, tiled=True)  72 us
    all_to_all x1, waiting for transfers between devices, local(): lax.all_to_all(jnp.broadcast_to(my_rows[None], (expert_devices,) + my_row...  48.8 us
    all_to_all x1, waiting for transfers between devices, local(): lax.all_to_all(produced.reshape(-1, capacity, model_width), 'expert', spl...  47.5 us
    all_to_all x1, starting transfers between devices, local(): lax.all_to_all(jnp.broadcast_to(my_rows[None], (expert_devices,) + my_row...  10.3 us
    all_to_all x1, starting transfers between devices, local(): lax.all_to_all(produced.reshape(-1, capacity, model_width), 'expert', spl...  8.05 us
    dot_general x1, matrix products, local(): gate_up = jnp.dot(all_rows, full_in[0], preferred_element_type=jnp.float32)  5.74 us
  transfers between devices with their start and end apart: 5, of which 2 were waited for; matrix products, arithmetic and copies ran while one was open for 16% of the time, Pallas kernels for 0%

profile of v2, /device:TPU:80, one launch (start us, length us, event | category | flops | bytes accessed | tf_op | source)
XLA Modules:
  0.0 273.2 jit_solution(11955176074812125987)
XLA Ops:
  6.5 1.8 pad_maximum_fusion.3
  8.4 0.0 all-gather.5.cloned.1.call-start
  8.4 1.1 copy.121
  9.5 1.8 pad_maximum_fusion.2
  11.4 1.6 broadcast_in_dim.111
  13.0 10.3 %all-to-all-start = ((bf16[32,512,64]{1,2,0:T(8,128)(2,1)}), bf16[32,512,64]{1,2,0:T(8,128)(2,1)}, u32[]{:S(2)}, u32[]{:S(2)}) async-start(bf16[32,512,64]{1,2,0:T(8,128)(2,1)} %broadcast_in_dim.111), calls=%async_computation | async-start | bytes 4194304 | tf_op jit(solution)/shard_map/all_to_all | solution.py:131
  23.3 0.1 copy.116
  23.4 0.1 eq.116
  23.5 0.1 eq.112
  23.6 0.2 reduce-window.18
  23.8 0.5 reshape_squeeze.3
  24.4 0.1 convert_reduce_fusion.2
  24.4 0.1 select_reduce_fusion.3
  24.5 48.8 %all-to-all-done = bf16[32,512,64]{1,2,0:T(8,128)(2,1)} async-done(((bf16[32,512,64]{1,2,0:T(8,128)(2,1)}), bf16[32,512,64]{1,2,0:T(8,128)(2,1)}, u32[]{:S(2)}, u32[]{:S(2)}) %all-to-all-start) | async-done | bytes 2097184 | tf_op jit(solution)/shard_map/all_to_all | solution.py:131
  73.3 1.9 collective-permute-start
  75.2 0.6 compare_reduce_fusion
  76.4 1.2 copy.114
  77.6 0.9 reduce-window.19
  78.5 0.2 slice_reduce_fusion
  78.8 0.1 fusion.50
  78.9 0.1 reshape.152
  79.0 0.1 copy.120
  79.1 0.1 convert_reduce_fusion.1
  79.2 0.8 convert_reduce_fusion
  80.0 0.1 fusion.42
  80.1 0.0 all-gather.3.cloned.1.call-done
  80.1 1.5 slice.55
  81.6 1.5 copy.129
  83.1 3.5 %slice.54 = bf16[2,1024,576]{2,1,0:T(8,128)(2,1)} slice(bf16[3,1024,576]{2,1,0:T(8,128)(2,1)} %all-gather.3.cloned.1.call-done), slice={[1:3], [0:1024], [0:576]} | slice | bytes 4718592 | tf_op jit(solution)/shard_map/slice | solution.py:71
  86.5 3.7 %multiply_bitcast_fusion.1 = f32[64,8,1024]{2,0,1:T(8,128)} fusion(bf16[64,8,576]{2,1,0:T(8,128)(2,1)S(1)} %reshape_squeeze.3, bf16[3,1024,576]{2,1,0:T(8,128)(2,1)} %all-gather.3.cloned.1.call-done), kind=kOutput, calls=%fused_computation.47 | convolution fusion | flops 604504064 | bytes 3997696 | tf_op jit(solution)/shard_map/thk,nk->thn/dot_general | solution.py:80
  90.2 14.8 %conditional.1 = (f32[64,8,512]{2,1,0:T(8,128)}, f32[64,8]{1,0:T(8,128)S(1)}) conditional(s32[]{:T(128)} %convert_element_type.73, (s32[64]{0:T(128)S(1)}, s32[64,2]{1,0:T(8,128)S(1)}, pred[64,1024]{1,0:T(8,128)(4,1)S(1)}, bf16[64,8,576]{2,1,0:T(8,128)(2,1)S(1)}, bf16[2,1024,576]{2,1,0:T(8,128)(2,1)}, /*index=5*/f32[64,8,1024]{2,0,1:T(8,128)}, ...), branch_computations={%region_5.8_spmd, %region_8.11_spmd} | conditional | flops 2843409920 | bytes 86914120 | solution.py:121
  90.3 0.7 copy-done.10
  91.1 2.9 %copy.107 = bf16[2,1024,576]{1,2,0:T(8,128)(2,1)S(1)} copy(bf16[2,1024,576]{2,1,0:T(8,128)(2,1)} %get-tuple-element.109) | data formatting | bytes 4718592 | tf_op jit(solution)/shard_map
  94.0 2.1 multiply_bitcast_fusion
  96.1 2.2 select_reduce_fusion.1
  98.4 2.6 fusion.18
  101.0 0.1 dynamic-slice_bitcast_fusion
  101.1 0.1 slice.53
  101.2 1.1 copy-done.4
  102.3 0.1 slice.29
  102.4 2.6 fusion.19
  105.0 0.1 copy.127
  105.1 1.4 divide_convert_fusion
  106.5 0.4 fusion.33
  106.9 2.3 fusion.46
  109.3 2.5 multiply_reduce_fusion.1
  111.8 0.3 copy.113
  112.1 0.1 fusion.40
  112.3 0.4 copy-done.12
  112.7 0.7 convolution_convert_fusion
  113.4 72.0 %all_to_all.15 = bf16[32,16,2048]{2,1,0:T(8,128)(2,1)S(1)} all-to-all(bf16[32,16,2048]{2,1,0:T(8,128)(2,1)S(1)} %bitcast.131), channel_id=1, replica_groups=mesh['seq'=16,'expert'=32] {'expert'}, dimensions={0} | all-to-all | bytes 4194304 | tf_op jit(solution)/shard_map/all_to_all | solution.py:169
  185.4 5.7 %fusion.28 = f32[512,1408]{1,0:T(8,128)S(1)} fusion(bf16[512,2048]{1,0:T(8,128)(2,1)S(1)} %bitcast.134, bf16[1,2048,2112]{2,1,0:T(8,128)(2,1)} %all-gather.5.cloned.1.call-done), kind=kOutput, calls=%fused_computation.41 | convolution fusion | flops 2952790016 | bytes 10747904 | tf_op jit(solution)/shard_map/dot_general | solution.py:176
  191.2 5.2 %fusion.30 = bf16[512,2048]{1,0:T(8,128)(2,1)} fusion(bf16[1,2048,2112]{2,1,0:T(8,128)(2,1)} %all-gather.5.cloned.1.call-done, f32[512,1408]{1,0:T(8,128)S(1)} %fusion.28), kind=kOutput, calls=%fused_computation.45 | convolution fusion | flops 1479606272 | bytes 8388608 | tf_op jit(solution)/shard_map/dot_general | solution.py:181
  196.3 8.1 %all-to-all-start.2 = ((bf16[32,16,2048]{2,1,0:T(8,128)(2,1)}), bf16[32,16,2048]{2,1,0:T(8,128)(2,1)S(1)}, u32[]{:S(2)}, u32[]{:S(2)}) async-start(bf16[32,16,2048]{2,1,0:T(8,128)(2,1)} %bitcast.133), calls=%async_computation.2 | async-start | bytes 4194304 | tf_op jit(solution)/shard_map/all_to_all | solution.py:184
  204.4 0.1 reshape.157
  204.6 0.1 reshape.162
  204.7 1.1 fusion.58
  205.9 0.1 copy.115
  206.0 1.1 copy.112
  207.1 47.5 %all-to-all-done.2 = bf16[32,16,2048]{2,1,0:T(8,128)(2,1)S(1)} async-done(((bf16[32,16,2048]{2,1,0:T(8,128)(2,1)}), bf16[32,16,2048]{2,1,0:T(8,128)(2,1)S(1)}, u32[]{:S(2)}, u32[]{:S(2)}) %all-to-all-start.2) | async-done | bytes 2097184 | tf_op jit(solution)/shard_map/all_to_all | solution.py:184
  254.7 3.1 %gather_fusion = bf16[384,2048]{1,0:T(8,128)(2,1)} fusion(bf16[512,2048]{1,0:T(8,128)(2,1)S(1)} %bitcast.123, s32[1024]{0:T(1024)S(1)} %pad_clamp_fusion), kind=kCustom, calls=%fused_computation | custom fusion | bytes 3147264 | tf_op jit(solution)/shard_map/gather | solution.py:192
  257.8 4.0 %reshape.169 = f32[64,6,2048]{2,1,0:T(8,128)} reshape(bf16[384,2048]{1,0:T(8,128)(2,1)} %gather_fusion) | data formatting | bytes 4718592 | tf_op jit(solution)/shard_map/convert_element_type | solution.py:193
  261.8 3.8 %multiply_reduce_fusion = f32[64,2048]{1,0:T(8,128)S(1)} fusion(f32[64,6,2048]{2,1,0:T(8,128)} %reshape.169, f32[64,6]{1,0:T(8,128)S(1)} %copy.115), kind=kLoop, calls=%fused_computation.42 | loop fusion | flops 1441792 | bytes 3671552 | tf_op jit(solution)/shard_map/reduce_sum | solution.py:193
  265.6 0.8 fusion.37
  (50 shorter events, 0.3 us)
Async XLA Ops:
  6.5 100.0 %copy-start = (bf16[8,512,128]{2,1,0:T(8,128)(2,1)S(1)}, bf16[8,512,128]{2,1,0:T(8,128)(2,1)}, u32[]{:S(2)}) copy-start(bf16[8,512,128]{2,1,0:T(8,128)(2,1)} %param.21) | copy-start | bytes 3145732
  6.5 4.8 %copy-start.13 = (bf16[1024,64]{0,1:T(8,128)(2,1)S(1)}, bf16[1024,64]{0,1:T(8,128)(2,1)}, u32[]{:S(2)}) copy-start(bf16[1024,64]{0,1:T(8,128)(2,1)} %param.22) | copy-start | bytes 393220
  6.5 73.6 %all-gather.3.cloned.1.call-start = ((), (), s32[]{:S(2)}) async-start(), calls=%async_computation.3 | async-start | bytes 4177920 | tf_op jit(solution)/shard_map/all_gather | solution.py:69
  8.4 177.0 %all-gather.5.cloned.1.call-start = ((), (), s32[]{:S(2)}) async-start(), calls=%async_computation.4 | async-start | bytes 9469952 | tf_op jit(solution)/shard_map/all_gather | solution.py:171
  13.0 10.3 %copy-start.14 = (s32[1,64,6]{1,0,2:T(1,128)S(1)}, s32[1,64,6]{1,0,2:T(1,128)}, u32[]{:S(2)}) copy-start(s32[1,64,6]{1,0,2:T(1,128)} %param.25) | copy-start | bytes 4612
  13.0 10.7 %copy-start.16 = (s32[1,4]{1,0:T(1,128)S(1)}, s32[1,4]{1,0:T(1,128)}, u32[]{:S(2)}) copy-start(s32[1,4]{1,0:T(1,128)} %param.19) | copy-start | bytes 52
  13.0 10.9 %copy-start.11 = (bf16[1,64,4608]{2,1,0:T(8,128)(2,1)S(1)}, bf16[1,64,4608]{2,1,0:T(8,128)(2,1)}, u32[]{:S(2)}) copy-start(bf16[1,64,4608]{2,1,0:T(8,128)(2,1)} %param.16) | copy-start | bytes 1769476
  13.0 11.5 %copy-start.17 = (s32[1,4]{1,0:T(1,128)S(1)}, s32[1,4]{1,0:T(1,128)}, u32[]{:S(2)}) copy-start(s32[1,4]{1,0:T(1,128)} %param.20) | copy-start | bytes 52
  13.0 63.5 %copy-start.6 = (bf16[1,64,2048]{2,1,0:T(8,128)(2,1)S(1)}, bf16[1,64,2048]{2,1,0:T(8,128)(2,1)}, u32[]{:S(2)}) copy-start(bf16[1,64,2048]{2,1,0:T(8,128)(2,1)} %param.15) | copy-start | bytes 786436
  13.0 60.3 %all-to-all-start = ((bf16[32,512,64]{1,2,0:T(8,128)(2,1)}), bf16[32,512,64]{1,2,0:T(8,128)(2,1)}, u32[]{:S(2)}, u32[]{:S(2)}) async-start(bf16[32,512,64]{1,2,0:T(8,128)(2,1)} %broadcast_in_dim.111), calls=%async_computation | async-start | bytes 4194304 | tf_op jit(solution)/shard_map/all_to_all | solution.py:131
  73.3 35.9 %collective-permute-start = (bf16[32,512,64]{1,2,0:T(8,128)(2,1)}, bf16[32,512,64]{1,2,0:T(8,128)(2,1)}, u32[]{:S(2)}, u32[]{:S(2)}) collective-permute-start(bf16[32,512,64]{1,2,0:T(8,128)(2,1)} %all-to-all-done), channel_id=1, source_target_pairs={{0,32},{32,0},{64,96},{96,64},{128,160},{160,128},{192,224},{224,1... | collective-permute-start | bytes 6291464 | tf_op jit(solution)/shard_map/ppermute | solution.py:138
  90.2 0.8 copy-start.10
  101.0 1.3 copy-start.4
  106.5 2.8 %copy-start.5 = (f32[1,64,2048]{1,2,0:T(8,128)S(1)}, f32[1,64,2048]{1,2,0:T(8,128)}, u32[]{:S(2)}) copy-start(f32[1,64,2048]{1,2,0:T(8,128)} %copy.114) | copy-start | bytes 1572868
  109.3 2.8 %copy-start.7 = (bf16[1,64,2048]{2,1,0:T(8,128)(2,1)S(1)}, bf16[1,64,2048]{2,1,0:T(8,128)(2,1)}, u32[]{:S(2)}) copy-start(bf16[1,64,2048]{2,1,0:T(8,128)(2,1)} %param.15) | copy-start | bytes 786436
  109.3 2.8 %copy-start.15 = (f32[2048]{0:T(1024)S(1)}, f32[2048]{0:T(1024)}, u32[]{:S(2)}) copy-start(f32[2048]{0:T(1024)} %param.23) | copy-start | bytes 24580
  111.8 0.9 copy-start.12
  196.3 58.3 %all-to-all-start.2 = ((bf16[32,16,2048]{2,1,0:T(8,128)(2,1)}), bf16[32,16,2048]{2,1,0:T(8,128)(2,1)S(1)}, u32[]{:S(2)}, u32[]{:S(2)}) async-start(bf16[32,16,2048]{2,1,0:T(8,128)(2,1)} %bitcast.133), calls=%async_computation.2 | async-start | bytes 4194304 | tf_op jit(solution)/shard_map/all_to_all | solution.py:184
  257.8 8.6 %copy-start.1 = (bf16[8,512,128]{2,1,0:T(8,128)(2,1)S(1)}, bf16[8,512,128]{2,1,0:T(8,128)(2,1)}, u32[]{:S(2)}) copy-start(bf16[8,512,128]{2,1,0:T(8,128)(2,1)} %param.21) | copy-start | bytes 3145732
  261.7 3.8 %copy-start.8 = (bf16[1,64,2048]{2,1,0:T(8,128)(2,1)S(1)}, bf16[1,64,2048]{2,1,0:T(8,128)(2,1)}, u32[]{:S(2)}) copy-start(bf16[1,64,2048]{2,1,0:T(8,128)(2,1)} %param.15) | copy-start | bytes 786436
  261.8 3.8 %copy-start.9 = (f32[1,64,2048]{2,1,0:T(8,128)S(1)}, f32[1,64,2048]{2,1,0:T(8,128)}, u32[]{:S(2)}) copy-start(f32[1,64,2048]{2,1,0:T(8,128)} %copy.112) | copy-start | bytes 1572868
Sparse Core Ops, SparseCore 0:
  9.5 48.2 all-gather.2
  59.9 58.3 all-gather.4

commit v3 on v2

--- a/solution.py
+++ b/solution.py
@@ -135,6 +135,7 @@
         concat_axis=0,
         tiled=True,
     )
+    my_blocks, value_out = lax.optimization_barrier((my_blocks, value_out))
     other_blocks = lax.ppermute(
         my_blocks, "seq", perm=[(i, i ^ 1) for i in range(seq_count)]
     )

time: 274 us -> 260 us (0.949)
  the two profiles are of different devices: /device:TPU:80 before, /device:TPU:16 now
where the time goes in v3:
time: 260 us; the launch traced here: 259 us
  waiting for transfers between devices  80.4 us (31%)
  blocking collectives  76.7 us (30%)
  matrix products  26.3 us (10%)
  local copies, waits for them, and re-layouts  24.6 us (9%)
  starting transfers between devices  19.4 us (7%)
  other arithmetic  17.1 us (7%)
  between operations  14.5 us (6%)
    all_to_all x1, blocking collectives, local(): lax.all_to_all(outgoing, 'expert', split_axis=0, concat_axis=0, tiled=True)  76.7 us
    all_to_all x1, waiting for transfers between devices, local(): lax.all_to_all(produced.reshape(-1, capacity, model_width), 'expert', spl...  46.8 us
    all_gather x1, waiting for transfers between devices, local(): key_stack = lax.all_gather(key_stack, 'seq', axis=1, tiled=True)  33.6 us
    all_to_all x1, starting transfers between devices, local(): lax.all_to_all(jnp.broadcast_to(my_rows[None], (expert_devices,) + my_row...  10.2 us
    all_to_all x1, starting transfers between devices, local(): lax.all_to_all(produced.reshape(-1, capacity, model_width), 'expert', spl...  7.02 us
    dot_general x1, matrix products, local(): gate_up = jnp.dot(all_rows, full_in[0], preferred_element_type=jnp.float32)  5.74 us
  transfers between devices with their start and end apart: 5, of which 2 were waited for; matrix products, arithmetic and copies ran while one was open for 16% of the time, Pallas kernels for 0%

profile of v3, /device:TPU:16, one launch (start us, length us, event | category | flops | bytes accessed | tf_op | source)
XLA Modules:
  0.0 259.2 jit_solution(16658979350616243681)
XLA Ops:
  6.5 1.8 pad_maximum_fusion.3
  8.3 0.0 all-gather.3.cloned.1.call-update
  8.4 0.0 all-gather.5.cloned.1.call-start
  8.4 1.1 copy.121
  9.5 1.8 pad_maximum_fusion.2
  11.3 0.0 all-gather.5.cloned.1.call-update
  11.4 1.6 broadcast_in_dim.108
  13.0 10.2 %all-to-all-start = ((bf16[32,512,64]{1,2,0:T(8,128)(2,1)}), bf16[32,512,64]{1,2,0:T(8,128)(2,1)}, u32[]{:S(2)}, u32[]{:S(2)}) async-start(bf16[32,512,64]{1,2,0:T(8,128)(2,1)} %broadcast_in_dim.108), calls=%async_computation | async-start | bytes 4194304 | tf_op jit(solution)/shard_map/all_to_all | solution.py:131
  23.3 0.2 reduce-window.18
  23.5 0.5 reshape_squeeze.3
  24.0 0.1 convert_reduce_fusion.2
  24.1 0.1 select_reduce_fusion.3
  24.2 0.8 compare_reduce_fusion
  25.6 0.1 convert_reduce_fusion.1
  25.7 0.1 fusion.42
  25.8 33.6 %all-gather.3.cloned.1.call-done = bf16[3,1024,576]{2,1,0:T(8,128)(2,1)} async-done(((bf16[3,64,576]{2,1,0:T(8,128)(2,1)}), bf16[3,1024,576]{2,1,0:T(8,128)(2,1)}) %all-gather.3.cloned.1.call-update) | async-done | bytes 3538960 | tf_op jit(solution)/shard_map/all_gather | solution.py:69
  59.4 1.4 slice.55
  60.8 1.5 copy.129
  62.3 3.4 %slice.54 = bf16[2,1024,576]{2,1,0:T(8,128)(2,1)} slice(bf16[3,1024,576]{2,1,0:T(8,128)(2,1)} %all-gather.3.cloned.1.call-done), slice={[1:3], [0:1024], [0:576]} | slice | bytes 4718592 | tf_op jit(solution)/shard_map/slice | solution.py:71
  65.7 3.7 %multiply_bitcast_fusion.1 = f32[64,8,1024]{2,0,1:T(8,128)} fusion(bf16[64,8,576]{2,1,0:T(8,128)(2,1)S(1)} %reshape_squeeze.3, bf16[3,1024,576]{2,1,0:T(8,128)(2,1)} %all-gather.3.cloned.1.call-done), kind=kOutput, calls=%fused_computation.47 | convolution fusion | flops 604504064 | bytes 3997696 | tf_op jit(solution)/shard_map/thk,nk->thn/dot_general | solution.py:80
  69.4 14.8 %conditional.1 = (f32[64,8,512]{2,1,0:T(8,128)}, f32[64,8]{1,0:T(8,128)S(1)}) conditional(s32[]{:T(128)} %convert_element_type.73, (s32[64]{0:T(128)S(1)}, s32[64,2]{1,0:T(8,128)S(1)}, pred[64,1024]{1,0:T(8,128)(4,1)S(1)}, bf16[64,8,576]{2,1,0:T(8,128)(2,1)S(1)}, bf16[2,1024,576]{2,1,0:T(8,128)(2,1)}, /*index=5*/f32[64,8,1024]{2,0,1:T(8,128)}, ...), branch_computations={%region_5.8_spmd, %region_8.11_spmd} | conditional | flops 2843409920 | bytes 86914120 | solution.py:121
  69.5 0.7 copy-done.8
  70.2 2.9 %copy.107 = bf16[2,1024,576]{1,2,0:T(8,128)(2,1)S(1)} copy(bf16[2,1024,576]{2,1,0:T(8,128)(2,1)} %get-tuple-element.113) | data formatting | bytes 4718592 | tf_op jit(solution)/shard_map
  73.2 2.1 multiply_bitcast_fusion
  75.4 2.2 select_reduce_fusion.1
  77.5 2.6 %fusion.18 = (f32[64,8]{0,1:T(8,128)S(1)}, bf16[64,8,2048]{2,0,1:T(8,128)(2,1)S(1)}) fusion(f32[64,8,1024]{2,0,1:T(8,128)S(1)} %multiply_bitcast_fusion, f32[64,8,1024]{2,0,1:T(8,128)} %get-tuple-element.41, f32[64,8]{0,1:T(8,128)S(1)} %broadcast_maximum_fusion.1, pred[64,2048]{1,0:T(8,128)(4,1)S(1)} %concatenate.19), kind=kLoop, calls=%fused_computation.26 | loop fusion | flops 5242368 | bytes 6426624 | tf_op jit(solution)/shard_map/cond/branch_1_fun/reduce_sum | solution.py:20
  80.1 0.1 dynamic-slice_bitcast_fusion
  80.2 0.1 slice.53
  80.3 1.1 copy-done.4
  81.5 0.1 slice.29
  81.5 2.6 fusion.19
  84.1 0.1 copy.127
  84.2 1.4 divide_convert_fusion
  85.6 0.4 fusion.33
  86.1 2.1 collective-permute-start
  88.2 0.1 copy.116
  88.3 0.1 eq.116
  88.5 0.1 eq.112
  88.6 0.2 copy.114
  88.9 0.9 reduce-window.19
  89.7 0.2 slice_reduce_fusion
  90.0 0.1 fusion.50
  90.1 0.1 reshape.152
  90.3 0.1 copy.120
  90.3 0.2 convert_reduce_fusion
  90.5 2.4 fusion.46
  92.9 2.3 multiply_reduce_fusion.1
  95.2 0.3 copy.113
  95.6 0.1 fusion.40
  95.7 0.7 convolution_convert_fusion
  96.4 76.7 %all_to_all.15 = bf16[32,16,2048]{2,1,0:T(8,128)(2,1)S(1)} all-to-all(bf16[32,16,2048]{2,1,0:T(8,128)(2,1)S(1)} %bitcast.131), channel_id=1, replica_groups=mesh['seq'=16,'expert'=32] {'expert'}, dimensions={0} | all-to-all | bytes 4194304 | tf_op jit(solution)/shard_map/all_to_all | solution.py:170
  173.2 5.7 %fusion.28 = f32[512,1408]{1,0:T(8,128)S(1)} fusion(bf16[512,2048]{1,0:T(8,128)(2,1)S(1)} %bitcast.134, bf16[1,2048,2112]{2,1,0:T(8,128)(2,1)} %all-gather.5.cloned.1.call-done), kind=kOutput, calls=%fused_computation.41 | convolution fusion | flops 2952790016 | bytes 10747904 | tf_op jit(solution)/shard_map/dot_general | solution.py:177
  178.9 5.2 %fusion.30 = bf16[512,2048]{1,0:T(8,128)(2,1)} fusion(bf16[1,2048,2112]{2,1,0:T(8,128)(2,1)} %all-gather.5.cloned.1.call-done, f32[512,1408]{1,0:T(8,128)S(1)} %fusion.28), kind=kOutput, calls=%fused_computation.45 | convolution fusion | flops 1479606272 | bytes 8388608 | tf_op jit(solution)/shard_map/dot_general | solution.py:182
  184.1 7.0 %all-to-all-start.2 = ((bf16[32,16,2048]{2,1,0:T(8,128)(2,1)}), bf16[32,16,2048]{2,1,0:T(8,128)(2,1)S(1)}, u32[]{:S(2)}, u32[]{:S(2)}) async-start(bf16[32,16,2048]{2,1,0:T(8,128)(2,1)} %bitcast.133), calls=%async_computation.2 | async-start | bytes 4194304 | tf_op jit(solution)/shard_map/all_to_all | solution.py:185
  191.1 0.1 reshape.157
  191.3 0.1 reshape.162
  191.4 1.1 fusion.58
  192.6 0.1 copy.115
  192.7 1.1 copy.112
  193.8 46.8 %all-to-all-done.2 = bf16[32,16,2048]{2,1,0:T(8,128)(2,1)S(1)} async-done(((bf16[32,16,2048]{2,1,0:T(8,128)(2,1)}), bf16[32,16,2048]{2,1,0:T(8,128)(2,1)S(1)}, u32[]{:S(2)}, u32[]{:S(2)}) %all-to-all-start.2) | async-done | bytes 2097184 | tf_op jit(solution)/shard_map/all_to_all | solution.py:185
  240.6 3.1 %gather_fusion = bf16[384,2048]{1,0:T(8,128)(2,1)} fusion(bf16[512,2048]{1,0:T(8,128)(2,1)S(1)} %bitcast.123, s32[1024]{0:T(1024)S(1)} %pad_clamp_fusion), kind=kCustom, calls=%fused_computation | custom fusion | bytes 3147264 | tf_op jit(solution)/shard_map/gather | solution.py:193
  243.7 4.0 %reshape.169 = f32[64,6,2048]{2,1,0:T(8,128)} reshape(bf16[384,2048]{1,0:T(8,128)(2,1)} %gather_fusion) | data formatting | bytes 4718592 | tf_op jit(solution)/shard_map/convert_element_type | solution.py:194
  247.7 3.8 %multiply_reduce_fusion = f32[64,2048]{1,0:T(8,128)S(1)} fusion(f32[64,6,2048]{2,1,0:T(8,128)} %reshape.169, f32[64,6]{1,0:T(8,128)S(1)} %copy.115), kind=kLoop, calls=%fused_computation.42 | loop fusion | flops 1441792 | bytes 3671552 | tf_op jit(solution)/shard_map/reduce_sum | solution.py:194
  251.6 0.8 fusion.37
  (44 shorter events, 0.3 us)
Async XLA Ops:
  6.5 79.1 %copy-start = (bf16[8,512,128]{2,1,0:T(8,128)(2,1)S(1)}, bf16[8,512,128]{2,1,0:T(8,128)(2,1)}, u32[]{:S(2)}) copy-start(bf16[8,512,128]{2,1,0:T(8,128)(2,1)} %param.21) | copy-start | bytes 3145732
  6.5 4.8 %copy-start.10 = (bf16[1024,64]{0,1:T(8,128)(2,1)S(1)}, bf16[1024,64]{0,1:T(8,128)(2,1)}, u32[]{:S(2)}) copy-start(bf16[1024,64]{0,1:T(8,128)(2,1)} %param.22) | copy-start | bytes 393220
  6.5 52.8 %all-gather.3.cloned.1.call-start = ((), (), s32[]{:S(2)}) async-start(), calls=%async_computation.3 | async-start | bytes 4177920 | tf_op jit(solution)/shard_map/all_gather | solution.py:69
  8.4 164.8 %all-gather.5.cloned.1.call-start = ((), (), s32[]{:S(2)}) async-start(), calls=%async_computation.4 | async-start | bytes 9469952 | tf_op jit(solution)/shard_map/all_gather | solution.py:172
  13.0 10.3 %copy-start.13 = (s32[1,4]{1,0:T(1,128)S(1)}, s32[1,4]{1,0:T(1,128)}, u32[]{:S(2)}) copy-start(s32[1,4]{1,0:T(1,128)} %param.19) | copy-start | bytes 52
  13.0 10.4 %copy-start.9 = (bf16[1,64,4608]{2,1,0:T(8,128)(2,1)S(1)}, bf16[1,64,4608]{2,1,0:T(8,128)(2,1)}, u32[]{:S(2)}) copy-start(bf16[1,64,4608]{2,1,0:T(8,128)(2,1)} %param.16) | copy-start | bytes 1769476
  13.0 11.1 %copy-start.14 = (s32[1,4]{1,0:T(1,128)S(1)}, s32[1,4]{1,0:T(1,128)}, u32[]{:S(2)}) copy-start(s32[1,4]{1,0:T(1,128)} %param.20) | copy-start | bytes 52
  13.0 73.0 %all-to-all-start = ((bf16[32,512,64]{1,2,0:T(8,128)(2,1)}), bf16[32,512,64]{1,2,0:T(8,128)(2,1)}, u32[]{:S(2)}, u32[]{:S(2)}) async-start(bf16[32,512,64]{1,2,0:T(8,128)(2,1)} %broadcast_in_dim.108), calls=%async_computation | async-start | bytes 4194304 | tf_op jit(solution)/shard_map/all_to_all | solution.py:131
  69.4 0.8 copy-start.8
  80.1 1.3 copy-start.4
  84.2 4.0 %copy-start.11 = (s32[1,64,6]{1,0,2:T(1,128)S(1)}, s32[1,64,6]{1,0,2:T(1,128)}, u32[]{:S(2)}) copy-start(s32[1,64,6]{1,0,2:T(1,128)} %param.25) | copy-start | bytes 4612
  84.2 4.4 %copy-start.5 = (bf16[1,64,2048]{2,1,0:T(8,128)(2,1)S(1)}, bf16[1,64,2048]{2,1,0:T(8,128)(2,1)}, u32[]{:S(2)}) copy-start(bf16[1,64,2048]{2,1,0:T(8,128)(2,1)} %param.15) | copy-start | bytes 786436
  86.1 6.8 %collective-permute-start = (bf16[32,512,64]{1,2,0:T(8,128)(2,1)}, bf16[32,512,64]{1,2,0:T(8,128)(2,1)}, u32[]{:S(2)}, u32[]{:S(2)}) collective-permute-start(bf16[32,512,64]{1,2,0:T(8,128)(2,1)} %all-to-all-done), channel_id=1, source_target_pairs={{0,32},{32,0},{64,96},{96,64},{128,160},{160,128},{192,224},{224,1... | collective-permute-start | bytes 6291464 | tf_op jit(solution)/shard_map/ppermute | solution.py:139
  92.9 2.7 %copy-start.12 = (f32[2048]{0:T(1024)S(1)}, f32[2048]{0:T(1024)}, u32[]{:S(2)}) copy-start(f32[2048]{0:T(1024)} %param.23) | copy-start | bytes 24580
  184.1 56.6 %all-to-all-start.2 = ((bf16[32,16,2048]{2,1,0:T(8,128)(2,1)}), bf16[32,16,2048]{2,1,0:T(8,128)(2,1)S(1)}, u32[]{:S(2)}, u32[]{:S(2)}) async-start(bf16[32,16,2048]{2,1,0:T(8,128)(2,1)} %bitcast.133), calls=%async_computation.2 | async-start | bytes 4194304 | tf_op jit(solution)/shard_map/all_to_all | solution.py:185
  243.7 8.6 %copy-start.1 = (bf16[8,512,128]{2,1,0:T(8,128)(2,1)S(1)}, bf16[8,512,128]{2,1,0:T(8,128)(2,1)}, u32[]{:S(2)}) copy-start(bf16[8,512,128]{2,1,0:T(8,128)(2,1)} %param.21) | copy-start | bytes 3145732
  247.7 3.8 %copy-start.6 = (bf16[1,64,2048]{2,1,0:T(8,128)(2,1)S(1)}, bf16[1,64,2048]{2,1,0:T(8,128)(2,1)}, u32[]{:S(2)}) copy-start(bf16[1,64,2048]{2,1,0:T(8,128)(2,1)} %param.15) | copy-start | bytes 786436
  247.7 3.8 %copy-start.7 = (f32[1,64,2048]{2,1,0:T(8,128)S(1)}, f32[1,64,2048]{2,1,0:T(8,128)}, u32[]{:S(2)}) copy-start(f32[1,64,2048]{2,1,0:T(8,128)} %copy.112) | copy-start | bytes 1572868
Sparse Core Ops, SparseCore 0:
  9.5 49.8 all-gather.2
  61.5 59.8 all-gather.4

commit v4 on v3

--- a/solution.py
+++ b/solution.py
@@ -190,8 +190,16 @@
         tiled=True,
     )
     returned_rows = returned.reshape(-1, model_width)
-    picked = returned_rows[cell_index]
-    routed_sum = jnp.sum(gate_values[:, :, None] * picked.astype(jnp.float32), axis=1)
+    combining = jnp.sum(
+        jnp.where(cell_index[:, :, None] == cell_ids[None, None, :], gate_values[:, :, None], 0.0),
+        axis=1,
+    )
+    routed_sum = jnp.dot(
+        combining,
+        returned_rows.astype(jnp.float32),
+        precision=lax.Precision.HIGHEST,
+        preferred_element_type=jnp.float32,
+    )
     layer_out = (residual + routed_sum).astype(jnp.bfloat16)
     return layer_out[None]
 

time: 260 us -> 255 us (0.981)
  local copies, waits for them, and re-layouts: 24.6 us -> 16.7 us
  matrix products: 26.3 us -> 30.5 us
  other arithmetic: 17.1 us -> 14 us
    convert_element_type x1 -> x0, local copies, waits for them, and re-layouts: 3.98 us -> none  [local(): picked.astype(jnp.float32)]
    reduce_sum x1, other arithmetic: 3.81 us -> 0.17 us  [local(): jnp.sum(jnp.where(cell_index[:, :, None] == cell_ids[None, None, :], gate...]
    gather x1 -> x0, local copies, waits for them, and re-layouts: 3.12 us -> none  [local(): picked = returned_rows[cell_index]]
    dot_general x0 -> x1, matrix products: none -> 2.95 us  [local(): jnp.dot(combining, returned_rows.astype(jnp.float32), precision=lax.Preci...]
  transfers between devices with their start and end apart: 5 -> 5, of which waited for: 2 -> 2; matrix products, arithmetic and copies ran while one was open for 16% -> 17% of each run, Pallas kernels for 0% -> 0%
where the time goes in v4:
time: 255 us; the launch traced here: 254 us
  waiting for transfers between devices  81.4 us (32%)
  blocking collectives  76.8 us (30%)
  matrix products  30.5 us (12%)
  starting transfers between devices  19.6 us (8%)
  local copies, waits for them, and re-layouts  16.7 us (7%)
  between operations  14.5 us (6%)
  other arithmetic  14 us (5%)
    all_to_all x1, blocking collectives, local(): lax.all_to_all(outgoing, 'expert', split_axis=0, concat_axis=0, tiled=True)  76.8 us
    all_to_all x1, waiting for transfers between devices, local(): lax.all_to_all(produced.reshape(-1, capacity, model_width), 'expert', spl...  47.8 us
    all_gather x1, waiting for transfers between devices, local(): key_stack = lax.all_gather(key_stack, 'seq', axis=1, tiled=True)  33.6 us
    all_to_all x1, starting transfers between devices, local(): lax.all_to_all(jnp.broadcast_to(my_rows[None], (expert_devices,) + my_row...  10.2 us
    all_to_all x1, starting transfers between devices, local(): lax.all_to_all(produced.reshape(-1, capacity, model_width), 'expert', spl...  7.2 us
    dot_general x1, matrix products, local(): gate_up = jnp.dot(all_rows, full_in[0], preferred_element_type=jnp.float32)  6.44 us
    unnamed x2, matrix products  5.23 us
    dot_general x1, matrix products, local(): lax.dot_general(active, full_out[0], (((1,), (1,)), ((), ())), preferred_...  5.17 us
  transfers between devices with their start and end apart: 5, of which 2 were waited for; matrix products, arithmetic and copies ran while one was open for 17% of the time, Pallas kernels for 0%

profile of v4, /device:TPU:16, one launch (start us, length us, event | category | flops | bytes accessed | tf_op | source)
XLA Modules:
  0.0 253.7 jit_solution(10934214437020985810)
XLA Ops:
  6.5 1.8 pad_maximum_fusion.3
  8.3 0.0 all-gather.3.cloned.1.call-update
  8.4 0.0 all-gather.5.cloned.1.call-start
  8.4 1.1 copy.147
  9.5 1.8 pad_maximum_fusion.2
  11.3 0.0 all-gather.5.cloned.1.call-update
  11.4 1.6 broadcast_in_dim.123
  13.0 10.2 %all-to-all-start = ((bf16[32,512,64]{1,2,0:T(8,128)(2,1)}), bf16[32,512,64]{1,2,0:T(8,128)(2,1)}, u32[]{:S(2)}, u32[]{:S(2)}) async-start(bf16[32,512,64]{1,2,0:T(8,128)(2,1)} %broadcast_in_dim.123), calls=%async_computation | async-start | bytes 4194304 | tf_op jit(solution)/shard_map/all_to_all | solution.py:131
  23.3 0.2 reduce-window.18
  23.5 0.5 reshape_squeeze.3
  24.0 0.1 convert_reduce_fusion.2
  24.1 0.1 select_reduce_fusion.4
  24.2 0.8 compare_reduce_fusion
  25.6 0.1 convert_reduce_fusion.1
  25.7 0.1 fusion.40
  25.8 33.6 %all-gather.3.cloned.1.call-done = bf16[3,1024,576]{2,1,0:T(8,128)(2,1)} async-done(((bf16[3,64,576]{2,1,0:T(8,128)(2,1)}), bf16[3,1024,576]{2,1,0:T(8,128)(2,1)}) %all-gather.3.cloned.1.call-update) | async-done | bytes 3538960 | tf_op jit(solution)/shard_map/all_gather | solution.py:69
  59.4 1.4 slice.53
  60.8 1.5 copy.156
  62.3 3.4 %slice.52 = bf16[2,1024,576]{2,1,0:T(8,128)(2,1)} slice(bf16[3,1024,576]{2,1,0:T(8,128)(2,1)} %all-gather.3.cloned.1.call-done), slice={[1:3], [0:1024], [0:576]} | slice | bytes 4718592 | tf_op jit(solution)/shard_map/slice | solution.py:71
  65.7 3.7 %multiply_bitcast_fusion.1 = f32[64,8,1024]{2,0,1:T(8,128)} fusion(bf16[64,8,576]{2,1,0:T(8,128)(2,1)S(1)} %reshape_squeeze.3, bf16[3,1024,576]{2,1,0:T(8,128)(2,1)} %all-gather.3.cloned.1.call-done), kind=kOutput, calls=%fused_computation.48 | convolution fusion | flops 604504064 | bytes 3997696 | tf_op jit(solution)/shard_map/thk,nk->thn/dot_general | solution.py:80
  69.4 14.8 %conditional.1 = (f32[64,8,512]{2,1,0:T(8,128)}, f32[64,8]{1,0:T(8,128)S(1)}) conditional(s32[]{:T(128)} %convert_element_type.68, (s32[64]{0:T(128)S(1)}, s32[64,2]{1,0:T(8,128)S(1)}, pred[64,1024]{1,0:T(8,128)(4,1)S(1)}, bf16[64,8,576]{2,1,0:T(8,128)(2,1)S(1)}, bf16[2,1024,576]{2,1,0:T(8,128)(2,1)}, /*index=5*/f32[64,8,1024]{2,0,1:T(8,128)}, ...), branch_computations={%region_5.8_spmd, %region_8.11_spmd} | conditional | flops 2843409920 | bytes 86914120 | solution.py:121
  69.5 0.7 copy-done.7
  70.2 2.9 %copy.133 = bf16[2,1024,576]{1,2,0:T(8,128)(2,1)S(1)} copy(bf16[2,1024,576]{2,1,0:T(8,128)(2,1)} %get-tuple-element.128) | data formatting | bytes 4718592 | tf_op jit(solution)/shard_map
  73.2 2.1 multiply_bitcast_fusion
  75.4 2.2 select_reduce_fusion.1
  77.5 2.6 %fusion.18 = (f32[64,8]{0,1:T(8,128)S(1)}, bf16[64,8,2048]{2,0,1:T(8,128)(2,1)S(1)}) fusion(f32[64,8,1024]{2,0,1:T(8,128)S(1)} %multiply_bitcast_fusion, f32[64,8,1024]{2,0,1:T(8,128)} %get-tuple-element.41, f32[64,8]{0,1:T(8,128)S(1)} %broadcast_maximum_fusion.1, pred[64,2048]{1,0:T(8,128)(4,1)S(1)} %concatenate.19), kind=kLoop, calls=%fused_computation.25 | loop fusion | flops 5242368 | bytes 6426624 | tf_op jit(solution)/shard_map/cond/branch_1_fun/reduce_sum | solution.py:20
  80.1 0.1 dynamic-slice_bitcast_fusion
  80.2 0.1 slice.51
  80.3 1.1 copy-done.3
  81.5 0.1 slice.29
  81.5 2.6 %fusion.19 = f32[64,8,512]{2,1,0:T(8,128)} fusion(bf16[1024,512]{0,1:T(8,128)(2,1)S(1)} %slice.51, bf16[1024,512]{0,1:T(8,128)(2,1)S(1)} %slice.29, bf16[64,8,2048]{2,0,1:T(8,128)(2,1)S(1)} %get-tuple-element.136), kind=kOutput, calls=%fused_computation.27 | convolution fusion | flops 1077936128 | bytes 5242880 | tf_op jit(solution)/shard_map/cond/branch_1_fun/thn,nl->thl/dot_general | solution.py:21
  84.1 0.1 copy.154
  84.2 1.4 divide_convert_fusion
  85.6 0.4 fusion.35
  86.1 2.1 collective-permute-start
  88.2 0.1 copy.139
  88.3 0.1 eq.122
  88.5 0.5 copy-done.10
  88.9 0.1 eq.118
  89.1 0.2 copy.145
  89.3 0.9 reduce-window.19
  90.2 0.2 slice_reduce_fusion
  90.4 0.1 fusion.48
  90.6 0.1 reshape.127
  90.7 0.1 copy.146
  90.8 0.8 convert_reduce_fusion
  91.6 2.3 fusion.44
  94.0 0.0 copy-start.14
  94.0 2.9 %multiply_reduce_fusion = (f32[64]{0:T(128)}, f32[64,32,64]{0,2,1:T(8,128)S(1)}) fusion(f32[64,32,64]{0,2,1:T(8,128)S(1)} %bitcast.126, f32[64,2048]{0,1:S(1)} %fusion.44, bf16[512,2048]{0,1:T(8,128)(2,1)} %bitcast.23, bf16[64,1024]{1,0:T(8,128)(2,1)S(1)} %bitcast.133, s32[]{:T(128)S(6)} %select_n.47), kind=kOutput, calls=%fused_computation.54 | convolution fusion | flops 134741952 | bytes 4784388
  96.9 0.3 copy.138
  97.2 0.6 add_rsqrt_fusion
  97.8 0.1 multiply_convert_fusion
  98.0 0.0 copy-start.6
  98.0 0.7 convolution_convert_fusion
  98.7 76.8 %all_to_all.15 = bf16[32,16,2048]{2,1,0:T(8,128)(2,1)} all-to-all(bf16[32,16,2048]{2,1,0:T(8,128)(2,1)S(1)} %bitcast.125), channel_id=1, replica_groups=mesh['seq'=16,'expert'=32] {'expert'}, dimensions={0} | all-to-all | bytes 4194304 | tf_op jit(solution)/shard_map/all_to_all | solution.py:170
  175.5 6.4 %fusion.28 = f32[512,1408]{1,0:T(8,128)S(1)} fusion(bf16[512,2048]{1,0:T(8,128)(2,1)} %bitcast.129, bf16[1,2048,2112]{2,1,0:T(8,128)(2,1)} %all-gather.5.cloned.1.call-done), kind=kOutput, calls=%fused_computation.40 | convolution fusion | flops 2952790016 | bytes 10747904 | tf_op jit(solution)/shard_map/dot_general | solution.py:177
  182.0 5.2 %fusion.30 = bf16[512,2048]{1,0:T(8,128)(2,1)} fusion(bf16[1,2048,2112]{2,1,0:T(8,128)(2,1)} %all-gather.5.cloned.1.call-done, f32[512,1408]{1,0:T(8,128)S(1)} %fusion.28), kind=kOutput, calls=%fused_computation.43 | convolution fusion | flops 1479606272 | bytes 8388608 | tf_op jit(solution)/shard_map/dot_general | solution.py:182
  187.1 7.2 %all-to-all-start.2 = ((bf16[32,16,2048]{2,1,0:T(8,128)(2,1)}), bf16[32,16,2048]{2,1,0:T(8,128)(2,1)S(1)}, u32[]{:S(2)}, u32[]{:S(2)}) async-start(bf16[32,16,2048]{2,1,0:T(8,128)(2,1)} %bitcast.128), calls=%async_computation.2 | async-start | bytes 4194304 | tf_op jit(solution)/shard_map/all_to_all | solution.py:185
  194.4 0.1 reshape.126
  194.5 0.1 copy.143
  194.6 1.2 fusion.57
  195.9 0.2 select_reduce_fusion.2
  196.1 47.8 %all-to-all-done.2 = bf16[32,16,2048]{2,1,0:T(8,128)(2,1)S(1)} async-done(((bf16[32,16,2048]{2,1,0:T(8,128)(2,1)}), bf16[32,16,2048]{2,1,0:T(8,128)(2,1)S(1)}, u32[]{:S(2)}, u32[]{:S(2)}) %all-to-all-start.2) | async-done | bytes 2097184 | tf_op jit(solution)/shard_map/all_to_all | solution.py:185
  243.9 3.0 %fusion.32 = bf16[1,64,2048]{2,1,0:T(8,128)(2,1)} fusion(f32[64,512]{1,0:T(8,128)S(1)} %select_reduce_fusion.2, bf16[512,2048]{1,0:T(8,128)(2,1)S(1)} %bitcast.124, f32[64,2048]{1,0:T(8,128)} %copy-done.4, bf16[1,64,2048]{2,1,0:T(8,128)(2,1)S(1)} %copy-done.5), kind=kOutput, calls=%fused_computation.47 | convolution fusion | flops 805830656 | bytes 3276800 | tf_op jit(solution)/shard_map/dot_general | solution.py:197
  (44 shorter events, 0.3 us)
Async XLA Ops:
  6.5 79.1 %copy-start = (bf16[8,512,128]{2,1,0:T(8,128)(2,1)S(1)}, bf16[8,512,128]{2,1,0:T(8,128)(2,1)}, u32[]{:S(2)}) copy-start(bf16[8,512,128]{2,1,0:T(8,128)(2,1)} %param.21) | copy-start | bytes 3145732
  6.5 4.8 %copy-start.12 = (bf16[1024,64]{0,1:T(8,128)(2,1)S(1)}, bf16[1024,64]{0,1:T(8,128)(2,1)}, u32[]{:S(2)}) copy-start(bf16[1024,64]{0,1:T(8,128)(2,1)} %param.22) | copy-start | bytes 393220
  6.5 52.8 %all-gather.3.cloned.1.call-start = ((), (), s32[]{:S(2)}) async-start(), calls=%async_computation.3 | async-start | bytes 4177920 | tf_op jit(solution)/shard_map/all_gather | solution.py:69
  8.4 167.1 %all-gather.5.cloned.1.call-start = ((), (), s32[]{:S(2)}) async-start(), calls=%async_computation.4 | async-start | bytes 9469952 | tf_op jit(solution)/shard_map/all_gather | solution.py:172
  13.0 10.3 %copy-start.15 = (s32[1,4]{1,0:T(1,128)S(1)}, s32[1,4]{1,0:T(1,128)}, u32[]{:S(2)}) copy-start(s32[1,4]{1,0:T(1,128)} %param.19) | copy-start | bytes 52
  13.0 10.4 %copy-start.8 = (bf16[1,64,4608]{2,1,0:T(8,128)(2,1)S(1)}, bf16[1,64,4608]{2,1,0:T(8,128)(2,1)}, u32[]{:S(2)}) copy-start(bf16[1,64,4608]{2,1,0:T(8,128)(2,1)} %param.16) | copy-start | bytes 1769476
  13.0 11.1 %copy-start.16 = (s32[1,4]{1,0:T(1,128)S(1)}, s32[1,4]{1,0:T(1,128)}, u32[]{:S(2)}) copy-start(s32[1,4]{1,0:T(1,128)} %param.20) | copy-start | bytes 52
  13.0 73.0 %all-to-all-start = ((bf16[32,512,64]{1,2,0:T(8,128)(2,1)}), bf16[32,512,64]{1,2,0:T(8,128)(2,1)}, u32[]{:S(2)}, u32[]{:S(2)}) async-start(bf16[32,512,64]{1,2,0:T(8,128)(2,1)} %broadcast_in_dim.123), calls=%async_computation | async-start | bytes 4194304 | tf_op jit(solution)/shard_map/all_to_all | solution.py:131
  69.4 0.8 copy-start.7
  80.1 1.3 copy-start.3
  84.2 4.0 %copy-start.13 = (s32[1,64,6]{1,0,2:T(1,128)S(1)}, s32[1,64,6]{1,0,2:T(1,128)}, u32[]{:S(2)}) copy-start(s32[1,64,6]{1,0,2:T(1,128)} %param.25) | copy-start | bytes 4612
  84.2 4.9 %copy-start.5 = (bf16[1,64,2048]{2,1,0:T(8,128)(2,1)S(1)}, bf16[1,64,2048]{2,1,0:T(8,128)(2,1)}, u32[]{:S(2)}) copy-start(bf16[1,64,2048]{2,1,0:T(8,128)(2,1)} %param.15) | copy-start | bytes 786436
  86.1 7.9 %collective-permute-start = (bf16[32,512,64]{1,2,0:T(8,128)(2,1)}, bf16[32,512,64]{1,2,0:T(8,128)(2,1)}, u32[]{:S(2)}, u32[]{:S(2)}) collective-permute-start(bf16[32,512,64]{1,2,0:T(8,128)(2,1)} %all-to-all-done), channel_id=1, source_target_pairs={{0,32},{32,0},{64,96},{96,64},{128,160},{160,128},{192,224},{224,1... | collective-permute-start | bytes 6291464 | tf_op jit(solution)/shard_map/ppermute | solution.py:139
  88.3 0.6 copy-start.10
  94.0 3.9 %copy-start.14 = (f32[2048]{0:T(1024)S(1)}, f32[2048]{0:T(1024)}, u32[]{:S(2)}) copy-start(f32[2048]{0:T(1024)} %param.23) | copy-start | bytes 24580
  96.9 1.1 copy-start.9
  97.2 78.3 %copy-start.4 = (f32[64,2048]{1,0:T(8,128)}, f32[64,2048]{1,0:T(8,128)S(1)}, u32[]{:S(2)}) copy-start(f32[64,2048]{1,0:T(8,128)S(1)} %copy.138) | copy-start | bytes 1572868
  98.0 77.6 %copy-start.6 = (bf16[64,2048]{1,0:T(8,128)(2,1)}, bf16[64,2048]{1,0:T(8,128)(2,1)S(1)}, u32[]{:S(2)}) copy-start(bf16[64,2048]{1,0:T(8,128)(2,1)S(1)} %multiply_convert_fusion) | copy-start | bytes 786436
  187.1 7.4 %copy-start.11 = (s32[1,64,6]{2,1,0:T(8,128)S(1)}, s32[1,64,6]{2,1,0:T(8,128)}, u32[]{:S(2)}) copy-start(s32[1,64,6]{2,1,0:T(8,128)} %copy-done.10) | copy-start | bytes 4612
  187.1 56.7 %all-to-all-start.2 = ((bf16[32,16,2048]{2,1,0:T(8,128)(2,1)}), bf16[32,16,2048]{2,1,0:T(8,128)(2,1)S(1)}, u32[]{:S(2)}, u32[]{:S(2)}) async-start(bf16[32,16,2048]{2,1,0:T(8,128)(2,1)} %bitcast.128), calls=%async_computation.2 | async-start | bytes 4194304 | tf_op jit(solution)/shard_map/all_to_all | solution.py:185
Sparse Core Ops, SparseCore 0:
  9.5 49.8 all-gather.2
  61.5 59.8 all-gather.4

commit v5 on v3

--- a/solution.py
+++ b/solution.py
@@ -167,31 +167,50 @@
     ).astype(jnp.bfloat16)
     outgoing = jnp.dot(placing, normed, preferred_element_type=jnp.float32).astype(jnp.bfloat16)
     outgoing = outgoing.reshape(expert_count, capacity, model_width)
-    incoming = lax.all_to_all(outgoing, "expert", split_axis=0, concat_axis=0, tiled=True)
     in_width = expert_in.shape[2]
     full_both = lax.all_gather(
         jnp.concatenate([expert_in, expert_out], axis=2), "seq", axis=1, tiled=True
     )
     full_in, full_out = full_both[:, :, :in_width], full_both[:, :, in_width:]
-    all_rows = incoming.reshape(-1, model_width)
-    gate_up = jnp.dot(all_rows, full_in[0], preferred_element_type=jnp.float32)
-    hidden_units = gate_up.shape[1] // 2
-    active = (jax.nn.silu(gate_up[:, :hidden_units]) * gate_up[:, hidden_units:]).astype(
-        jnp.bfloat16
-    )
-    produced = lax.dot_general(
-        active, full_out[0], (((1,), (1,)), ((), ())), preferred_element_type=jnp.float32
-    ).astype(jnp.bfloat16)
-    returned = lax.all_to_all(
-        produced.reshape(-1, capacity, model_width),
-        "expert",
-        split_axis=0,
-        concat_axis=0,
-        tiled=True,
-    )
-    returned_rows = returned.reshape(-1, model_width)
-    picked = returned_rows[cell_index]
-    routed_sum = jnp.sum(gate_values[:, :, None] * picked.astype(jnp.float32), axis=1)
+    combining = jnp.sum(
+        jnp.where(cell_index[:, :, None] == cell_ids[None, None, :], gate_values[:, :, None], 0.0),
+        axis=1,
+    ).reshape(local_tokens, expert_count, capacity)
+    chunk_count = 2
+    chunk_slots = capacity // chunk_count
+    routed_parts = []
+    for chunk in range(chunk_count):
+        slots = slice(chunk * chunk_slots, (chunk + 1) * chunk_slots)
+        incoming = lax.all_to_all(
+            outgoing[:, slots], "expert", split_axis=0, concat_axis=0, tiled=True
+        )
+        all_rows = incoming.reshape(-1, model_width)
+        gate_up = jnp.dot(all_rows, full_in[0], preferred_element_type=jnp.float32)
+        hidden_units = gate_up.shape[1] // 2
+        active = (jax.nn.silu(gate_up[:, :hidden_units]) * gate_up[:, hidden_units:]).astype(
+            jnp.bfloat16
+        )
+        produced = lax.dot_general(
+            active, full_out[0], (((1,), (1,)), ((), ())), preferred_element_type=jnp.float32
+        ).astype(jnp.bfloat16)
+        returned = lax.all_to_all(
+            produced.reshape(expert_count, chunk_slots, model_width),
+            "expert",
+            split_axis=0,
+            concat_axis=0,
+            tiled=True,
+        )
+        routed_parts.append(
+            jnp.dot(
+                combining[:, :, slots].reshape(local_tokens, expert_count * chunk_slots),
+                returned.reshape(-1, model_width).astype(jnp.float32),
+                precision=lax.Precision.HIGHEST,
+                preferred_element_type=jnp.float32,
+            )
+        )
+    routed_sum = routed_parts[0]
+    for part in routed_parts[1:]:
+        routed_sum = routed_sum + part
     layer_out = (residual + routed_sum).astype(jnp.bfloat16)
     return layer_out[None]
 

time: 260 us -> 267 us (1.027)
  the two profiles are of different devices: /device:TPU:16 before, /device:TPU:8 now
where the time goes in v5:
time: 267 us; the launch traced here: 266 us
  waiting for transfers between devices  96.8 us (36%)
  blocking collectives  55.3 us (21%)
  matrix products  36.7 us (14%)
  starting transfers between devices  28.1 us (11%)
  local copies, waits for them, and re-layouts  20 us (7%)
  between operations  14.5 us (5%)
  other arithmetic  14 us (5%)
    all_to_all x1, blocking collectives, local(): lax.all_to_all(outgoing[:, slots], 'expert', split_axis=0, concat_axis=0,...  55.3 us
    all_to_all x2, waiting for transfers between devices, local(): lax.all_to_all(produced.reshape(expert_count, chunk_slots, model_width),...  44 us
    all_gather x1, waiting for transfers between devices, local(): key_stack = lax.all_gather(key_stack, 'seq', axis=1, tiled=True)  33.5 us
    all_to_all x1, waiting for transfers between devices, local(): lax.all_to_all(outgoing[:, slots], 'expert', split_axis=0, concat_axis=0,...  19.2 us
    all_to_all x2, starting transfers between devices, local(): lax.all_to_all(produced.reshape(expert_count, chunk_slots, model_width),...  10.4 us
    all_to_all x1, starting transfers between devices, local(): lax.all_to_all(jnp.broadcast_to(my_rows[None], (expert_devices,) + my_row...  10.4 us
    dot_general x2, matrix products, local(): gate_up = jnp.dot(all_rows, full_in[0], preferred_element_type=jnp.float32)  9.53 us
    dot_general x2, matrix products, local(): lax.dot_general(active, full_out[0], (((1,), (1,)), ((), ())), preferred_...  7.95 us
  transfers between devices with their start and end apart: 7, of which 4 were waited for; matrix products, arithmetic and copies ran while one was open for 24% of the time, Pallas kernels for 0%

profile of v5, /device:TPU:8, one launch (start us, length us, event | category | flops | bytes accessed | tf_op | source)
XLA Modules:
  0.0 265.7 jit_solution(1316934741753173432)
XLA Ops:
  6.5 1.8 pad_maximum_fusion.3
  8.4 1.1 copy.168
  9.5 1.8 pad_maximum_fusion.2
  11.4 1.6 broadcast_in_dim.123
  13.0 10.4 %all-to-all-start = ((bf16[32,512,64]{1,2,0:T(8,128)(2,1)}), bf16[32,512,64]{1,2,0:T(8,128)(2,1)}, u32[]{:S(2)}, u32[]{:S(2)}) async-start(bf16[32,512,64]{1,2,0:T(8,128)(2,1)} %broadcast_in_dim.123), calls=%async_computation | async-start | bytes 4194304 | tf_op jit(solution)/shard_map/all_to_all | solution.py:131
  23.4 0.2 reduce-window.18
  23.6 0.5 reshape_squeeze.3
  24.1 0.1 convert_reduce_fusion.2
  24.2 0.1 select_reduce_fusion.4
  24.3 0.8 compare_reduce_fusion
  25.8 0.1 fusion.54
  25.9 33.5 %all-gather.3.cloned.1.call-done = bf16[3,1024,576]{2,1,0:T(8,128)(2,1)} async-done(((bf16[3,64,576]{2,1,0:T(8,128)(2,1)}), bf16[3,1024,576]{2,1,0:T(8,128)(2,1)}) %all-gather.3.cloned.1.call-update) | async-done | bytes 3538960 | tf_op jit(solution)/shard_map/all_gather | solution.py:69
  59.5 1.4 slice.77
  60.9 1.5 copy.180
  62.4 3.4 %slice.76 = bf16[2,1024,576]{2,1,0:T(8,128)(2,1)} slice(bf16[3,1024,576]{2,1,0:T(8,128)(2,1)} %all-gather.3.cloned.1.call-done), slice={[1:3], [0:1024], [0:576]} | slice | bytes 4718592 | tf_op jit(solution)/shard_map/slice | solution.py:71
  65.8 3.7 %multiply_bitcast_fusion.1 = f32[64,8,1024]{2,0,1:T(8,128)} fusion(bf16[64,8,576]{2,1,0:T(8,128)(2,1)S(1)} %reshape_squeeze.3, bf16[3,1024,576]{2,1,0:T(8,128)(2,1)} %all-gather.3.cloned.1.call-done), kind=kOutput, calls=%fused_computation.56 | convolution fusion | flops 604504064 | bytes 3997696 | tf_op jit(solution)/shard_map/thk,nk->thn/dot_general | solution.py:80
  69.5 14.8 %conditional.1 = (f32[64,8,512]{2,1,0:T(8,128)}, f32[64,8]{1,0:T(8,128)S(1)}) conditional(s32[]{:T(128)} %convert_element_type.75, (s32[64]{0:T(128)S(1)}, s32[64,2]{1,0:T(8,128)S(1)}, pred[64,1024]{1,0:T(8,128)(4,1)S(1)}, bf16[64,8,576]{2,1,0:T(8,128)(2,1)S(1)}, bf16[2,1024,576]{2,1,0:T(8,128)(2,1)}, /*index=5*/f32[64,8,1024]{2,0,1:T(8,128)}, ...), branch_computations={%region_5.8_spmd, %region_8.11_spmd} | conditional | flops 2843409920 | bytes 86914120 | solution.py:121
  69.6 0.7 copy-done.7
  70.3 2.9 %copy.152 = bf16[2,1024,576]{1,2,0:T(8,128)(2,1)S(1)} copy(bf16[2,1024,576]{2,1,0:T(8,128)(2,1)} %get-tuple-element.128) | data formatting | bytes 4718592 | tf_op jit(solution)/shard_map
  73.3 2.1 multiply_bitcast_fusion
  75.5 2.2 select_reduce_fusion.1
  77.6 2.6 fusion.18
  80.2 0.1 dynamic-slice_bitcast_fusion
  80.4 1.1 copy-done.3
  81.6 2.6 fusion.19
  84.3 1.4 divide_convert_fusion
  85.7 0.4 fusion.41
  86.2 2.1 collective-permute-start
  88.3 0.1 copy.158
  88.4 0.1 eq.122
  88.6 0.5 copy-done.10
  89.0 0.1 eq.118
  89.2 0.2 copy.164
  89.4 0.9 reduce-window.19
  90.3 0.2 slice_reduce_fusion
  90.5 0.1 fusion.64
  90.6 0.1 reshape.138
  90.9 0.8 convert_reduce_fusion
  91.7 2.3 fusion.60
  94.1 2.9 %multiply_reduce_fusion = (f32[64]{0:T(128)}, f32[64,32,64]{0,2,1:T(8,128)S(1)}) fusion(f32[64,32,64]{0,2,1:T(8,128)S(1)} %bitcast.150, f32[64,2048]{0,1:S(1)} %fusion.60, bf16[512,2048]{0,1:T(8,128)(2,1)} %bitcast.23, bf16[64,1024]{1,0:T(8,128)(2,1)S(1)} %bitcast.156, s32[]{:T(128)S(6)} %select_n.47), kind=kOutput, calls=%fused_computation.64 | convolution fusion | flops 134741952 | bytes 4784388
  97.0 0.3 copy.157
  97.3 0.7 add_rsqrt_fusion
  98.0 0.1 multiply_convert_fusion
  98.1 0.7 convolution_convert_fusion
  98.8 1.2 fusion.74
  100.0 55.3 %all_to_all.25 = bf16[32,8,2048]{2,1,0:T(8,128)(2,1)} all-to-all(bf16[32,8,2048]{2,1,0:T(8,128)(2,1)S(1)} %get-tuple-element.138), channel_id=1, replica_groups=mesh['seq'=16,'expert'=32] {'expert'}, dimensions={0} | all-to-all | bytes 2097152 | tf_op jit(solution)/shard_map/all_to_all | solution.py:184
  155.4 5.2 %all-to-all-start.3 = ((bf16[32,8,2048]{2,1,0:T(8,128)(2,1)}), bf16[32,8,2048]{2,1,0:T(8,128)(2,1)S(1)}, u32[]{:S(2)}, u32[]{:S(2)}) async-start(bf16[32,8,2048]{2,1,0:T(8,128)(2,1)} %get-tuple-element.137), calls=%async_computation.3 | async-start | bytes 2097152 | tf_op jit(solution)/shard_map/all_to_all | solution.py:184
  160.6 4.8 %fusion.29 = f32[256,1408]{1,0:T(8,128)S(1)} fusion(bf16[1,2048,2112]{2,1,0:T(8,128)(2,1)} %all-gather.5.cloned.1.call-done, bf16[32,8,2048]{2,1,0:T(8,128)(2,1)} %all_to_all.25), kind=kOutput, calls=%fused_computation.41 | convolution fusion | flops 1476395008 | bytes 8257536 | tf_op jit(solution)/shard_map/dot_general | solution.py:188
  165.4 4.0 %fusion.35 = bf16[32,8,2048]{2,1,0:T(8,128)(2,1)} fusion(bf16[1,2048,2112]{2,1,0:T(8,128)(2,1)} %all-gather.5.cloned.1.call-done, f32[256,1408]{1,0:T(8,128)S(1)} %fusion.29), kind=kOutput, calls=%fused_computation.49 | convolution fusion | flops 739803136 | bytes 5767168 | tf_op jit(solution)/shard_map/dot_general | solution.py:193
  169.3 19.2 %all-to-all-done.3 = bf16[32,8,2048]{2,1,0:T(8,128)(2,1)S(1)} async-done(((bf16[32,8,2048]{2,1,0:T(8,128)(2,1)}), bf16[32,8,2048]{2,1,0:T(8,128)(2,1)S(1)}, u32[]{:S(2)}, u32[]{:S(2)}) %all-to-all-start.3) | async-done | bytes 1048608 | tf_op jit(solution)/shard_map/all_to_all | solution.py:184
  188.6 1.0 copy-done.6
  189.6 5.2 %all-to-all-start.2 = ((bf16[32,8,2048]{2,1,0:T(8,128)(2,1)}), bf16[32,8,2048]{2,1,0:T(8,128)(2,1)S(1)}, u32[]{:S(2)}, u32[]{:S(2)}) async-start(bf16[32,8,2048]{2,1,0:T(8,128)(2,1)} %fusion.35), calls=%async_computation.2 | async-start | bytes 2097152 | tf_op jit(solution)/shard_map/all_to_all | solution.py:196
  194.8 4.8 %fusion.28 = f32[256,1408]{1,0:T(8,128)S(1)} fusion(bf16[1,2048,2112]{2,1,0:T(8,128)(2,1)} %all-gather.5.cloned.1.call-done, bf16[32,8,2048]{2,1,0:T(8,128)(2,1)} %copy-done.6), kind=kOutput, calls=%fused_computation.40 | convolution fusion | flops 1476395008 | bytes 8257536 | tf_op jit(solution)/shard_map/dot_general | solution.py:188
  199.6 4.0 %fusion.34 = bf16[32,8,2048]{2,1,0:T(8,128)(2,1)} fusion(bf16[1,2048,2112]{2,1,0:T(8,128)(2,1)} %all-gather.5.cloned.1.call-done, f32[256,1408]{1,0:T(8,128)S(1)} %fusion.28), kind=kOutput, calls=%fused_computation.48 | convolution fusion | flops 739803136 | bytes 5767168 | tf_op jit(solution)/shard_map/dot_general | solution.py:193
  203.6 19.2 %all-to-all-done.2 = bf16[32,8,2048]{2,1,0:T(8,128)(2,1)S(1)} async-done(((bf16[32,8,2048]{2,1,0:T(8,128)(2,1)}), bf16[32,8,2048]{2,1,0:T(8,128)(2,1)S(1)}, u32[]{:S(2)}, u32[]{:S(2)}) %all-to-all-start.2) | async-done | bytes 1048608 | tf_op jit(solution)/shard_map/all_to_all | solution.py:196
  222.8 1.0 copy-done.4
  223.8 5.2 %all-to-all-start.4 = ((bf16[32,8,2048]{2,1,0:T(8,128)(2,1)}), bf16[32,8,2048]{2,1,0:T(8,128)(2,1)S(1)}, u32[]{:S(2)}, u32[]{:S(2)}) async-start(bf16[32,8,2048]{2,1,0:T(8,128)(2,1)} %fusion.34), calls=%async_computation.4 | async-start | bytes 2097152 | tf_op jit(solution)/shard_map/all_to_all | solution.py:196
  229.0 0.1 reshape.136
  229.3 0.2 fusion.76
  229.6 0.2 select_reduce_fusion.2
  229.7 0.1 copy.165
  229.9 2.4 convolution_bitcast_fusion.1
  232.3 24.8 %all-to-all-done.4 = bf16[32,8,2048]{2,1,0:T(8,128)(2,1)S(1)} async-done(((bf16[32,8,2048]{2,1,0:T(8,128)(2,1)}), bf16[32,8,2048]{2,1,0:T(8,128)(2,1)S(1)}, u32[]{:S(2)}, u32[]{:S(2)}) %all-to-all-start.4) | async-done | bytes 1048608 | tf_op jit(solution)/shard_map/all_to_all | solution.py:196
  257.0 1.9 fusion.39
  (56 shorter events, 0.8 us)
Async XLA Ops:
  6.5 79.2 %copy-start = (bf16[8,512,128]{2,1,0:T(8,128)(2,1)S(1)}, bf16[8,512,128]{2,1,0:T(8,128)(2,1)}, u32[]{:S(2)}) copy-start(bf16[8,512,128]{2,1,0:T(8,128)(2,1)} %param.21) | copy-start | bytes 3145732
  6.5 4.8 %copy-start.13 = (bf16[1024,64]{0,1:T(8,128)(2,1)S(1)}, bf16[1024,64]{0,1:T(8,128)(2,1)}, u32[]{:S(2)}) copy-start(bf16[1024,64]{0,1:T(8,128)(2,1)} %param.22) | copy-start | bytes 393220
  6.5 52.9 %all-gather.3.cloned.1.call-start = ((), (), s32[]{:S(2)}) async-start(), calls=%async_computation.5 | async-start | bytes 4177920 | tf_op jit(solution)/shard_map/all_gather | solution.py:69
  8.4 152.2 %all-gather.5.cloned.1.call-start = ((), (), s32[]{:S(2)}) async-start(), calls=%async_computation.6 | async-start | bytes 9469952 | tf_op jit(solution)/shard_map/all_gather | solution.py:171
  13.0 10.4 %copy-start.16 = (s32[1,4]{1,0:T(1,128)S(1)}, s32[1,4]{1,0:T(1,128)}, u32[]{:S(2)}) copy-start(s32[1,4]{1,0:T(1,128)} %param.19) | copy-start | bytes 52
  13.0 10.6 %copy-start.8 = (bf16[1,64,4608]{2,1,0:T(8,128)(2,1)S(1)}, bf16[1,64,4608]{2,1,0:T(8,128)(2,1)}, u32[]{:S(2)}) copy-start(bf16[1,64,4608]{2,1,0:T(8,128)(2,1)} %param.16) | copy-start | bytes 1769476
  13.0 11.2 %copy-start.17 = (s32[1,4]{1,0:T(1,128)S(1)}, s32[1,4]{1,0:T(1,128)}, u32[]{:S(2)}) copy-start(s32[1,4]{1,0:T(1,128)} %param.20) | copy-start | bytes 52
  13.0 73.2 %all-to-all-start = ((bf16[32,512,64]{1,2,0:T(8,128)(2,1)}), bf16[32,512,64]{1,2,0:T(8,128)(2,1)}, u32[]{:S(2)}, u32[]{:S(2)}) async-start(bf16[32,512,64]{1,2,0:T(8,128)(2,1)} %broadcast_in_dim.123), calls=%async_computation | async-start | bytes 4194304 | tf_op jit(solution)/shard_map/all_to_all | solution.py:131
  69.5 0.8 copy-start.7
  80.2 1.3 copy-start.3
  84.3 4.0 %copy-start.14 = (s32[1,64,6]{1,0,2:T(1,128)S(1)}, s32[1,64,6]{1,0,2:T(1,128)}, u32[]{:S(2)}) copy-start(s32[1,64,6]{1,0,2:T(1,128)} %param.25) | copy-start | bytes 4612
  84.3 4.9 %copy-start.5 = (bf16[1,64,2048]{2,1,0:T(8,128)(2,1)S(1)}, bf16[1,64,2048]{2,1,0:T(8,128)(2,1)}, u32[]{:S(2)}) copy-start(bf16[1,64,2048]{2,1,0:T(8,128)(2,1)} %param.15) | copy-start | bytes 786436
  86.2 7.9 %collective-permute-start = (bf16[32,512,64]{1,2,0:T(8,128)(2,1)}, bf16[32,512,64]{1,2,0:T(8,128)(2,1)}, u32[]{:S(2)}, u32[]{:S(2)}) collective-permute-start(bf16[32,512,64]{1,2,0:T(8,128)(2,1)} %all-to-all-done), channel_id=1, source_target_pairs={{0,32},{32,0},{64,96},{96,64},{128,160},{160,128},{192,224},{224,1... | collective-permute-start | bytes 6291464 | tf_op jit(solution)/shard_map/ppermute | solution.py:139
  88.4 0.6 copy-start.10
  94.1 3.9 %copy-start.15 = (f32[2048]{0:T(1024)S(1)}, f32[2048]{0:T(1024)}, u32[]{:S(2)}) copy-start(f32[2048]{0:T(1024)} %param.23) | copy-start | bytes 24580
  97.0 1.1 copy-start.9
  155.4 33.2 %all-to-all-start.3 = ((bf16[32,8,2048]{2,1,0:T(8,128)(2,1)}), bf16[32,8,2048]{2,1,0:T(8,128)(2,1)S(1)}, u32[]{:S(2)}, u32[]{:S(2)}) async-start(bf16[32,8,2048]{2,1,0:T(8,128)(2,1)} %get-tuple-element.137), calls=%async_computation.3 | async-start | bytes 2097152 | tf_op jit(solution)/shard_map/all_to_all | solution.py:184
  188.6 1.0 copy-start.6
  189.6 33.2 %all-to-all-start.2 = ((bf16[32,8,2048]{2,1,0:T(8,128)(2,1)}), bf16[32,8,2048]{2,1,0:T(8,128)(2,1)S(1)}, u32[]{:S(2)}, u32[]{:S(2)}) async-start(bf16[32,8,2048]{2,1,0:T(8,128)(2,1)} %fusion.35), calls=%async_computation.2 | async-start | bytes 2097152 | tf_op jit(solution)/shard_map/all_to_all | solution.py:196
  199.6 29.6 %copy-start.11 = (s32[1,64,6]{2,1,0:T(8,128)S(1)}, s32[1,64,6]{2,1,0:T(8,128)}, u32[]{:S(2)}) copy-start(s32[1,64,6]{2,1,0:T(8,128)} %copy-done.10) | copy-start | bytes 4612
  199.6 29.7 %copy-start.12 = (bf16[2048,32]{0,1:T(8,128)(2,1)S(1)}, bf16[2048,32]{0,1:T(8,128)(2,1)}, u32[]{:S(2)}) copy-start(bf16[2048,32]{0,1:T(8,128)(2,1)} %param.24) | copy-start | bytes 393220
  222.8 1.0 copy-start.4
  223.8 33.2 %all-to-all-start.4 = ((bf16[32,8,2048]{2,1,0:T(8,128)(2,1)}), bf16[32,8,2048]{2,1,0:T(8,128)(2,1)S(1)}, u32[]{:S(2)}, u32[]{:S(2)}) async-start(bf16[32,8,2048]{2,1,0:T(8,128)(2,1)} %fusion.34), calls=%async_computation.4 | async-start | bytes 2097152 | tf_op jit(solution)/shard_map/all_to_all | solution.py:196
Sparse Core Ops, SparseCore 0:
  9.5 49.9 all-gather.2
  61.6 59.8 all-gather.4

commit v6 on v4

--- a/solution.py
+++ b/solution.py
@@ -57,68 +57,32 @@
         jnp.where(my_requests[:, None] == request_ids[None, :], prefix_of[0][None, :], 0), axis=1
     )
     prefix_pick = chosen[:, None] == jnp.arange(2, dtype=jnp.int32)[None, :]
-    single_prefix = jnp.all(chosen == chosen[0])
-    my_prefix = chosen[0]
     query_rows = queries[0].reshape(local_tokens, head_count, key_width)
-    start_state = (
-        jnp.full((local_tokens, head_count), big_negative, jnp.float32),
-        jnp.zeros((local_tokens, head_count), jnp.float32),
-        jnp.zeros((local_tokens, head_count, latent_width), jnp.float32),
-    )
     key_stack = jnp.concatenate([suffix_latent, prefix_latent], axis=0)
     key_stack = lax.all_gather(key_stack, "seq", axis=1, tiled=True)
-    suffix_piece = key_stack[:1]
-    prefix_piece = key_stack[1:]
-    piece_rows = suffix_piece.shape[1]
-    suffix_keys = suffix_piece[0]
+    block_count, piece_rows = key_stack.shape[0], key_stack.shape[1]
     key_positions = jnp.arange(piece_rows, dtype=jnp.int32)
     key_requests = request_of(key_positions, request_ends)
     suffix_allowed = (key_requests[None, :] == my_requests[:, None]) & (
         key_positions[None, :] <= my_positions[:, None]
     )
-    suffix_scores = (
-        jnp.einsum("thk,nk->thn", query_rows, suffix_keys, preferred_element_type=jnp.float32)
+    prefix_allowed = jnp.broadcast_to(
+        prefix_pick[:, :, None], (local_tokens, block_count - 1, piece_rows)
+    )
+    allowed = jnp.concatenate([suffix_allowed[:, None, :], prefix_allowed], axis=1)[:, None]
+    scores = (
+        jnp.einsum("thk,pnk->thpn", query_rows, key_stack, preferred_element_type=jnp.float32)
         * qk_scale
     )
-
-    def one_prefix(running_state):
-        chosen_keys = lax.dynamic_index_in_dim(prefix_piece, my_prefix, 0, keepdims=False)
-        prefix_scores = (
-            jnp.einsum("thk,nk->thn", query_rows, chosen_keys, preferred_element_type=jnp.float32)
-            * qk_scale
-        )
-        scores = jnp.concatenate([suffix_scores, prefix_scores], axis=2)
-        every_key = jnp.ones((local_tokens, piece_rows), dtype=bool)
-        allowed = jnp.concatenate([suffix_allowed, every_key], axis=1)[:, None, :]
-        values = jnp.concatenate(
-            [suffix_keys[:, :latent_width], chosen_keys[:, :latent_width]], axis=0
-        )
-        return merge_scores(running_state, scores, allowed, values)
-
-    def two_prefixes(running_state):
-        prefix_scores = (
-            jnp.einsum(
-                "thk,pnk->thpn", query_rows, prefix_piece, preferred_element_type=jnp.float32
-            )
-            * qk_scale
-        )
-        scores = jnp.concatenate(
-            [suffix_scores, prefix_scores.reshape(local_tokens, head_count, 2 * piece_rows)], axis=2
-        )
-        prefix_allowed = jnp.broadcast_to(
-            prefix_pick[:, :, None], (local_tokens, 2, piece_rows)
-        ).reshape(local_tokens, 2 * piece_rows)
-        allowed = jnp.concatenate([suffix_allowed, prefix_allowed], axis=1)[:, None, :]
-        values = jnp.concatenate(
-            [
-                suffix_keys[:, :latent_width],
-                prefix_piece[:, :, :latent_width].reshape(2 * piece_rows, latent_width),
-            ],
-            axis=0,
-        )
-        return merge_scores(running_state, scores, allowed, values)
-
-    final_max, final_sum, final_acc = lax.cond(single_prefix, one_prefix, two_prefixes, start_state)
+    final_max = jnp.max(jnp.where(allowed, scores, big_negative), axis=(2, 3))
+    weights = jnp.where(allowed, jnp.exp(scores - final_max[:, :, None, None]), 0.0)
+    final_sum = jnp.sum(weights, axis=(2, 3))
+    final_acc = jnp.einsum(
+        "thpn,pnl->thl",
+        weights.astype(jnp.bfloat16),
+        key_stack[:, :, :latent_width],
+        preferred_element_type=jnp.float32,
+    )
     latent_out = (final_acc / final_sum[:, :, None]).astype(jnp.bfloat16)
     value_out = jnp.einsum(
         "thl,hlv->thv", latent_out, value_up, preferred_element_type=jnp.float32

time: 255 us -> 233 us (0.914)
  the two profiles are of different devices: /device:TPU:16 before, /device:TPU:8 now
where the time goes in v6:
time: 233 us; the launch traced here: 232 us
  waiting for transfers between devices  79.9 us (34%)
  blocking collectives  61 us (26%)
  matrix products  31.3 us (13%)
  starting transfers between devices  17.9 us (8%)
  local copies, waits for them, and re-layouts  17.2 us (7%)
  between operations  13.7 us (6%)
  other arithmetic  11.2 us (5%)
    all_to_all x1, blocking collectives, local(): lax.all_to_all(outgoing, 'expert', split_axis=0, concat_axis=0, tiled=True)  61 us
    all_to_all x1, waiting for transfers between devices, local(): lax.all_to_all(produced.reshape(-1, capacity, model_width), 'expert', spl...  47.7 us
    all_gather x1, waiting for transfers between devices, local(): key_stack = lax.all_gather(key_stack, 'seq', axis=1, tiled=True)  32.2 us
    all_to_all x1, starting transfers between devices, local(): lax.all_to_all(jnp.broadcast_to(my_rows[None], (expert_devices,) + my_row...  10.3 us
    dot_general x1, matrix products, local(): jnp.einsum('thl,hlv->thv', latent_out, value_up, preferred_element_type=j...  6.5 us
    dot_general x1, matrix products, local(): gate_up = jnp.dot(all_rows, full_in[0], preferred_element_type=jnp.float32)  6.42 us
    all_to_all x1, starting transfers between devices, local(): lax.all_to_all(produced.reshape(-1, capacity, model_width), 'expert', spl...  5.43 us
    unnamed x29, local copies, waits for them, and re-layouts  5.19 us
  transfers between devices with their start and end apart: 5, of which 2 were waited for; matrix products, arithmetic and copies ran while one was open for 17% of the time, Pallas kernels for 0%

profile of v6, /device:TPU:8, one launch (start us, length us, event | category | flops | bytes accessed | tf_op | source)
XLA Modules:
  0.0 232.3 jit_solution(14968233654710048534)
XLA Ops:
  6.5 0.0 copy-start
  6.5 0.0 all-gather.3.cloned.1.call-start
  6.5 1.8 pad_maximum_fusion.1
  8.3 0.0 all-gather.3.cloned.1.call-update
  8.3 0.0 all-gather.5.cloned.1.call-start
  8.4 1.1 copy.59
  9.5 1.8 pad_maximum_fusion
  11.3 0.0 all-gather.5.cloned.1.call-update
  11.3 0.8 constant_dynamic-slice_fusion
  12.2 1.6 broadcast_in_dim.58
  13.7 10.3 %all-to-all-start = ((bf16[32,512,64]{1,2,0:T(8,128)(2,1)}), bf16[32,512,64]{1,2,0:T(8,128)(2,1)S(1)}, u32[]{:S(2)}, u32[]{:S(2)}) async-start(bf16[32,512,64]{1,2,0:T(8,128)(2,1)} %broadcast_in_dim.58), calls=%async_computation | async-start | bytes 4194304 | tf_op jit(solution)/shard_map/all_to_all | solution.py:95
  24.1 0.0 copy-done.11
  24.1 0.2 reduce-window.18
  24.2 2.4 %reshape_squeeze.3 = bf16[64,8,576]{2,1,0:T(8,128)(2,1)} reshape(bf16[1,64,4608]{2,1,0:T(8,128)(2,1)} %param.14) | data formatting | bytes 1179648 | tf_op jit(solution)/shard_map/reshape;squeeze | solution.py:60
  26.7 0.1 convert_reduce_fusion.1
  26.8 0.1 convert_reduce_fusion.2
  26.9 0.0 copy-done.12
  26.9 0.1 select_reduce_fusion.2
  27.0 0.1 fusion.32
  27.1 0.1 broadcast_in_dim.62
  27.2 0.0 copy-start.6
  27.2 32.2 %all-gather.3.cloned.1.call-done = bf16[3,1024,576]{2,1,0:T(8,128)(2,1)} async-done(((bf16[3,64,576]{2,1,0:T(8,128)(2,1)}), bf16[3,1024,576]{2,1,0:T(8,128)(2,1)}) %all-gather.3.cloned.1.call-update) | async-done | bytes 3538960 | tf_op jit(solution)/shard_map/all_gather | solution.py:62
  59.5 5.2 %fusion = (f32[64,8]{0,1:T(8,128)S(1)}, f32[3,1024,64,8]{1,2,3,0:T(8,128)S(1)}) fusion(pred[64,3,1024]{2,0,1:T(8,128)(4,1)S(1)} %pad_add_fusion, bf16[64,8,576]{2,1,0:T(8,128)(2,1)} %reshape_squeeze.3, bf16[3,1024,576]{2,1,0:T(8,128)(2,1)} %all-gather.3.cloned.1.call-done), kind=kOutput, calls=%fused_computation.2 | convolution fusion | flops 1816657408 | bytes 10618880 | tf_op jit(solution)/shard_map/thk,pnk->thpn/dot_general | solution.py:74
  64.7 0.0 copy-start.1
  64.7 0.0 copy-done.6
  64.7 2.7 %copy-done.1 = f32[3,1024,64,8]{1,2,3,0:T(8,128)} copy-done((f32[3,1024,64,8]{1,2,3,0:T(8,128)}, f32[3,1024,64,8]{1,2,3,0:T(8,128)S(1)}, u32[]{:S(2)}) %copy-start.1) | copy-done | bytes 6291480
  67.3 1.6 fusion.4
  69.0 0.0 copy-done
  69.0 6.5 %fusion.22 = bf16[8,8,8,128]{3,2,1,0:T(8,128)(2,1)} fusion(bf16[8,512,128]{2,1,0:T(8,128)(2,1)S(1)} %copy-done, bf16[3,1024,576]{2,1,0:T(8,128)(2,1)} %all-gather.3.cloned.1.call-done, f32[3,1024,64,8]{1,2,3,0:T(8,128)} %copy-done.1, f32[64,8]{0,1:T(8,128)S(1)} %get-tuple-element.11, pred[64,3,1024]{2,0,1:T(8,128)(4,1)} %copy-done.6, f32[64,8]{0,1:T(8,128)S(1)} %fusion.4), kind=kOutput, calls=%fused_computation.28 | convolution fusion | flops 1684602880 | bytes 10817536 | tf_op jit(solution)/shard_map/thl,hlv->thv/dot_general | solution.py:87
  75.5 0.9 copy.76
  76.4 0.0 all-to-all-done
  76.4 2.1 collective-permute-start
  78.6 0.0 copy-done.9
  78.6 0.7 copy.51
  79.3 0.9 eq.121
  80.2 0.9 eq.125
  81.1 1.2 copy.57
  82.3 0.6 fusion.41
  82.9 2.6 %reduce-window.19 = s32[32,3,128]{2,0,1:T(8,128)} reduce-window(s32[32,3,128]{2,0,1:T(8,128)} %fusion.41, s32[]{:T(128)} %constant.19.clone.1), window={size=1x1x128 pad=0_0x0_0x127_0}, to_apply=%region_6.7 | reduce-window | flops 1560576 | bytes 98308 | tf_op jit(solution)/shard_map/reduce-window.1
  85.5 1.0 slice_reduce_fusion
  86.6 0.9 fusion.40
  87.5 0.8 reshape.198
  88.3 0.8 copy.58
  89.1 0.8 convert_reduce_fusion
  89.9 0.7 fusion.36
  90.6 0.0 collective-permute-done
  90.6 0.0 copy-start.10
  90.6 0.0 copy-start.7
  90.6 2.5 %multiply_reduce_fusion = (f32[64]{0:T(128)S(1)}, f32[64,32,64]{0,2,1:T(8,128)S(1)}) fusion(f32[64,32,64]{0,2,1:T(8,128)S(1)} %bitcast.134, f32[64,2048]{0,1:S(1)} %fusion.36, bf16[512,2048]{0,1:T(8,128)(2,1)} %bitcast.16, bf16[64,1024]{1,0:T(8,128)(2,1)S(1)} %bitcast.139, s32[]{:T(128)S(6)} %select_n.38), kind=kOutput, calls=%fused_computation.29 | convolution fusion | flops 134741952 | bytes 4784388
  93.1 0.3 copy.50
  93.5 0.1 multiply_convert_fusion
  93.6 0.0 copy-start.5
  93.6 0.7 copy-done.5
  94.3 0.7 convolution_convert_fusion
  95.1 61.0 %all_to_all.15 = bf16[32,16,2048]{2,1,0:T(8,128)(2,1)} all-to-all(bf16[32,16,2048]{2,1,0:T(8,128)(2,1)S(1)} %bitcast.133), channel_id=1, replica_groups=mesh['seq'=16,'expert'=32] {'expert'}, dimensions={0} | all-to-all | bytes 4194304 | tf_op jit(solution)/shard_map/all_to_all | solution.py:134
  156.1 6.4 %fusion.3 = f32[512,1408]{1,0:T(8,128)S(1)} fusion(bf16[512,2048]{1,0:T(8,128)(2,1)} %bitcast.137, bf16[1,2048,2112]{2,1,0:T(8,128)(2,1)} %all-gather.5.cloned.1.call-done), kind=kOutput, calls=%fused_computation.6 | convolution fusion | flops 2952790016 | bytes 10747904 | tf_op jit(solution)/shard_map/dot_general | solution.py:141
  162.5 5.2 %fusion.15 = bf16[512,2048]{1,0:T(8,128)(2,1)} fusion(bf16[1,2048,2112]{2,1,0:T(8,128)(2,1)} %all-gather.5.cloned.1.call-done, f32[512,1408]{1,0:T(8,128)S(1)} %fusion.3), kind=kOutput, calls=%fused_computation.19 | convolution fusion | flops 1479606272 | bytes 8388608 | tf_op jit(solution)/shard_map/dot_general | solution.py:146
  167.7 5.4 %all-to-all-start.2 = ((bf16[32,16,2048]{2,1,0:T(8,128)(2,1)}), bf16[32,16,2048]{2,1,0:T(8,128)(2,1)S(1)}, u32[]{:S(2)}, u32[]{:S(2)}) async-start(bf16[32,16,2048]{2,1,0:T(8,128)(2,1)} %bitcast.136), calls=%async_computation.2 | async-start | bytes 4194304 | tf_op jit(solution)/shard_map/all_to_all | solution.py:149
  173.1 0.1 reshape.197
  173.3 0.1 copy.55
  173.4 1.2 fusion.52
  174.6 0.2 select_reduce_fusion
  174.8 47.7 %all-to-all-done.2 = bf16[32,16,2048]{2,1,0:T(8,128)(2,1)S(1)} async-done(((bf16[32,16,2048]{2,1,0:T(8,128)(2,1)}), bf16[32,16,2048]{2,1,0:T(8,128)(2,1)S(1)}, u32[]{:S(2)}, u32[]{:S(2)}) %all-to-all-start.2) | async-done | bytes 2097184 | tf_op jit(solution)/shard_map/all_to_all | solution.py:149
  222.5 3.0 %fusion.17 = bf16[1,64,2048]{2,1,0:T(8,128)(2,1)} fusion(f32[64,512]{1,0:T(8,128)S(1)} %select_reduce_fusion, bf16[512,2048]{1,0:T(8,128)(2,1)S(1)} %bitcast.132, f32[64,2048]{1,0:T(8,128)} %copy-done.2, bf16[1,64,2048]{2,1,0:T(8,128)(2,1)S(1)} %copy-done.4), kind=kOutput, calls=%fused_computation.23 | convolution fusion | flops 805830656 | bytes 3276800 | tf_op jit(solution)/shard_map/dot_general | solution.py:161
  (26 shorter events, 0.2 us)
Async XLA Ops:
  6.5 62.5 %copy-start = (bf16[8,512,128]{2,1,0:T(8,128)(2,1)S(1)}, bf16[8,512,128]{2,1,0:T(8,128)(2,1)}, u32[]{:S(2)}) copy-start(bf16[8,512,128]{2,1,0:T(8,128)(2,1)} %param.19) | copy-start | bytes 3145732
  6.5 52.9 %all-gather.3.cloned.1.call-start = ((), (), s32[]{:S(2)}) async-start(), calls=%async_computation.3 | async-start | bytes 4177920 | tf_op jit(solution)/shard_map/all_gather | solution.py:62
  8.3 147.7 %all-gather.5.cloned.1.call-start = ((), (), s32[]{:S(2)}) async-start(), calls=%async_computation.4 | async-start | bytes 9469952 | tf_op jit(solution)/shard_map/all_gather | solution.py:136
  12.2 11.9 %copy-start.11 = (s32[1,4]{1,0:T(1,128)S(1)}, s32[1,4]{1,0:T(1,128)}, u32[]{:S(2)}) copy-start(s32[1,4]{1,0:T(1,128)} %param.17) | copy-start | bytes 52
  13.7 13.1 %copy-start.12 = (s32[1,4]{1,0:T(1,128)S(1)}, s32[1,4]{1,0:T(1,128)}, u32[]{:S(2)}) copy-start(s32[1,4]{1,0:T(1,128)} %param.18) | copy-start | bytes 52
  13.7 62.7 %all-to-all-start = ((bf16[32,512,64]{1,2,0:T(8,128)(2,1)}), bf16[32,512,64]{1,2,0:T(8,128)(2,1)S(1)}, u32[]{:S(2)}, u32[]{:S(2)}) async-start(bf16[32,512,64]{1,2,0:T(8,128)(2,1)} %broadcast_in_dim.58), calls=%async_computation | async-start | bytes 4194304 | tf_op jit(solution)/shard_map/all_to_all | solution.py:95
  27.2 37.4 %copy-start.6 = (pred[64,3,1024]{2,0,1:T(8,128)(4,1)}, pred[64,3,1024]{2,0,1:T(8,128)(4,1)S(1)}, u32[]{:S(2)}) copy-start(pred[64,3,1024]{2,0,1:T(8,128)(4,1)S(1)} %pad_add_fusion) | copy-start | bytes 589828
  64.7 2.7 %copy-start.1 = (f32[3,1024,64,8]{1,2,3,0:T(8,128)}, f32[3,1024,64,8]{1,2,3,0:T(8,128)S(1)}, u32[]{:S(2)}) copy-start(f32[3,1024,64,8]{1,2,3,0:T(8,128)S(1)} %get-tuple-element.12) | copy-start | bytes 18874372
  69.0 9.6 %copy-start.9 = (s32[1,64,6]{1,0,2:T(1,128)S(1)}, s32[1,64,6]{1,0,2:T(1,128)}, u32[]{:S(2)}) copy-start(s32[1,64,6]{1,0,2:T(1,128)} %param.23) | copy-start | bytes 4612
  69.0 12.1 %copy-start.4 = (bf16[1,64,2048]{2,1,0:T(8,128)(2,1)S(1)}, bf16[1,64,2048]{2,1,0:T(8,128)(2,1)}, u32[]{:S(2)}) copy-start(bf16[1,64,2048]{2,1,0:T(8,128)(2,1)} %param.13) | copy-start | bytes 786436
  76.4 14.2 %collective-permute-start = (bf16[32,512,64]{1,2,0:T(8,128)(2,1)S(1)}, bf16[32,512,64]{1,2,0:T(8,128)(2,1)}, u32[]{:S(2)}, u32[]{:S(2)}) collective-permute-start(bf16[32,512,64]{1,2,0:T(8,128)(2,1)S(1)} %all-to-all-done), channel_id=1, source_target_pairs={{0,32},{32,0},{64,96},{96,64},{128,160},{160,128},{192,224},{224,1... | collective-permute-start | bytes 6291464 | tf_op jit(solution)/shard_map/ppermute | solution.py:103
  89.1 1.5 copy-start.3
  90.6 2.9 %copy-start.10 = (f32[2048]{0:T(1024)S(1)}, f32[2048]{0:T(1024)}, u32[]{:S(2)}) copy-start(f32[2048]{0:T(1024)} %param.21) | copy-start | bytes 24580
  90.6 3.7 %copy-start.7 = (s32[512,64]{0,1:T(8,128)S(1)}, s32[512,64]{0,1:T(8,128)}, u32[]{:S(2)}) copy-start(s32[512,64]{0,1:T(8,128)} %convert_reduce_fusion) | copy-start | bytes 393220
  93.5 62.6 %copy-start.2 = (f32[64,2048]{1,0:T(8,128)}, f32[64,2048]{1,0:T(8,128)S(1)}, u32[]{:S(2)}) copy-start(f32[64,2048]{1,0:T(8,128)S(1)} %copy.50) | copy-start | bytes 1572868
  93.6 0.7 copy-start.5
  167.7 5.6 %copy-start.8 = (s32[1,64,6]{2,1,0:T(8,128)S(1)}, s32[1,64,6]{2,1,0:T(8,128)}, u32[]{:S(2)}) copy-start(s32[1,64,6]{2,1,0:T(8,128)} %copy.51) | copy-start | bytes 4612
  167.7 54.8 %all-to-all-start.2 = ((bf16[32,16,2048]{2,1,0:T(8,128)(2,1)}), bf16[32,16,2048]{2,1,0:T(8,128)(2,1)S(1)}, u32[]{:S(2)}, u32[]{:S(2)}) async-start(bf16[32,16,2048]{2,1,0:T(8,128)(2,1)} %bitcast.136), calls=%async_computation.2 | async-start | bytes 4194304 | tf_op jit(solution)/shard_map/all_to_all | solution.py:149
Sparse Core Ops, SparseCore 0:
  9.5 49.9 all-gather.2
  61.6 59.8 all-gather.4

commit v7 on v6

--- a/solution.py
+++ b/solution.py
@@ -100,14 +100,16 @@
         tiled=True,
     )
     my_blocks, value_out = lax.optimization_barrier((my_blocks, value_out))
-    other_blocks = lax.ppermute(
-        my_blocks, "seq", perm=[(i, i ^ 1) for i in range(seq_count)]
-    )
+    pair = [(i, i ^ 1) for i in range(seq_count)]
     my_part = lax.dynamic_slice_in_dim(value_out, core * half_rows, half_rows, axis=1)
     other_part = lax.dynamic_slice_in_dim(value_out, (1 - core) * half_rows, half_rows, axis=1)
+    partner_part = lax.ppermute(other_part, "seq", perm=pair)
+    partner_partial = jnp.einsum(
+        "tr,jrc->tjc", partner_part, my_blocks, preferred_element_type=jnp.float32
+    )
     projected = (
         jnp.einsum("tr,jrc->tjc", my_part, my_blocks, preferred_element_type=jnp.float32)
-        + jnp.einsum("tr,jrc->tjc", other_part, other_blocks, preferred_element_type=jnp.float32)
+        + lax.ppermute(partner_partial, "seq", perm=pair)
     ).reshape(local_tokens, model_width)
     residual = hidden[0].astype(jnp.float32) + projected
     normed = (

time: 233 us -> 231 us (level)
  the two profiles are of different devices: /device:TPU:8 before, /device:TPU:16 now
where the time goes in v7:
time: 231 us; the launch traced here: 230 us
  waiting for transfers between devices  78.7 us (34%)
  blocking collectives  58.7 us (25%)
  matrix products  32.2 us (14%)
  starting transfers between devices  22.2 us (10%)
  local copies, waits for them, and re-layouts  14.9 us (6%)
  between operations  13.8 us (6%)
  other arithmetic  9.75 us (4%)
    all_to_all x1, blocking collectives, local(): lax.all_to_all(outgoing, 'expert', split_axis=0, concat_axis=0, tiled=True)  58.7 us
    all_to_all x1, waiting for transfers between devices, local(): lax.all_to_all(produced.reshape(-1, capacity, model_width), 'expert', spl...  47.9 us
    all_gather x1, waiting for transfers between devices, local(): key_stack = lax.all_gather(key_stack, 'seq', axis=1, tiled=True)  30.7 us
    all_to_all x1, starting transfers between devices, local(): lax.all_to_all(jnp.broadcast_to(my_rows[None], (expert_devices,) + my_row...  10.2 us
    all_to_all x1, starting transfers between devices, local(): lax.all_to_all(produced.reshape(-1, capacity, model_width), 'expert', spl...  7.63 us
    dot_general x1, matrix products, local(): gate_up = jnp.dot(all_rows, full_in[0], preferred_element_type=jnp.float32)  6.42 us
    dot_general x1, matrix products, local(): jnp.einsum('thl,hlv->thv', latent_out, value_up, preferred_element_type=j...  6.36 us
    dot_general x1, matrix products, local(): jnp.einsum('thk,pnk->thpn', query_rows, key_stack, preferred_element_type...  5.18 us
  transfers between devices with their start and end apart: 6, of which 2 were waited for; matrix products, arithmetic and copies ran while one was open for 16% of the time, Pallas kernels for 0%

profile of v7, /device:TPU:16, one launch (start us, length us, event | category | flops | bytes accessed | tf_op | source)
XLA Modules:
  0.0 230.2 jit_solution(13872588368954222305)
XLA Ops:
  6.5 0.0 copy-start
  6.5 0.0 all-gather.3.cloned.1.call-start
  6.5 1.8 pad_maximum_fusion.1
  8.3 0.0 all-gather.3.cloned.1.call-update
  8.3 0.0 all-gather.5.cloned.1.call-start
  8.4 1.1 copy.63
  9.5 1.8 pad_maximum_fusion
  11.3 0.0 all-gather.5.cloned.1.call-update
  11.3 0.8 constant_dynamic-slice_fusion.1
  12.2 1.6 broadcast_in_dim.58
  13.8 10.2 %all-to-all-start = ((bf16[32,512,64]{1,2,0:T(8,128)(2,1)}), bf16[32,512,64]{1,2,0:T(8,128)(2,1)S(1)}, u32[]{:S(2)}, u32[]{:S(2)}) async-start(bf16[32,512,64]{1,2,0:T(8,128)(2,1)} %broadcast_in_dim.58), calls=%async_computation | async-start | bytes 4194304 | tf_op jit(solution)/shard_map/all_to_all | solution.py:95
  24.0 0.1 copy.55
  24.1 0.1 eq.121
  24.2 0.1 eq.125
  24.3 0.0 copy-done.12
  24.4 0.2 reduce-window.18
  24.5 2.4 %reshape_squeeze.3 = bf16[64,8,576]{2,1,0:T(8,128)(2,1)} reshape(bf16[1,64,4608]{2,1,0:T(8,128)(2,1)} %param.14) | data formatting | bytes 1179648 | tf_op jit(solution)/shard_map/reshape;squeeze | solution.py:60
  27.0 0.9 reduce-window.19
  27.9 0.2 slice_reduce_fusion
  28.1 0.1 convert_reduce_fusion.1
  28.2 0.1 convert_reduce_fusion.2
  28.3 0.1 select_reduce_fusion.2
  28.4 0.1 fusion.32
  28.5 0.0 copy-done.7
  28.5 0.0 copy-done.9
  28.6 0.1 broadcast_in_dim.62
  28.7 30.7 %all-gather.3.cloned.1.call-done = bf16[3,1024,576]{2,1,0:T(8,128)(2,1)} async-done(((bf16[3,64,576]{2,1,0:T(8,128)(2,1)}), bf16[3,1024,576]{2,1,0:T(8,128)(2,1)}) %all-gather.3.cloned.1.call-update) | async-done | bytes 3538960 | tf_op jit(solution)/shard_map/all_gather | solution.py:62
  59.4 5.2 %fusion = (f32[64,8]{0,1:T(8,128)S(1)}, f32[3,1024,64,8]{1,2,3,0:T(8,128)S(1)}) fusion(pred[64,3,1024]{2,0,1:T(8,128)(4,1)S(1)} %pad_add_fusion, bf16[64,8,576]{2,1,0:T(8,128)(2,1)} %reshape_squeeze.3, bf16[3,1024,576]{2,1,0:T(8,128)(2,1)} %all-gather.3.cloned.1.call-done), kind=kOutput, calls=%fused_computation.2 | convolution fusion | flops 1816657408 | bytes 10618880 | tf_op jit(solution)/shard_map/thk,pnk->thpn/dot_general | solution.py:74
  64.6 2.7 %copy-done.1 = f32[3,1024,64,8]{1,2,3,0:T(8,128)} copy-done((f32[3,1024,64,8]{1,2,3,0:T(8,128)}, f32[3,1024,64,8]{1,2,3,0:T(8,128)S(1)}, u32[]{:S(2)}) %copy-start.1) | copy-done | bytes 6291480
  67.3 1.6 fusion.4
  69.0 6.4 %fusion.22 = bf16[8,8,8,128]{3,2,1,0:T(8,128)(2,1)} fusion(bf16[8,512,128]{2,1,0:T(8,128)(2,1)S(1)} %copy-done, bf16[3,1024,576]{2,1,0:T(8,128)(2,1)} %all-gather.3.cloned.1.call-done, f32[3,1024,64,8]{1,2,3,0:T(8,128)} %copy-done.1, f32[64,8]{0,1:T(8,128)S(1)} %get-tuple-element.11, pred[64,3,1024]{2,0,1:T(8,128)(4,1)S(1)} %pad_add_fusion, ...), kind=kOutput, calls=%fused_computation.28 | convolution fusion | flops 1684602880 | bytes 10817536 | tf_op jit(solution)/shard_map/thl,hlv->thv/dot_general | solution.py:87
  75.3 1.0 copy.81
  76.3 0.0 copy-start.6
  76.3 0.0 all-to-all-done
  76.3 0.6 constant_dynamic-slice_fusion
  77.0 2.1 collective-permute-start
  79.1 0.9 fusion.40
  80.0 0.8 reshape.198
  80.8 0.8 copy.62
  81.6 0.0 collective-permute-done
  81.6 2.6 %fusion.33 = f32[64,32,64]{0,2,1:T(8,128)} fusion(bf16[32,512,64]{1,2,0:T(8,128)(2,1)S(1)} %all-to-all-done, bf16[64,512]{1,0:T(8,128)(2,1)} %collective-permute-done), kind=kOutput, calls=%fused_computation.49 | convolution fusion | flops 134217728 | bytes 2686976 | tf_op jit(solution)/shard_map/tr,jrc->tjc/dot_general | solution.py:107
  84.2 2.2 collective-permute-start.1
  86.4 1.2 copy.61
  87.5 0.0 copy-done.6
  87.5 0.1 convert_reduce_fusion
  87.7 1.6 fusion.36
  89.3 0.0 copy-start.11
  89.3 0.0 collective-permute-done.1
  89.4 1.6 multiply_reduce_fusion
  90.9 0.3 copy.54
  91.3 0.1 multiply_convert_fusion
  91.4 0.0 copy-start.5
  91.4 0.7 copy-done.5
  92.1 0.7 convolution_convert_fusion
  92.9 58.7 %all_to_all.15 = bf16[32,16,2048]{2,1,0:T(8,128)(2,1)} all-to-all(bf16[32,16,2048]{2,1,0:T(8,128)(2,1)S(1)} %bitcast.129), channel_id=1, replica_groups=mesh['seq'=16,'expert'=32] {'expert'}, dimensions={0} | all-to-all | bytes 4194304 | tf_op jit(solution)/shard_map/all_to_all | solution.py:136
  151.6 6.4 %fusion.3 = f32[512,1408]{1,0:T(8,128)S(1)} fusion(bf16[512,2048]{1,0:T(8,128)(2,1)} %bitcast.133, bf16[1,2048,2112]{2,1,0:T(8,128)(2,1)} %all-gather.5.cloned.1.call-done), kind=kOutput, calls=%fused_computation.6 | convolution fusion | flops 2952790016 | bytes 10747904 | tf_op jit(solution)/shard_map/dot_general | solution.py:143
  158.1 5.2 %fusion.15 = bf16[512,2048]{1,0:T(8,128)(2,1)} fusion(bf16[1,2048,2112]{2,1,0:T(8,128)(2,1)} %all-gather.5.cloned.1.call-done, f32[512,1408]{1,0:T(8,128)S(1)} %fusion.3), kind=kOutput, calls=%fused_computation.19 | convolution fusion | flops 1479606272 | bytes 8388608 | tf_op jit(solution)/shard_map/dot_general | solution.py:148
  163.2 7.6 %all-to-all-start.2 = ((bf16[32,16,2048]{2,1,0:T(8,128)(2,1)}), bf16[32,16,2048]{2,1,0:T(8,128)(2,1)S(1)}, u32[]{:S(2)}, u32[]{:S(2)}) async-start(bf16[32,16,2048]{2,1,0:T(8,128)(2,1)} %bitcast.132), calls=%async_computation.2 | async-start | bytes 4194304 | tf_op jit(solution)/shard_map/all_to_all | solution.py:151
  170.9 0.1 reshape.197
  171.0 0.1 copy.59
  171.1 1.2 fusion.51
  172.4 0.2 select_reduce_fusion
  172.6 47.9 %all-to-all-done.2 = bf16[32,16,2048]{2,1,0:T(8,128)(2,1)S(1)} async-done(((bf16[32,16,2048]{2,1,0:T(8,128)(2,1)}), bf16[32,16,2048]{2,1,0:T(8,128)(2,1)S(1)}, u32[]{:S(2)}, u32[]{:S(2)}) %all-to-all-start.2) | async-done | bytes 2097184 | tf_op jit(solution)/shard_map/all_to_all | solution.py:151
  220.4 3.0 %fusion.17 = bf16[1,64,2048]{2,1,0:T(8,128)(2,1)} fusion(f32[64,512]{1,0:T(8,128)S(1)} %select_reduce_fusion, bf16[512,2048]{1,0:T(8,128)(2,1)S(1)} %bitcast.128, f32[64,2048]{1,0:T(8,128)} %copy-done.2, bf16[1,64,2048]{2,1,0:T(8,128)(2,1)S(1)} %copy-done.4), kind=kOutput, calls=%fused_computation.23 | convolution fusion | flops 805830656 | bytes 3276800 | tf_op jit(solution)/shard_map/dot_general | solution.py:163
  (32 shorter events, 0.2 us)
Async XLA Ops:
  6.5 62.4 %copy-start = (bf16[8,512,128]{2,1,0:T(8,128)(2,1)S(1)}, bf16[8,512,128]{2,1,0:T(8,128)(2,1)}, u32[]{:S(2)}) copy-start(bf16[8,512,128]{2,1,0:T(8,128)(2,1)} %param.19) | copy-start | bytes 3145732
  6.5 52.9 %all-gather.3.cloned.1.call-start = ((), (), s32[]{:S(2)}) async-start(), calls=%async_computation.3 | async-start | bytes 4177920 | tf_op jit(solution)/shard_map/all_gather | solution.py:62
  8.3 143.3 %all-gather.5.cloned.1.call-start = ((), (), s32[]{:S(2)}) async-start(), calls=%async_computation.4 | async-start | bytes 9469952 | tf_op jit(solution)/shard_map/all_gather | solution.py:138
  12.2 11.8 %copy-start.10 = (s32[1,64,6]{1,0,2:T(1,128)S(1)}, s32[1,64,6]{1,0,2:T(1,128)}, u32[]{:S(2)}) copy-start(s32[1,64,6]{1,0,2:T(1,128)} %param.23) | copy-start | bytes 4612
  12.2 12.2 %copy-start.12 = (s32[1,4]{1,0:T(1,128)S(1)}, s32[1,4]{1,0:T(1,128)}, u32[]{:S(2)}) copy-start(s32[1,4]{1,0:T(1,128)} %param.17) | copy-start | bytes 52
  13.7 14.6 %copy-start.13 = (s32[1,4]{1,0:T(1,128)S(1)}, s32[1,4]{1,0:T(1,128)}, u32[]{:S(2)}) copy-start(s32[1,4]{1,0:T(1,128)} %param.18) | copy-start | bytes 52
  13.8 62.6 %all-to-all-start = ((bf16[32,512,64]{1,2,0:T(8,128)(2,1)}), bf16[32,512,64]{1,2,0:T(8,128)(2,1)S(1)}, u32[]{:S(2)}, u32[]{:S(2)}) async-start(bf16[32,512,64]{1,2,0:T(8,128)(2,1)} %broadcast_in_dim.58), calls=%async_computation | async-start | bytes 4194304 | tf_op jit(solution)/shard_map/all_to_all | solution.py:95
  24.1 4.5 %copy-start.7 = (s32[1,64,6]{2,1,0:T(8,128)}, s32[1,64,6]{2,1,0:T(8,128)S(1)}, u32[]{:S(2)}) copy-start(s32[1,64,6]{2,1,0:T(8,128)S(1)} %copy.55) | copy-start | bytes 4612
  27.9 0.7 copy-start.9
  64.6 2.7 %copy-start.1 = (f32[3,1024,64,8]{1,2,3,0:T(8,128)}, f32[3,1024,64,8]{1,2,3,0:T(8,128)S(1)}, u32[]{:S(2)}) copy-start(f32[3,1024,64,8]{1,2,3,0:T(8,128)S(1)} %get-tuple-element.12) | copy-start | bytes 18874372
  75.3 11.0 %copy-start.4 = (bf16[1,64,2048]{2,1,0:T(8,128)(2,1)S(1)}, bf16[1,64,2048]{2,1,0:T(8,128)(2,1)}, u32[]{:S(2)}) copy-start(bf16[1,64,2048]{2,1,0:T(8,128)(2,1)} %param.13) | copy-start | bytes 786436
  76.3 11.2 %copy-start.6 = (bf16[8,8,8,128]{3,2,0,1:T(8,128)(2,1)}, bf16[8,8,8,128]{3,2,0,1:T(8,128)(2,1)S(1)}, u32[]{:S(2)}) copy-start(bf16[8,8,8,128]{3,2,0,1:T(8,128)(2,1)S(1)} %copy.81) | copy-start | bytes 393220
  77.0 4.6 %collective-permute-start = (bf16[64,512]{1,0:T(8,128)(2,1)}, bf16[64,512]{1,0:T(8,128)(2,1)}, u32[]{:S(2)}, u32[]{:S(2)}) collective-permute-start(bf16[64,512]{1,0:T(8,128)(2,1)} %constant_dynamic-slice_fusion), channel_id=1, source_target_pairs={{0,32},{32,0},{64,96},{96,64},{128,160},{160,128},{192,224},{224,1... | collective-permute-start | bytes 196616 | tf_op jit(solution)/shard_map/ppermute | solution.py:106
  84.2 5.2 %collective-permute-start.1 = (f32[64,32,64]{0,2,1:T(8,128)}, f32[64,32,64]{0,2,1:T(8,128)}, u32[]{:S(2)}, u32[]{:S(2)}) collective-permute-start(f32[64,32,64]{0,2,1:T(8,128)} %fusion.33), channel_id=1, source_target_pairs={{0,32},{32,0},{64,96},{96,64},{128,160},{160,128},{192,224},{224,1... | collective-permute-start | bytes 1572872 | tf_op jit(solution)/shard_map/ppermute | solution.py:112
  87.5 1.8 copy-start.3
  89.3 2.0 copy-start.11
  91.3 60.4 %copy-start.2 = (f32[64,2048]{1,0:T(8,128)}, f32[64,2048]{1,0:T(8,128)S(1)}, u32[]{:S(2)}) copy-start(f32[64,2048]{1,0:T(8,128)S(1)} %copy.54) | copy-start | bytes 1572868
  91.4 0.7 copy-start.5
  163.2 7.8 %copy-start.8 = (s32[1,64,6]{2,1,0:T(8,128)S(1)}, s32[1,64,6]{2,1,0:T(8,128)}, u32[]{:S(2)}) copy-start(s32[1,64,6]{2,1,0:T(8,128)} %copy-done.7) | copy-start | bytes 4612
  163.2 57.2 %all-to-all-start.2 = ((bf16[32,16,2048]{2,1,0:T(8,128)(2,1)}), bf16[32,16,2048]{2,1,0:T(8,128)(2,1)S(1)}, u32[]{:S(2)}, u32[]{:S(2)}) async-start(bf16[32,16,2048]{2,1,0:T(8,128)(2,1)} %bitcast.132), calls=%async_computation.2 | async-start | bytes 4194304 | tf_op jit(solution)/shard_map/all_to_all | solution.py:151
Sparse Core Ops, SparseCore 0:
  9.5 49.8 all-gather.2
  61.6 59.6 all-gather.4

commit v8 on v7

--- a/solution.py
+++ b/solution.py
@@ -69,18 +69,20 @@
     prefix_allowed = jnp.broadcast_to(
         prefix_pick[:, :, None], (local_tokens, block_count - 1, piece_rows)
     )
-    allowed = jnp.concatenate([suffix_allowed[:, None, :], prefix_allowed], axis=1)[:, None]
+    allowed = jnp.concatenate([suffix_allowed[:, None, :], prefix_allowed], axis=1)
+    allowed = allowed.reshape(local_tokens, 1, block_count * piece_rows)
+    every_key = key_stack.reshape(block_count * piece_rows, key_width)
     scores = (
-        jnp.einsum("thk,pnk->thpn", query_rows, key_stack, preferred_element_type=jnp.float32)
+        jnp.einsum("thk,nk->thn", query_rows, every_key, preferred_element_type=jnp.float32)
         * qk_scale
     )
-    final_max = jnp.max(jnp.where(allowed, scores, big_negative), axis=(2, 3))
-    weights = jnp.where(allowed, jnp.exp(scores - final_max[:, :, None, None]), 0.0)
-    final_sum = jnp.sum(weights, axis=(2, 3))
+    final_max = jnp.max(jnp.where(allowed, scores, big_negative), axis=2)
+    weights = jnp.where(allowed, jnp.exp(scores - final_max[:, :, None]), 0.0)
+    final_sum = jnp.sum(weights, axis=2)
     final_acc = jnp.einsum(
-        "thpn,pnl->thl",
+        "thn,nl->thl",
         weights.astype(jnp.bfloat16),
-        key_stack[:, :, :latent_width],
+        every_key[:, :latent_width],
         preferred_element_type=jnp.float32,
     )
     latent_out = (final_acc / final_sum[:, :, None]).astype(jnp.bfloat16)

time: 231 us -> 229 us (level)
  other arithmetic: 9.75 us -> 12.8 us
  local copies, waits for them, and re-layouts: 14.9 us -> 12 us
    sub x0 -> x1, other arithmetic: none -> 3.96 us  [local(): weights = jnp.where(allowed, jnp.exp(scores - final_max[:, :, None]), 0.0)]
    unnamed x31 -> x30, local copies, waits for them, and re-layouts: 4.6 us -> 1.33 us
  transfers between devices with their start and end apart: 6 -> 6, of which waited for: 2 -> 2; matrix products, arithmetic and copies ran while one was open for 16% -> 17% of each run, Pallas kernels for 0% -> 0%
where the time goes in v8:
time: 229 us; the launch traced here: 228 us
  waiting for transfers between devices  77.5 us (34%)
  blocking collectives  58.8 us (26%)
  matrix products  31.1 us (14%)
  starting transfers between devices  22 us (10%)
  between operations  13.8 us (6%)
  other arithmetic  12.8 us (6%)
  local copies, waits for them, and re-layouts  12 us (5%)
    all_to_all x1, blocking collectives, local(): lax.all_to_all(outgoing, 'expert', split_axis=0, concat_axis=0, tiled=True)  58.8 us
    all_to_all x1, waiting for transfers between devices, local(): lax.all_to_all(produced.reshape(-1, capacity, model_width), 'expert', spl...  47.8 us
    all_gather x1, waiting for transfers between devices, local(): key_stack = lax.all_gather(key_stack, 'seq', axis=1, tiled=True)  29.7 us
    all_to_all x1, starting transfers between devices, local(): lax.all_to_all(jnp.broadcast_to(my_rows[None], (expert_devices,) + my_row...  10.1 us
    all_to_all x1, starting transfers between devices, local(): lax.all_to_all(produced.reshape(-1, capacity, model_width), 'expert', spl...  7.61 us
    dot_general x1, matrix products, local(): gate_up = jnp.dot(all_rows, full_in[0], preferred_element_type=jnp.float32)  6.44 us
    dot_general x1, matrix products, local(): jnp.einsum('thl,hlv->thv', latent_out, value_up, preferred_element_type=j...  5.43 us
    dot_general x1, matrix products, local(): lax.dot_general(active, full_out[0], (((1,), (1,)), ((), ())), preferred_...  5.17 us
  transfers between devices with their start and end apart: 6, of which 2 were waited for; matrix products, arithmetic and copies ran while one was open for 17% of the time, Pallas kernels for 0%

profile of v8, /device:TPU:16, one launch (start us, length us, event | category | flops | bytes accessed | tf_op | source)
XLA Modules:
  0.0 227.9 jit_solution(16014201136013462797)
XLA Ops:
  6.5 0.0 all-gather.3.cloned.1.call-start
  6.5 1.8 pad_maximum_fusion.1
  8.3 0.0 all-gather.3.cloned.1.call-update
  8.3 0.0 all-gather.5.cloned.1.call-start
  8.4 1.1 copy.68
  9.5 1.9 pad_maximum_fusion
  11.3 0.0 all-gather.5.cloned.1.call-update
  11.4 0.8 constant_dynamic-slice_fusion.1
  12.2 0.0 copy-start.12
  12.2 1.5 broadcast_in_dim.60
  13.8 10.1 %all-to-all-start = ((bf16[32,512,64]{1,2,0:T(8,128)(2,1)}), bf16[32,512,64]{1,2,0:T(8,128)(2,1)S(1)}, u32[]{:S(2)}, u32[]{:S(2)}) async-start(bf16[32,512,64]{1,2,0:T(8,128)(2,1)} %broadcast_in_dim.60), calls=%async_computation | async-start | bytes 4194304 | tf_op jit(solution)/shard_map/all_to_all | solution.py:97
  23.9 0.1 copy.60
  24.0 0.1 eq.125
  24.1 0.1 eq.121
  24.2 0.2 reduce-window.18
  24.4 0.1 convert_reduce_fusion.1
  24.5 0.1 convert_reduce_fusion.2
  24.6 0.1 fusion.36
  24.7 0.2 copy.54
  25.0 0.1 select_reduce_fusion.2
  25.1 0.1 iota_compare_fusion.6
  25.2 0.2 broadcast_in_dim.103
  25.4 0.6 pad_add_fusion
  26.0 0.1 copy.76
  26.1 2.4 %reshape_squeeze.3 = bf16[64,8,576]{2,1,0:T(8,128)(2,1)} reshape(bf16[1,64,4608]{2,1,0:T(8,128)(2,1)} %param.14) | data formatting | bytes 1179648 | tf_op jit(solution)/shard_map/reshape;squeeze | solution.py:60
  28.6 0.9 reduce-window.19
  29.4 0.2 slice_reduce_fusion
  29.7 29.7 %all-gather.3.cloned.1.call-done = bf16[3,1024,576]{2,1,0:T(8,128)(2,1)} async-done(((bf16[3,64,576]{2,1,0:T(8,128)(2,1)}), bf16[3,1024,576]{2,1,0:T(8,128)(2,1)}) %all-gather.3.cloned.1.call-update) | async-done | bytes 3538960 | tf_op jit(solution)/shard_map/all_gather | solution.py:62
  59.4 4.9 %fusion.33 = f32[3072,64,8]{0,1,2:T(8,128)S(1)} fusion(bf16[3072,576,1]{1,0,2:T(8,128)(2,1)} %bitcast.128, bf16[64,8,576]{2,1,0:T(8,128)(2,1)} %reshape_squeeze.3), kind=kOutput, calls=%fused_computation.36 | convolution fusion | flops 1811939328 | bytes 10420224 | tf_op jit(solution)/shard_map/thk,nk->thn/dot_general | solution.py:76
  64.3 4.0 %fusion.53 = (f32[64,8]{0,1:T(8,128)S(1)}, bf16[64,8,3072]{2,0,1:T(8,128)(2,1)}) fusion(f32[3072,64,8]{0,1,2:T(8,128)S(1)} %fusion.33, pred[64,3072]{1,0:T(8,128)(4,1)S(1)} %bitcast.122), kind=kOutput, calls=%fused_computation.84 | output fusion | flops 11013119 | bytes 9635840 | tf_op jit(solution)/shard_map/sub | solution.py:80
  68.3 5.4 %fusion.28 = bf16[8,8,8,128]{3,2,1,0:T(8,128)(2,1)} fusion(bf16[8,512,128]{2,1,0:T(8,128)(2,1)S(1)} %copy-done, bf16[3072,576]{1,0:T(8,128)(2,1)} %bitcast.129, bf16[64,8,3072]{2,0,1:T(8,128)(2,1)} %get-tuple-element.12, f32[64,8]{0,1:T(8,128)S(1)} %get-tuple-element.11), kind=kOutput, calls=%fused_computation.28 | convolution fusion | flops 1678311424 | bytes 7473152 | tf_op jit(solution)/shard_map/thl,hlv->thv/dot_general | solution.py:89
  73.7 1.0 copy.83
  74.7 0.0 copy-start.5
  74.7 0.0 all-to-all-done
  74.7 0.6 constant_dynamic-slice_fusion
  75.3 2.1 collective-permute-start
  77.5 0.9 fusion.44
  78.4 0.7 reshape.203
  79.1 0.8 copy.67
  80.0 0.0 collective-permute-done
  80.0 2.6 %fusion.37 = f32[64,32,64]{0,2,1:T(8,128)} fusion(bf16[32,512,64]{1,2,0:T(8,128)(2,1)S(1)} %all-to-all-done, bf16[64,512]{1,0:T(8,128)(2,1)} %collective-permute-done), kind=kOutput, calls=%fused_computation.48 | convolution fusion | flops 134217728 | bytes 2686976 | tf_op jit(solution)/shard_map/tr,jrc->tjc/dot_general | solution.py:109
  82.5 2.2 collective-permute-start.1
  84.7 1.2 copy.66
  85.9 0.0 copy-done.5
  85.9 0.1 convert_reduce_fusion
  86.1 1.7 fusion.40
  87.8 0.0 copy-start.10
  87.8 0.0 collective-permute-done.1
  87.8 1.6 multiply_reduce_fusion
  89.4 0.3 copy.59
  89.7 0.0 copy-done.10
  89.7 0.1 multiply_convert_fusion
  89.8 0.0 copy-start.4
  89.9 0.7 convolution_convert_fusion
  90.6 58.8 %all_to_all.15 = bf16[32,16,2048]{2,1,0:T(8,128)(2,1)} all-to-all(bf16[32,16,2048]{2,1,0:T(8,128)(2,1)S(1)} %bitcast.114), channel_id=1, replica_groups=mesh['seq'=16,'expert'=32] {'expert'}, dimensions={0} | all-to-all | bytes 4194304 | tf_op jit(solution)/shard_map/all_to_all | solution.py:138
  149.4 6.4 %fusion.4 = f32[512,1408]{1,0:T(8,128)S(1)} fusion(bf16[512,2048]{1,0:T(8,128)(2,1)} %bitcast.118, bf16[1,2048,2112]{2,1,0:T(8,128)(2,1)} %all-gather.5.cloned.1.call-done), kind=kOutput, calls=%fused_computation.7 | convolution fusion | flops 2952790016 | bytes 10747904 | tf_op jit(solution)/shard_map/dot_general | solution.py:145
  155.8 5.2 %fusion.12 = bf16[512,2048]{1,0:T(8,128)(2,1)} fusion(bf16[1,2048,2112]{2,1,0:T(8,128)(2,1)} %all-gather.5.cloned.1.call-done, f32[512,1408]{1,0:T(8,128)S(1)} %fusion.4), kind=kOutput, calls=%fused_computation.17 | convolution fusion | flops 1479606272 | bytes 8388608 | tf_op jit(solution)/shard_map/dot_general | solution.py:150
  161.0 7.6 %all-to-all-start.2 = ((bf16[32,16,2048]{2,1,0:T(8,128)(2,1)}), bf16[32,16,2048]{2,1,0:T(8,128)(2,1)S(1)}, u32[]{:S(2)}, u32[]{:S(2)}) async-start(bf16[32,16,2048]{2,1,0:T(8,128)(2,1)} %bitcast.117), calls=%async_computation.2 | async-start | bytes 4194304 | tf_op jit(solution)/shard_map/all_to_all | solution.py:153
  168.6 0.1 reshape.202
  168.8 0.1 copy.64
  168.9 1.2 fusion.54
  170.2 0.2 select_reduce_fusion
  170.3 47.8 %all-to-all-done.2 = bf16[32,16,2048]{2,1,0:T(8,128)(2,1)S(1)} async-done(((bf16[32,16,2048]{2,1,0:T(8,128)(2,1)}), bf16[32,16,2048]{2,1,0:T(8,128)(2,1)S(1)}, u32[]{:S(2)}, u32[]{:S(2)}) %all-to-all-start.2) | async-done | bytes 2097184 | tf_op jit(solution)/shard_map/all_to_all | solution.py:153
  218.1 3.0 %fusion.14 = bf16[1,64,2048]{2,1,0:T(8,128)(2,1)} fusion(f32[64,512]{1,0:T(8,128)S(1)} %select_reduce_fusion, bf16[512,2048]{1,0:T(8,128)(2,1)S(1)} %bitcast.113, f32[64,2048]{1,0:T(8,128)} %copy-done.1, bf16[1,64,2048]{2,1,0:T(8,128)(2,1)S(1)} %copy-done.3), kind=kOutput, calls=%fused_computation.21 | convolution fusion | flops 805830656 | bytes 3276800 | tf_op jit(solution)/shard_map/dot_general | solution.py:165
  (32 shorter events, 0.2 us)
Async XLA Ops:
  6.5 61.7 %copy-start = (bf16[8,512,128]{2,1,0:T(8,128)(2,1)S(1)}, bf16[8,512,128]{2,1,0:T(8,128)(2,1)}, u32[]{:S(2)}) copy-start(bf16[8,512,128]{2,1,0:T(8,128)(2,1)} %param.19) | copy-start | bytes 3145732
  6.5 52.8 %all-gather.3.cloned.1.call-start = ((), (), s32[]{:S(2)}) async-start(), calls=%async_computation.3 | async-start | bytes 4177920 | tf_op jit(solution)/shard_map/all_gather | solution.py:62
  8.3 141.0 %all-gather.5.cloned.1.call-start = ((), (), s32[]{:S(2)}) async-start(), calls=%async_computation.4 | async-start | bytes 9469952 | tf_op jit(solution)/shard_map/all_gather | solution.py:140
  12.2 11.6 %copy-start.9 = (s32[1,64,6]{1,0,2:T(1,128)S(1)}, s32[1,64,6]{1,0,2:T(1,128)}, u32[]{:S(2)}) copy-start(s32[1,64,6]{1,0,2:T(1,128)} %param.23) | copy-start | bytes 4612
  12.2 12.0 %copy-start.11 = (s32[1,4]{1,0:T(1,128)S(1)}, s32[1,4]{1,0:T(1,128)}, u32[]{:S(2)}) copy-start(s32[1,4]{1,0:T(1,128)} %param.17) | copy-start | bytes 52
  12.2 12.8 %copy-start.12 = (s32[1,4]{1,0:T(1,128)S(1)}, s32[1,4]{1,0:T(1,128)}, u32[]{:S(2)}) copy-start(s32[1,4]{1,0:T(1,128)} %param.18) | copy-start | bytes 52
  13.8 60.9 %all-to-all-start = ((bf16[32,512,64]{1,2,0:T(8,128)(2,1)}), bf16[32,512,64]{1,2,0:T(8,128)(2,1)S(1)}, u32[]{:S(2)}, u32[]{:S(2)}) async-start(bf16[32,512,64]{1,2,0:T(8,128)(2,1)} %broadcast_in_dim.60), calls=%async_computation | async-start | bytes 4194304 | tf_op jit(solution)/shard_map/all_to_all | solution.py:97
  24.0 40.3 %copy-start.6 = (s32[1,64,6]{2,1,0:T(8,128)}, s32[1,64,6]{2,1,0:T(8,128)S(1)}, u32[]{:S(2)}) copy-start(s32[1,64,6]{2,1,0:T(8,128)S(1)} %copy.60) | copy-start | bytes 4612
  29.4 34.9 %copy-start.8 = (s32[32,3,128]{2,0,1:T(8,128)}, s32[32,3,128]{2,0,1:T(8,128)S(1)}, u32[]{:S(2)}) copy-start(s32[32,3,128]{2,0,1:T(8,128)S(1)} %reduce-window.19) | copy-start | bytes 147460
  73.7 11.0 %copy-start.3 = (bf16[1,64,2048]{2,1,0:T(8,128)(2,1)S(1)}, bf16[1,64,2048]{2,1,0:T(8,128)(2,1)}, u32[]{:S(2)}) copy-start(bf16[1,64,2048]{2,1,0:T(8,128)(2,1)} %param.13) | copy-start | bytes 786436
  74.7 11.2 %copy-start.5 = (bf16[8,8,8,128]{3,2,0,1:T(8,128)(2,1)}, bf16[8,8,8,128]{3,2,0,1:T(8,128)(2,1)S(1)}, u32[]{:S(2)}) copy-start(bf16[8,8,8,128]{3,2,0,1:T(8,128)(2,1)S(1)} %copy.83) | copy-start | bytes 393220
  75.3 4.6 %collective-permute-start = (bf16[64,512]{1,0:T(8,128)(2,1)}, bf16[64,512]{1,0:T(8,128)(2,1)}, u32[]{:S(2)}, u32[]{:S(2)}) collective-permute-start(bf16[64,512]{1,0:T(8,128)(2,1)} %constant_dynamic-slice_fusion), channel_id=1, source_target_pairs={{0,32},{32,0},{64,96},{96,64},{128,160},{160,128},{192,224},{224,1... | collective-permute-start | bytes 196616 | tf_op jit(solution)/shard_map/ppermute | solution.py:108
  82.5 5.2 %collective-permute-start.1 = (f32[64,32,64]{0,2,1:T(8,128)}, f32[64,32,64]{0,2,1:T(8,128)}, u32[]{:S(2)}, u32[]{:S(2)}) collective-permute-start(f32[64,32,64]{0,2,1:T(8,128)} %fusion.37), channel_id=1, source_target_pairs={{0,32},{32,0},{64,96},{96,64},{128,160},{160,128},{192,224},{224,1... | collective-permute-start | bytes 1572872 | tf_op jit(solution)/shard_map/ppermute | solution.py:114
  85.9 1.9 copy-start.2
  87.8 2.0 copy-start.10
  89.7 59.7 %copy-start.1 = (f32[64,2048]{1,0:T(8,128)}, f32[64,2048]{1,0:T(8,128)S(1)}, u32[]{:S(2)}) copy-start(f32[64,2048]{1,0:T(8,128)S(1)} %copy.59) | copy-start | bytes 1572868
  89.8 59.5 %copy-start.4 = (bf16[64,2048]{1,0:T(8,128)(2,1)}, bf16[64,2048]{1,0:T(8,128)(2,1)S(1)}, u32[]{:S(2)}) copy-start(bf16[64,2048]{1,0:T(8,128)(2,1)S(1)} %multiply_convert_fusion) | copy-start | bytes 786436
  161.0 7.8 %copy-start.7 = (s32[1,64,6]{2,1,0:T(8,128)S(1)}, s32[1,64,6]{2,1,0:T(8,128)}, u32[]{:S(2)}) copy-start(s32[1,64,6]{2,1,0:T(8,128)} %copy-done.6) | copy-start | bytes 4612
  161.0 57.1 %all-to-all-start.2 = ((bf16[32,16,2048]{2,1,0:T(8,128)(2,1)}), bf16[32,16,2048]{2,1,0:T(8,128)(2,1)S(1)}, u32[]{:S(2)}, u32[]{:S(2)}) async-start(bf16[32,16,2048]{2,1,0:T(8,128)(2,1)} %bitcast.117), calls=%async_computation.2 | async-start | bytes 4194304 | tf_op jit(solution)/shard_map/all_to_all | solution.py:153
Sparse Core Ops, SparseCore 0:
  9.5 49.8 all-gather.2
  61.5 59.8 all-gather.4

commit v9 on v8

--- a/solution.py
+++ b/solution.py
@@ -77,6 +77,18 @@
         * qk_scale
     )
     final_max = jnp.max(jnp.where(allowed, scores, big_negative), axis=2)
+    expert_devices = model_width // out_proj.shape[1]
+    half_rows = out_proj.shape[0] // 2
+    core = lax.axis_index("seq") % 2
+    my_rows = lax.dynamic_slice_in_dim(out_proj, core * half_rows, half_rows, axis=0)
+    my_blocks = lax.all_to_all(
+        jnp.broadcast_to(my_rows[None], (expert_devices,) + my_rows.shape),
+        "expert",
+        split_axis=0,
+        concat_axis=0,
+        tiled=True,
+    )
+    my_blocks, final_max = lax.optimization_barrier((my_blocks, final_max))
     weights = jnp.where(allowed, jnp.exp(scores - final_max[:, :, None]), 0.0)
     final_sum = jnp.sum(weights, axis=2)
     final_acc = jnp.einsum(
@@ -90,28 +102,13 @@
         "thl,hlv->thv", latent_out, value_up, preferred_element_type=jnp.float32
     ).astype(jnp.bfloat16)
     value_out = value_out.reshape(local_tokens, head_count * value_up.shape[2])
-    expert_devices = model_width // out_proj.shape[1]
-    half_rows = out_proj.shape[0] // 2
-    core = lax.axis_index("seq") % 2
-    my_rows = lax.dynamic_slice_in_dim(out_proj, core * half_rows, half_rows, axis=0)
-    my_blocks = lax.all_to_all(
-        jnp.broadcast_to(my_rows[None], (expert_devices,) + my_rows.shape),
-        "expert",
-        split_axis=0,
-        concat_axis=0,
-        tiled=True,
-    )
-    my_blocks, value_out = lax.optimization_barrier((my_blocks, value_out))
     pair = [(i, i ^ 1) for i in range(seq_count)]
+    other_blocks = lax.ppermute(my_blocks, "seq", perm=pair)
     my_part = lax.dynamic_slice_in_dim(value_out, core * half_rows, half_rows, axis=1)
     other_part = lax.dynamic_slice_in_dim(value_out, (1 - core) * half_rows, half_rows, axis=1)
-    partner_part = lax.ppermute(other_part, "seq", perm=pair)
-    partner_partial = jnp.einsum(
-        "tr,jrc->tjc", partner_part, my_blocks, preferred_element_type=jnp.float32
-    )
     projected = (
         jnp.einsum("tr,jrc->tjc", my_part, my_blocks, preferred_element_type=jnp.float32)
-        + lax.ppermute(partner_partial, "seq", perm=pair)
+        + jnp.einsum("tr,jrc->tjc", other_part, other_blocks, preferred_element_type=jnp.float32)
     ).reshape(local_tokens, model_width)
     residual = hidden[0].astype(jnp.float32) + projected
     normed = (

time: 229 us -> 229 us (level)
  the two profiles are of different devices: /device:TPU:16 before, /device:TPU:144 now
where the time goes in v9:
time: 229 us; the launch traced here: 228 us
  waiting for transfers between devices  82.5 us (36%)
  blocking collectives  55.6 us (24%)
  matrix products  34 us (15%)
  starting transfers between devices  19.8 us (9%)
  between operations  13.7 us (6%)
  local copies, waits for them, and re-layouts  11.4 us (5%)
  other arithmetic  11 us (5%)
    all_to_all x1, blocking collectives, local(): lax.all_to_all(outgoing, 'expert', split_axis=0, concat_axis=0, tiled=True)  55.6 us
    all_to_all x1, waiting for transfers between devices, local(): lax.all_to_all(produced.reshape(-1, capacity, model_width), 'expert', spl...  48.2 us
    all_gather x1, waiting for transfers between devices, local(): key_stack = lax.all_gather(key_stack, 'seq', axis=1, tiled=True)  24.2 us
    all_to_all x1, starting transfers between devices, local(): lax.all_to_all(jnp.broadcast_to(my_rows[None], (expert_devices,) + my_row...  10.2 us
    all_to_all x1, waiting for transfers between devices, local(): lax.all_to_all(jnp.broadcast_to(my_rows[None], (expert_devices,) + my_row...  9.97 us
    dot_general x1, matrix products, local(): jnp.einsum('thk,nk->thn', query_rows, every_key, preferred_element_type=j...  7.83 us
    all_to_all x1, starting transfers between devices, local(): lax.all_to_all(produced.reshape(-1, capacity, model_width), 'expert', spl...  7.66 us
    dot_general x1, matrix products, local(): jnp.einsum('thl,hlv->thv', latent_out, value_up, preferred_element_type=j...  6.65 us
  transfers between devices with their start and end apart: 5, of which 3 were waited for; matrix products, arithmetic and copies ran while one was open for 17% of the time, Pallas kernels for 0%

profile of v9, /device:TPU:144, one launch (start us, length us, event | category | flops | bytes accessed | tf_op | source)
XLA Modules:
  0.0 228.0 jit_solution(6206033769009937720)
XLA Ops:
  6.5 0.0 copy-start
  6.5 0.0 all-gather.3.cloned.1.call-start
  6.5 1.8 pad_maximum_fusion.1
  8.3 0.0 all-gather.3.cloned.1.call-update
  8.3 0.0 all-gather.5.cloned.1.call-start
  8.4 1.1 copy.64
  9.5 1.9 pad_maximum_fusion
  11.3 0.0 all-gather.5.cloned.1.call-update
  11.4 0.8 constant_dynamic-slice_fusion
  12.2 1.6 broadcast_in_dim.105
  13.8 10.2 %all-to-all-start = ((bf16[32,512,64]{1,2,0:T(8,128)(2,1)}), bf16[32,512,64]{1,2,0:T(8,128)(2,1)S(1)}, u32[]{:S(2)}, u32[]{:S(2)}) async-start(bf16[32,512,64]{1,2,0:T(8,128)(2,1)} %broadcast_in_dim.105), calls=%async_computation | async-start | bytes 4194304 | tf_op jit(solution)/shard_map/all_to_all | solution.py:84
  24.0 0.0 copy-done.7
  24.0 0.1 copy.56
  24.1 0.1 eq.121
  24.2 0.1 eq.125
  24.4 0.0 copy-done.3
  24.4 1.2 copy.62
  25.6 0.2 reduce-window.18
  25.7 0.1 convert_reduce_fusion.1
  25.8 0.1 convert_reduce_fusion.2
  25.9 0.1 fusion.27
  26.0 0.2 copy.51
  26.3 0.1 select_reduce_fusion.2
  26.4 0.1 iota_compare_fusion.6
  26.5 0.2 broadcast_in_dim.102
  26.7 0.6 pad_add_fusion
  27.3 0.8 copy.71
  28.1 2.4 %reshape_squeeze.3 = bf16[64,8,576]{2,1,0:T(8,128)(2,1)} reshape(bf16[1,64,4608]{2,1,0:T(8,128)(2,1)} %param.14) | data formatting | bytes 1179648 | tf_op jit(solution)/shard_map/reshape;squeeze | solution.py:60
  30.5 0.9 reduce-window.19
  31.4 0.2 slice_reduce_fusion
  31.6 0.1 fusion.35
  31.7 0.1 reshape.203
  31.9 0.1 copy.63
  31.9 24.2 %all-gather.3.cloned.1.call-done = bf16[3,1024,576]{2,1,0:T(8,128)(2,1)} async-done(((bf16[3,64,576]{2,1,0:T(8,128)(2,1)}), bf16[3,1024,576]{2,1,0:T(8,128)(2,1)}) %all-gather.3.cloned.1.call-update) | async-done | bytes 3538960 | tf_op jit(solution)/shard_map/all_gather | solution.py:62
  56.2 7.8 %fusion = (f32[64,8]{0,1:T(8,128)S(1)}, f32[3072,64,8]{0,1,2:T(8,128)}) fusion(pred[64,3072]{1,0:T(8,128)(4,1)} %bitcast.121, bf16[3072,576,1]{1,0,2:T(8,128)(2,1)} %bitcast.131, bf16[64,8,576]{2,1,0:T(8,128)(2,1)} %reshape_squeeze.3), kind=kOutput, calls=%fused_computation.2 | convolution fusion | flops 1816657408 | bytes 10618880 | tf_op jit(solution)/shard_map/thk,nk->thn/dot_general | solution.py:76
  64.0 0.0 copy-done.5
  64.0 10.0 %all-to-all-done = bf16[32,512,64]{1,2,0:T(8,128)(2,1)S(1)} async-done(((bf16[32,512,64]{1,2,0:T(8,128)(2,1)}), bf16[32,512,64]{1,2,0:T(8,128)(2,1)S(1)}, u32[]{:S(2)}, u32[]{:S(2)}) %all-to-all-start) | async-done | bytes 2097184 | tf_op jit(solution)/shard_map/all_to_all | solution.py:84
  74.0 1.9 collective-permute-start
  75.9 0.1 convert_reduce_fusion
  76.1 4.5 %fusion.4 = f32[64,8]{0,1:T(8,128)S(1)} fusion(f32[3072,64,8]{0,1,2:T(8,128)} %get-tuple-element.12, f32[64,8]{0,1:T(8,128)S(1)} %get-tuple-element.7, pred[64,3072]{1,0:T(8,128)(4,1)} %bitcast.122), kind=kLoop, calls=%fused_computation.7 | loop fusion | flops 6290944 | bytes 6492160 | tf_op jit(solution)/shard_map/reduce_sum | solution.py:93
  80.6 0.0 copy-done
  80.6 6.7 %fusion.17 = bf16[8,8,8,128]{3,2,1,0:T(8,128)(2,1)} fusion(bf16[8,512,128]{2,1,0:T(8,128)(2,1)S(1)} %copy-done, bf16[3072,576]{1,0:T(8,128)(2,1)} %bitcast.132, f32[3072,64,8]{0,1,2:T(8,128)} %get-tuple-element.12, f32[64,8]{0,1:T(8,128)S(1)} %get-tuple-element.7, pred[64,3072]{1,0:T(8,128)(4,1)} %bitcast.123, f32[64,8]{0,1:T(8,128)S(1)} %fusion.4), kind=kOutput, calls=%fused_computation.25 | convolution fusion | flops 1684602880 | bytes 10817536 | tf_op jit(solution)/shard_map/thl,hlv->thv/dot_general | solution.py:101
  87.3 1.0 copy.80
  88.3 0.7 fusion.31
  89.0 0.0 collective-permute-done
  89.0 0.0 copy-done.2
  89.0 0.0 copy-start.8
  89.0 2.4 %multiply_reduce_fusion = (f32[64]{0:T(128)S(1)}, f32[64,32,64]{0,2,1:T(8,128)S(1)}) fusion(f32[64,32,64]{0,2,1:T(8,128)S(1)} %bitcast.116, f32[64,2048]{0,1:S(1)} %fusion.31, bf16[512,2048]{0,1:T(8,128)(2,1)} %bitcast.13, bf16[64,1024]{1,0:T(8,128)(2,1)S(1)} %bitcast.125, s32[]{:T(128)S(6)} %select_n.38), kind=kOutput, calls=%fused_computation.26 | convolution fusion | flops 134741952 | bytes 4784388
  91.4 0.3 copy.55
  91.8 0.0 copy-done.8
  91.8 0.1 multiply_convert_fusion
  91.9 0.0 copy-start.4
  91.9 0.7 copy-done.4
  92.6 0.7 convolution_convert_fusion
  93.4 55.6 %all_to_all.15 = bf16[32,16,2048]{2,1,0:T(8,128)(2,1)} all-to-all(bf16[32,16,2048]{2,1,0:T(8,128)(2,1)S(1)} %bitcast.115), channel_id=1, replica_groups=mesh['seq'=16,'expert'=32] {'expert'}, dimensions={0} | all-to-all | bytes 4194304 | tf_op jit(solution)/shard_map/all_to_all | solution.py:135
  149.0 6.4 %fusion.3 = f32[512,1408]{1,0:T(8,128)S(1)} fusion(bf16[512,2048]{1,0:T(8,128)(2,1)} %bitcast.119, bf16[1,2048,2112]{2,1,0:T(8,128)(2,1)} %all-gather.5.cloned.1.call-done), kind=kOutput, calls=%fused_computation.6 | convolution fusion | flops 2952790016 | bytes 10747904 | tf_op jit(solution)/shard_map/dot_general | solution.py:142
  155.4 5.2 %fusion.13 = bf16[512,2048]{1,0:T(8,128)(2,1)} fusion(bf16[1,2048,2112]{2,1,0:T(8,128)(2,1)} %all-gather.5.cloned.1.call-done, f32[512,1408]{1,0:T(8,128)S(1)} %fusion.3), kind=kOutput, calls=%fused_computation.17 | convolution fusion | flops 1479606272 | bytes 8388608 | tf_op jit(solution)/shard_map/dot_general | solution.py:147
  160.6 7.7 %all-to-all-start.2 = ((bf16[32,16,2048]{2,1,0:T(8,128)(2,1)}), bf16[32,16,2048]{2,1,0:T(8,128)(2,1)S(1)}, u32[]{:S(2)}, u32[]{:S(2)}) async-start(bf16[32,16,2048]{2,1,0:T(8,128)(2,1)} %bitcast.118), calls=%async_computation.2 | async-start | bytes 4194304 | tf_op jit(solution)/shard_map/all_to_all | solution.py:150
  168.3 0.1 reshape.202
  168.4 0.1 copy.60
  168.5 1.2 fusion.47
  169.8 0.2 select_reduce_fusion
  170.0 48.2 %all-to-all-done.2 = bf16[32,16,2048]{2,1,0:T(8,128)(2,1)S(1)} async-done(((bf16[32,16,2048]{2,1,0:T(8,128)(2,1)}), bf16[32,16,2048]{2,1,0:T(8,128)(2,1)S(1)}, u32[]{:S(2)}, u32[]{:S(2)}) %all-to-all-start.2) | async-done | bytes 2097184 | tf_op jit(solution)/shard_map/all_to_all | solution.py:150
  218.2 3.0 %fusion.15 = bf16[1,64,2048]{2,1,0:T(8,128)(2,1)} fusion(f32[64,512]{1,0:T(8,128)S(1)} %select_reduce_fusion, bf16[512,2048]{1,0:T(8,128)(2,1)S(1)} %bitcast.114, f32[64,2048]{1,0:T(8,128)} %copy-done.1, bf16[1,64,2048]{2,1,0:T(8,128)(2,1)S(1)} %copy-done.3), kind=kOutput, calls=%fused_computation.21 | convolution fusion | flops 805830656 | bytes 3276800 | tf_op jit(solution)/shard_map/dot_general | solution.py:162
  (24 shorter events, 0.2 us)
Async XLA Ops:
  6.5 74.1 %copy-start = (bf16[8,512,128]{2,1,0:T(8,128)(2,1)S(1)}, bf16[8,512,128]{2,1,0:T(8,128)(2,1)}, u32[]{:S(2)}) copy-start(bf16[8,512,128]{2,1,0:T(8,128)(2,1)} %param.19) | copy-start | bytes 3145732
  6.5 49.7 %all-gather.3.cloned.1.call-start = ((), (), s32[]{:S(2)}) async-start(), calls=%async_computation.3 | async-start | bytes 4177920 | tf_op jit(solution)/shard_map/all_gather | solution.py:62
  8.3 140.6 %all-gather.5.cloned.1.call-start = ((), (), s32[]{:S(2)}) async-start(), calls=%async_computation.4 | async-start | bytes 9469952 | tf_op jit(solution)/shard_map/all_gather | solution.py:137
  12.2 11.8 %copy-start.7 = (s32[1,64,6]{1,0,2:T(1,128)S(1)}, s32[1,64,6]{1,0,2:T(1,128)}, u32[]{:S(2)}) copy-start(s32[1,64,6]{1,0,2:T(1,128)} %param.23) | copy-start | bytes 4612
  12.2 12.2 %copy-start.3 = (bf16[1,64,2048]{2,1,0:T(8,128)(2,1)S(1)}, bf16[1,64,2048]{2,1,0:T(8,128)(2,1)}, u32[]{:S(2)}) copy-start(bf16[1,64,2048]{2,1,0:T(8,128)(2,1)} %param.13) | copy-start | bytes 786436
  13.8 11.8 %copy-start.9 = (s32[1,4]{1,0:T(1,128)S(1)}, s32[1,4]{1,0:T(1,128)}, u32[]{:S(2)}) copy-start(s32[1,4]{1,0:T(1,128)} %param.17) | copy-start | bytes 52
  13.8 12.5 %copy-start.10 = (s32[1,4]{1,0:T(1,128)S(1)}, s32[1,4]{1,0:T(1,128)}, u32[]{:S(2)}) copy-start(s32[1,4]{1,0:T(1,128)} %param.18) | copy-start | bytes 52
  13.8 60.2 %all-to-all-start = ((bf16[32,512,64]{1,2,0:T(8,128)(2,1)}), bf16[32,512,64]{1,2,0:T(8,128)(2,1)S(1)}, u32[]{:S(2)}, u32[]{:S(2)}) async-start(bf16[32,512,64]{1,2,0:T(8,128)(2,1)} %broadcast_in_dim.105), calls=%async_computation | async-start | bytes 4194304 | tf_op jit(solution)/shard_map/all_to_all | solution.py:84
  24.1 39.9 %copy-start.5 = (s32[1,64,6]{2,1,0:T(8,128)}, s32[1,64,6]{2,1,0:T(8,128)S(1)}, u32[]{:S(2)}) copy-start(s32[1,64,6]{2,1,0:T(8,128)S(1)} %copy.56) | copy-start | bytes 4612
  74.0 15.0 %collective-permute-start = (bf16[32,512,64]{1,2,0:T(8,128)(2,1)S(1)}, bf16[32,512,64]{1,2,0:T(8,128)(2,1)}, u32[]{:S(2)}, u32[]{:S(2)}) collective-permute-start(bf16[32,512,64]{1,2,0:T(8,128)(2,1)S(1)} %all-to-all-done), channel_id=1, source_target_pairs={{0,32},{32,0},{64,96},{96,64},{128,160},{160,128},{192,224},{224,1... | collective-permute-start | bytes 6291464 | tf_op jit(solution)/shard_map/ppermute | solution.py:106
  87.3 1.7 copy-start.2
  89.0 2.8 %copy-start.8 = (f32[2048]{0:T(1024)S(1)}, f32[2048]{0:T(1024)}, u32[]{:S(2)}) copy-start(f32[2048]{0:T(1024)} %param.21) | copy-start | bytes 24580
  91.8 57.2 %copy-start.1 = (f32[64,2048]{1,0:T(8,128)}, f32[64,2048]{1,0:T(8,128)S(1)}, u32[]{:S(2)}) copy-start(f32[64,2048]{1,0:T(8,128)S(1)} %copy.55) | copy-start | bytes 1572868
  91.9 0.7 copy-start.4
  160.6 7.8 %copy-start.6 = (s32[1,64,6]{2,1,0:T(8,128)S(1)}, s32[1,64,6]{2,1,0:T(8,128)}, u32[]{:S(2)}) copy-start(s32[1,64,6]{2,1,0:T(8,128)} %copy-done.5) | copy-start | bytes 4612
  160.6 57.6 %all-to-all-start.2 = ((bf16[32,16,2048]{2,1,0:T(8,128)(2,1)}), bf16[32,16,2048]{2,1,0:T(8,128)(2,1)S(1)}, u32[]{:S(2)}, u32[]{:S(2)}) async-start(bf16[32,16,2048]{2,1,0:T(8,128)(2,1)} %bitcast.118), calls=%async_computation.2 | async-start | bytes 4194304 | tf_op jit(solution)/shard_map/all_to_all | solution.py:150
Sparse Core Ops, SparseCore 0:
  9.5 46.6 all-gather.2
  58.3 59.2 all-gather.4

commit v10 on v8

--- a/solution.py
+++ b/solution.py
@@ -3,6 +3,7 @@
 import jax
 import jax.numpy as jnp
 from jax import lax
+from jax.experimental import pallas as pl
 from jax.sharding import PartitionSpec as P
 
 qk_scale = 192.0 ** (-0.5)
@@ -22,6 +23,48 @@
         "thn,nl->thl", weights.astype(jnp.bfloat16), values, preferred_element_type=jnp.float32
     )
     return (new_max, new_sum, new_acc)
+
+
+def attention_kernel(q_ref, k_ref, m_ref, o_ref, *, heads, latent_width):
+    keys = k_ref[...]
+    scores = (
+        lax.dot_general(
+            q_ref[...], keys, (((1,), (1,)), ((), ())), preferred_element_type=jnp.float32
+        )
+        * qk_scale
+    )
+    rows, count = scores.shape
+    scores = scores.reshape(rows // heads, heads, count)
+    allowed = m_ref[...][:, None, :] > 0.5
+    top = jnp.max(jnp.where(allowed, scores, big_negative), axis=2, keepdims=True)
+    weights = jnp.where(allowed, jnp.exp(scores - top), 0.0)
+    total = jnp.sum(weights, axis=2, keepdims=True)
+    acc = jnp.dot(
+        weights.reshape(rows, count).astype(jnp.bfloat16),
+        keys[:, :latent_width],
+        preferred_element_type=jnp.float32,
+    )
+    o_ref[...] = (
+        (acc.reshape(rows // heads, heads, latent_width) / total)
+        .reshape(rows, latent_width)
+        .astype(o_ref.dtype)
+    )
+
+
+def attend(query_rows, every_key, allowed, heads, latent_width):
+    rows, key_width = query_rows.shape
+    count = every_key.shape[0]
+    flops = 2 * rows * count * (key_width + latent_width)
+    return pl.pallas_call(
+        functools.partial(attention_kernel, heads=heads, latent_width=latent_width),
+        out_shape=jax.ShapeDtypeStruct((rows, latent_width), jnp.bfloat16),
+        cost_estimate=pl.CostEstimate(
+            flops=flops,
+            transcendentals=rows * count,
+            bytes_accessed=2 * (rows * key_width + count * key_width + rows * latent_width)
+            + 4 * allowed.size,
+        ),
+    )(query_rows, every_key, allowed)
 
 
 def local(
@@ -70,22 +113,15 @@
         prefix_pick[:, :, None], (local_tokens, block_count - 1, piece_rows)
     )
     allowed = jnp.concatenate([suffix_allowed[:, None, :], prefix_allowed], axis=1)
-    allowed = allowed.reshape(local_tokens, 1, block_count * piece_rows)
+    allowed = allowed.reshape(local_tokens, block_count * piece_rows).astype(jnp.float32)
     every_key = key_stack.reshape(block_count * piece_rows, key_width)
-    scores = (
-        jnp.einsum("thk,nk->thn", query_rows, every_key, preferred_element_type=jnp.float32)
-        * qk_scale
-    )
-    final_max = jnp.max(jnp.where(allowed, scores, big_negative), axis=2)
-    weights = jnp.where(allowed, jnp.exp(scores - final_max[:, :, None]), 0.0)
-    final_sum = jnp.sum(weights, axis=2)
-    final_acc = jnp.einsum(
-        "thn,nl->thl",
-        weights.astype(jnp.bfloat16),
-        every_key[:, :latent_width],
-        preferred_element_type=jnp.float32,
-    )
-    latent_out = (final_acc / final_sum[:, :, None]).astype(jnp.bfloat16)
+    latent_out = attend(
+        query_rows.reshape(local_tokens * head_count, key_width),
+        every_key,
+        allowed,
+        head_count,
+        latent_width,
+    ).reshape(local_tokens, head_count, latent_width)
     value_out = jnp.einsum(
         "thl,hlv->thv", latent_out, value_up, preferred_element_type=jnp.float32
     ).astype(jnp.bfloat16)

time: 229 us -> 226 us (0.987)
  Pallas kernels: 0 us -> 10.1 us
  matrix products: 31.1 us -> 22.2 us
  other arithmetic: 12.8 us -> 8.79 us
    pallas_call x0 -> x1, Pallas kernels: none -> 10.1 us  [attend(): pl.pallas_call(functools.partial(attention_kernel, heads=heads, latent_wi...]
    dot_general x1 -> x0, matrix products: 4.91 us -> none  [local(): jnp.einsum('thk,nk->thn', query_rows, every_key, preferred_element_type=j...]
    dot_general x1, matrix products: 5.43 us -> 1.42 us  [local(): jnp.einsum('thl,hlv->thv', latent_out, value_up, preferred_element_type=j...]
    sub x1 -> x0, other arithmetic: 3.96 us -> none  [local(): weights = jnp.where(allowed, jnp.exp(scores - final_max[:, :, None]), 0.0)]
  transfers between devices with their start and end apart: 6 -> 6, of which waited for: 2 -> 3; matrix products, arithmetic and copies ran while one was open for 17% -> 12% of each run, Pallas kernels for 0% -> 4%
where the time goes in v10:
time: 226 us; the launch traced here: 225 us
  waiting for transfers between devices  79.5 us (35%)
  blocking collectives  56.6 us (25%)
  starting transfers between devices  22.3 us (10%)
  matrix products  22.2 us (10%)
  between operations  13.7 us (6%)
  local copies, waits for them, and re-layouts  11.4 us (5%)
  Pallas kernels  10.1 us (4%)
  other arithmetic  8.79 us (4%)
    all_to_all x1, blocking collectives, local(): lax.all_to_all(outgoing, 'expert', split_axis=0, concat_axis=0, tiled=True)  56.6 us
    all_to_all x1, waiting for transfers between devices, local(): lax.all_to_all(produced.reshape(-1, capacity, model_width), 'expert', spl...  48 us
    all_gather x1, waiting for transfers between devices, local(): key_stack = lax.all_gather(key_stack, 'seq', axis=1, tiled=True)  29.2 us
    all_to_all x1, starting transfers between devices, local(): lax.all_to_all(jnp.broadcast_to(my_rows[None], (expert_devices,) + my_row...  10.2 us
    pallas_call x1, Pallas kernels, attend(): pl.pallas_call(functools.partial(attention_kernel, heads=heads, latent_wi...  10.1 us
    all_to_all x1, starting transfers between devices, local(): lax.all_to_all(produced.reshape(-1, capacity, model_width), 'expert', spl...  7.63 us
    dot_general x1, matrix products, local(): gate_up = jnp.dot(all_rows, full_in[0], preferred_element_type=jnp.float32)  6.44 us
    dot_general x1, matrix products, local(): lax.dot_general(active, full_out[0], (((1,), (1,)), ((), ())), preferred_...  5.17 us
  transfers between devices with their start and end apart: 6, of which 3 were waited for; matrix products, arithmetic and copies ran while one was open for 12% of the time, Pallas kernels for 4%

profile of v10, /device:TPU:16, one launch (start us, length us, event | category | flops | bytes accessed | tf_op | source)
XLA Modules:
  0.0 224.6 jit_solution(11149266321706969062)
XLA Ops:
  6.5 0.0 copy-start
  6.5 0.0 all-gather.3.cloned.1.call-start
  6.5 1.8 pad_maximum_fusion.1
  8.3 0.0 all-gather.3.cloned.1.call-update
  8.4 0.0 all-gather.5.cloned.1.call-start
  8.4 1.1 copy.64
  9.5 1.9 pad_maximum_fusion
  11.3 0.0 all-gather.5.cloned.1.call-update
  11.4 1.6 broadcast_in_dim.36
  13.0 10.2 %all-to-all-start = ((bf16[32,512,64]{1,2,0:T(8,128)(2,1)}), bf16[32,512,64]{1,2,0:T(8,128)(2,1)S(1)}, u32[]{:S(2)}, u32[]{:S(2)}) async-start(bf16[32,512,64]{1,2,0:T(8,128)(2,1)} %broadcast_in_dim.36), calls=%async_computation | async-start | bytes 4194304 | tf_op jit(solution)/shard_map/all_to_all | solution.py:133
  23.2 0.1 copy.56
  23.3 0.1 eq.121
  23.4 0.1 eq.125
  23.6 2.4 %reshape_reshape_squeeze.3.q_ref = bf16[512,576]{1,0:T(8,128)(2,1)} reshape(bf16[1,64,4608]{2,1,0:T(8,128)(2,1)} %param.14) | data formatting | bytes 1179648 | tf_op jit(solution)/shard_map/reshape;reshape;squeeze | solution.py:119
  25.9 0.0 copy-done.12
  25.9 0.2 reduce-window.18
  26.1 0.1 convert_reduce_fusion.1
  26.2 0.1 convert_reduce_fusion.2
  26.3 0.1 fusion.10
  26.4 0.2 copy.51
  26.7 0.1 select_reduce_fusion.2
  26.8 0.1 iota_compare_fusion.6
  26.9 0.2 broadcast_in_dim.44
  27.1 0.6 add_convert_fusion
  27.7 1.4 copy.70
  29.0 0.9 reduce-window.19
  29.9 0.2 slice_reduce_fusion
  30.2 29.2 %all-gather.3.cloned.1.call-done = bf16[3,1024,576]{2,1,0:T(8,128)(2,1)} async-done(((bf16[3,64,576]{2,1,0:T(8,128)(2,1)}), bf16[3,1024,576]{2,1,0:T(8,128)(2,1)}) %all-gather.3.cloned.1.call-update) | async-done | bytes 3538960 | tf_op jit(solution)/shard_map/all_gather | solution.py:105
  59.4 10.1 %shard_map.127 = bf16[512,512]{1,0:T(8,128)(2,1)} custom-call(bf16[512,576]{1,0:T(8,128)(2,1)} %reshape_reshape_squeeze.3.q_ref, bf16[3072,576]{1,0:T(8,128)(2,1)} %bitcast.99, f32[64,3072]{1,0:T(8,128)} %bitcast.90), custom_call_target="tpu_custom_call" | custom-call | flops 3422552064 | bytes 5439488 | tf_op jit(solution)/shard_map/pallas_call | solution.py:58
  69.5 0.0 copy-done
  69.5 1.4 fusion.6
  70.9 0.0 copy-start.3
  70.9 0.0 copy-start.5
  70.9 2.3 %all-to-all-done = bf16[32,512,64]{1,2,0:T(8,128)(2,1)S(1)} async-done(((bf16[32,512,64]{1,2,0:T(8,128)(2,1)}), bf16[32,512,64]{1,2,0:T(8,128)(2,1)S(1)}, u32[]{:S(2)}, u32[]{:S(2)}) %all-to-all-start) | async-done | bytes 2097184 | tf_op jit(solution)/shard_map/all_to_all | solution.py:133
  73.2 0.6 constant_dynamic-slice_fusion
  73.8 1.9 collective-permute-start
  75.8 0.9 fusion.18
  76.6 0.8 reshape.206
  77.4 0.8 copy.63
  78.2 0.0 collective-permute-done
  78.2 2.6 %fusion.11 = f32[64,32,64]{0,2,1:T(8,128)} fusion(bf16[32,512,64]{1,2,0:T(8,128)(2,1)S(1)} %all-to-all-done, bf16[64,512]{1,0:T(8,128)(2,1)} %collective-permute-done), kind=kOutput, calls=%fused_computation.30 | convolution fusion | flops 134217728 | bytes 2686976 | tf_op jit(solution)/shard_map/tr,jrc->tjc/dot_general | solution.py:145
  80.8 2.6 %collective-permute-start.1 = (f32[64,32,64]{0,2,1:T(8,128)}, f32[64,32,64]{0,2,1:T(8,128)}, u32[]{:S(2)}, u32[]{:S(2)}) collective-permute-start(f32[64,32,64]{0,2,1:T(8,128)} %fusion.11), channel_id=1, source_target_pairs={{0,32},{32,0},{64,96},{96,64},{128,160},{160,128},{192,224},{224,1... | collective-permute-start | bytes 1572872 | tf_op jit(solution)/shard_map/ppermute | solution.py:150
  83.4 0.0 copy-done.3
  83.4 1.2 copy.62
  84.6 0.0 copy-done.5
  84.6 0.1 convert_reduce_fusion
  84.7 1.7 fusion.14
  86.4 0.0 collective-permute-done.1
  86.4 0.0 copy-start.11
  86.5 1.6 multiply_reduce_fusion
  88.0 0.3 copy.55
  88.4 0.1 multiply_convert_fusion
  88.5 0.0 copy-start.4
  88.5 0.7 convolution_convert_fusion
  89.3 56.6 %all_to_all.15 = bf16[32,16,2048]{2,1,0:T(8,128)(2,1)} all-to-all(bf16[32,16,2048]{2,1,0:T(8,128)(2,1)S(1)} %bitcast.84), channel_id=1, replica_groups=mesh['seq'=16,'expert'=32] {'expert'}, dimensions={0} | all-to-all | bytes 4194304 | tf_op jit(solution)/shard_map/all_to_all | solution.py:174
  145.8 6.4 %fusion = f32[512,1408]{1,0:T(8,128)S(1)} fusion(bf16[512,2048]{1,0:T(8,128)(2,1)} %bitcast.89, bf16[1,2048,2112]{2,1,0:T(8,128)(2,1)} %all-gather.5.cloned.1.call-done), kind=kOutput, calls=%fused_computation.1 | convolution fusion | flops 2952790016 | bytes 10747904 | tf_op jit(solution)/shard_map/dot_general | solution.py:181
  152.3 5.2 %fusion.2 = bf16[512,2048]{1,0:T(8,128)(2,1)} fusion(bf16[1,2048,2112]{2,1,0:T(8,128)(2,1)} %all-gather.5.cloned.1.call-done, f32[512,1408]{1,0:T(8,128)S(1)} %fusion), kind=kOutput, calls=%fused_computation.4 | convolution fusion | flops 1479606272 | bytes 8388608 | tf_op jit(solution)/shard_map/dot_general | solution.py:186
  157.4 7.6 %all-to-all-start.2 = ((bf16[32,16,2048]{2,1,0:T(8,128)(2,1)}), bf16[32,16,2048]{2,1,0:T(8,128)(2,1)S(1)}, u32[]{:S(2)}, u32[]{:S(2)}) async-start(bf16[32,16,2048]{2,1,0:T(8,128)(2,1)} %bitcast.88), calls=%async_computation.2 | async-start | bytes 4194304 | tf_op jit(solution)/shard_map/all_to_all | solution.py:189
  165.1 0.1 reshape.205
  165.3 0.1 copy.60
  165.3 1.2 fusion.25
  166.6 0.2 select_reduce_fusion
  166.8 48.0 %all-to-all-done.2 = bf16[32,16,2048]{2,1,0:T(8,128)(2,1)S(1)} async-done(((bf16[32,16,2048]{2,1,0:T(8,128)(2,1)}), bf16[32,16,2048]{2,1,0:T(8,128)(2,1)S(1)}, u32[]{:S(2)}, u32[]{:S(2)}) %all-to-all-start.2) | async-done | bytes 2097184 | tf_op jit(solution)/shard_map/all_to_all | solution.py:189
  214.8 3.0 %fusion.4 = bf16[1,64,2048]{2,1,0:T(8,128)(2,1)} fusion(f32[64,512]{1,0:T(8,128)S(1)} %select_reduce_fusion, bf16[512,2048]{1,0:T(8,128)(2,1)S(1)} %bitcast.83, f32[64,2048]{1,0:T(8,128)} %copy-done.1, bf16[1,64,2048]{2,1,0:T(8,128)(2,1)S(1)} %copy-done.3), kind=kOutput, calls=%fused_computation.8 | convolution fusion | flops 805830656 | bytes 3276800 | tf_op jit(solution)/shard_map/dot_general | solution.py:201
  (33 shorter events, 0.2 us)
Async XLA Ops:
  6.5 62.9 %copy-start = (bf16[8,512,128]{2,1,0:T(8,128)(2,1)S(1)}, bf16[8,512,128]{2,1,0:T(8,128)(2,1)}, u32[]{:S(2)}) copy-start(bf16[8,512,128]{2,1,0:T(8,128)(2,1)} %param.19) | copy-start | bytes 3145732
  6.5 4.8 %copy-start.9 = (bf16[1024,64]{0,1:T(8,128)(2,1)S(1)}, bf16[1024,64]{0,1:T(8,128)(2,1)}, u32[]{:S(2)}) copy-start(bf16[1024,64]{0,1:T(8,128)(2,1)} %param.20) | copy-start | bytes 393220
  6.5 52.8 %all-gather.3.cloned.1.call-start = ((), (), s32[]{:S(2)}) async-start(), calls=%async_computation.3 | async-start | bytes 4177920 | tf_op jit(solution)/shard_map/all_gather | solution.py:105
  8.4 137.5 %all-gather.5.cloned.1.call-start = ((), (), s32[]{:S(2)}) async-start(), calls=%async_computation.4 | async-start | bytes 9469952 | tf_op jit(solution)/shard_map/all_gather | solution.py:176
  13.0 10.2 %copy-start.10 = (s32[1,64,6]{1,0,2:T(1,128)S(1)}, s32[1,64,6]{1,0,2:T(1,128)}, u32[]{:S(2)}) copy-start(s32[1,64,6]{1,0,2:T(1,128)} %param.23) | copy-start | bytes 4612
  13.0 13.0 %copy-start.12 = (s32[1,4]{1,0:T(1,128)S(1)}, s32[1,4]{1,0:T(1,128)}, u32[]{:S(2)}) copy-start(s32[1,4]{1,0:T(1,128)} %param.17) | copy-start | bytes 52
  13.0 13.7 %copy-start.13 = (s32[1,4]{1,0:T(1,128)S(1)}, s32[1,4]{1,0:T(1,128)}, u32[]{:S(2)}) copy-start(s32[1,4]{1,0:T(1,128)} %param.18) | copy-start | bytes 52
  13.0 60.2 %all-to-all-start = ((bf16[32,512,64]{1,2,0:T(8,128)(2,1)}), bf16[32,512,64]{1,2,0:T(8,128)(2,1)S(1)}, u32[]{:S(2)}, u32[]{:S(2)}) async-start(bf16[32,512,64]{1,2,0:T(8,128)(2,1)} %broadcast_in_dim.36), calls=%async_computation | async-start | bytes 4194304 | tf_op jit(solution)/shard_map/all_to_all | solution.py:133
  23.3 5.7 %copy-start.6 = (s32[1,64,6]{2,1,0:T(8,128)}, s32[1,64,6]{2,1,0:T(8,128)S(1)}, u32[]{:S(2)}) copy-start(s32[1,64,6]{2,1,0:T(8,128)S(1)} %copy.56) | copy-start | bytes 4612
  29.9 39.5 %copy-start.8 = (s32[32,3,128]{2,0,1:T(8,128)}, s32[32,3,128]{2,0,1:T(8,128)S(1)}, u32[]{:S(2)}) copy-start(s32[32,3,128]{2,0,1:T(8,128)S(1)} %reduce-window.19) | copy-start | bytes 147460
  70.9 12.5 %copy-start.3 = (bf16[1,64,2048]{2,1,0:T(8,128)(2,1)S(1)}, bf16[1,64,2048]{2,1,0:T(8,128)(2,1)}, u32[]{:S(2)}) copy-start(bf16[1,64,2048]{2,1,0:T(8,128)(2,1)} %param.13) | copy-start | bytes 786436
  70.9 13.7 %copy-start.5 = (bf16[8,8,8,128]{3,2,0,1:T(8,128)(2,1)}, bf16[8,8,8,128]{3,2,0,1:T(8,128)(2,1)S(1)}, u32[]{:S(2)}) copy-start(bf16[8,8,8,128]{3,2,0,1:T(8,128)(2,1)S(1)} %copy.77) | copy-start | bytes 393220
  73.8 4.4 %collective-permute-start = (bf16[64,512]{1,0:T(8,128)(2,1)}, bf16[64,512]{1,0:T(8,128)(2,1)}, u32[]{:S(2)}, u32[]{:S(2)}) collective-permute-start(bf16[64,512]{1,0:T(8,128)(2,1)} %constant_dynamic-slice_fusion), channel_id=1, source_target_pairs={{0,32},{32,0},{64,96},{96,64},{128,160},{160,128},{192,224},{224,1... | collective-permute-start | bytes 196616 | tf_op jit(solution)/shard_map/ppermute | solution.py:144
  80.8 5.6 %collective-permute-start.1 = (f32[64,32,64]{0,2,1:T(8,128)}, f32[64,32,64]{0,2,1:T(8,128)}, u32[]{:S(2)}, u32[]{:S(2)}) collective-permute-start(f32[64,32,64]{0,2,1:T(8,128)} %fusion.11), channel_id=1, source_target_pairs={{0,32},{32,0},{64,96},{96,64},{128,160},{160,128},{192,224},{224,1... | collective-permute-start | bytes 1572872 | tf_op jit(solution)/shard_map/ppermute | solution.py:150
  84.6 1.8 copy-start.2
  86.4 1.9 copy-start.11
  88.4 57.5 %copy-start.1 = (f32[64,2048]{1,0:T(8,128)}, f32[64,2048]{1,0:T(8,128)S(1)}, u32[]{:S(2)}) copy-start(f32[64,2048]{1,0:T(8,128)S(1)} %copy.55) | copy-start | bytes 1572868
  88.5 57.3 %copy-start.4 = (bf16[64,2048]{1,0:T(8,128)(2,1)}, bf16[64,2048]{1,0:T(8,128)(2,1)S(1)}, u32[]{:S(2)}) copy-start(bf16[64,2048]{1,0:T(8,128)(2,1)S(1)} %multiply_convert_fusion) | copy-start | bytes 786436
  157.4 7.8 %copy-start.7 = (s32[1,64,6]{2,1,0:T(8,128)S(1)}, s32[1,64,6]{2,1,0:T(8,128)}, u32[]{:S(2)}) copy-start(s32[1,64,6]{2,1,0:T(8,128)} %copy-done.6) | copy-start | bytes 4612
  157.4 57.4 %all-to-all-start.2 = ((bf16[32,16,2048]{2,1,0:T(8,128)(2,1)}), bf16[32,16,2048]{2,1,0:T(8,128)(2,1)S(1)}, u32[]{:S(2)}, u32[]{:S(2)}) async-start(bf16[32,16,2048]{2,1,0:T(8,128)(2,1)} %bitcast.88), calls=%async_computation.2 | async-start | bytes 4194304 | tf_op jit(solution)/shard_map/all_to_all | solution.py:189
Sparse Core Ops, SparseCore 0:
  9.5 49.8 all-gather.2
  61.5 59.8 all-gather.4

commit v11 on v10

--- a/solution.py
+++ b/solution.py
@@ -65,6 +65,31 @@
             + 4 * allowed.size,
         ),
     )(query_rows, every_key, allowed)
+
+
+def expert_kernel(x_ref, w_ref, o_ref, *, in_width):
+    weights = w_ref[...]
+    gate_up = jnp.dot(x_ref[...], weights[:, :in_width], preferred_element_type=jnp.float32)
+    hidden_units = in_width // 2
+    gate = gate_up[:, :hidden_units]
+    active = (gate / (1.0 + jnp.exp(-gate)) * gate_up[:, hidden_units:]).astype(jnp.bfloat16)
+    o_ref[...] = lax.dot_general(
+        active, weights[:, in_width:], (((1,), (1,)), ((), ())), preferred_element_type=jnp.float32
+    ).astype(o_ref.dtype)
+
+
+def expert_ffn(rows, both, in_width):
+    count, model_width = rows.shape
+    hidden_units = in_width // 2
+    return pl.pallas_call(
+        functools.partial(expert_kernel, in_width=in_width),
+        out_shape=jax.ShapeDtypeStruct((count, both.shape[0]), jnp.bfloat16),
+        cost_estimate=pl.CostEstimate(
+            flops=2 * count * model_width * (in_width + hidden_units),
+            transcendentals=count * hidden_units,
+            bytes_accessed=2 * (2 * count * model_width + both.size),
+        ),
+    )(rows, both)
 
 
 def local(
@@ -176,16 +201,8 @@
     full_both = lax.all_gather(
         jnp.concatenate([expert_in, expert_out], axis=2), "seq", axis=1, tiled=True
     )
-    full_in, full_out = full_both[:, :, :in_width], full_both[:, :, in_width:]
     all_rows = incoming.reshape(-1, model_width)
-    gate_up = jnp.dot(all_rows, full_in[0], preferred_element_type=jnp.float32)
-    hidden_units = gate_up.shape[1] // 2
-    active = (jax.nn.silu(gate_up[:, :hidden_units]) * gate_up[:, hidden_units:]).astype(
-        jnp.bfloat16
-    )
-    produced = lax.dot_general(
-        active, full_out[0], (((1,), (1,)), ((), ())), preferred_element_type=jnp.float32
-    ).astype(jnp.bfloat16)
+    produced = expert_ffn(all_rows, full_both[0], in_width)
     returned = lax.all_to_all(
         produced.reshape(-1, capacity, model_width),
         "expert",

time: 226 us -> 224 us (level)
  matrix products: 22.2 us -> 10.5 us
  Pallas kernels: 10.1 us -> 20.7 us
    dot_general x2 -> x0, matrix products: 11.6 us -> none  [the longest x1 6.44 us: local(): gate_up = jnp.dot(all_rows, full_in[0], preferred_element_type=jnp.float32)]
    pallas_call x0 -> x1, Pallas kernels: none -> 10.6 us  [expert_ffn(): pl.pallas_call(functools.partial(expert_kernel, in_width=in_width), out_s...]
  transfers between devices with their start and end apart: 6 -> 6, of which waited for: 3 -> 3; matrix products, arithmetic and copies ran while one was open for 12% -> 12% of each run, Pallas kernels for 4% -> 5%
where the time goes in v11:
time: 224 us
  waiting for transfers between devices  79.5 us (35%)
  blocking collectives  56.6 us (25%)
  starting transfers between devices  22.3 us (10%)
  Pallas kernels  20.7 us (9%)
  between operations  13.7 us (6%)
  local copies, waits for them, and re-layouts  11.4 us (5%)
  matrix products  10.5 us (5%)
  other arithmetic  8.79 us (4%)
    all_to_all x1, blocking collectives, local(): lax.all_to_all(outgoing, 'expert', split_axis=0, concat_axis=0, tiled=True)  56.6 us
    all_to_all x1, waiting for transfers between devices, local(): lax.all_to_all(produced.reshape(-1, capacity, model_width), 'expert', spl...  48 us
    all_gather x1, waiting for transfers between devices, local(): key_stack = lax.all_gather(key_stack, 'seq', axis=1, tiled=True)  29.2 us
    pallas_call x1, Pallas kernels, expert_ffn(): pl.pallas_call(functools.partial(expert_kernel, in_width=in_width), out_s...  10.6 us
    all_to_all x1, starting transfers between devices, local(): lax.all_to_all(jnp.broadcast_to(my_rows[None], (expert_devices,) + my_row...  10.2 us
    pallas_call x1, Pallas kernels, attend(): pl.pallas_call(functools.partial(attention_kernel, heads=heads, latent_wi...  10.1 us
    all_to_all x1, starting transfers between devices, local(): lax.all_to_all(produced.reshape(-1, capacity, model_width), 'expert', spl...  7.63 us
  transfers between devices with their start and end apart: 6, of which 3 were waited for; matrix products, arithmetic and copies ran while one was open for 12% of the time, Pallas kernels for 5%

profile of v11, /device:TPU:16, one launch (start us, length us, event | category | flops | bytes accessed | tf_op | source)
XLA Modules:
  0.0 223.6 jit_solution(12802970558681892831)
XLA Ops:
  6.5 0.0 copy-start
  6.5 0.0 all-gather.3.cloned.1.call-start
  6.5 1.8 pad_maximum_fusion.1
  8.3 0.0 all-gather.3.cloned.1.call-update
  8.4 0.0 all-gather.5.cloned.1.call-start
  8.4 1.1 copy.64
  9.5 1.9 pad_maximum_fusion
  11.3 0.0 all-gather.5.cloned.1.call-update
  11.4 0.0 copy-done.9
  11.4 1.6 broadcast_in_dim.36
  13.0 10.2 %all-to-all-start = ((bf16[32,512,64]{1,2,0:T(8,128)(2,1)}), bf16[32,512,64]{1,2,0:T(8,128)(2,1)S(1)}, u32[]{:S(2)}, u32[]{:S(2)}) async-start(bf16[32,512,64]{1,2,0:T(8,128)(2,1)} %broadcast_in_dim.36), calls=%async_computation | async-start | bytes 4194304 | tf_op jit(solution)/shard_map/all_to_all | solution.py:158
  23.2 0.1 copy.56
  23.3 0.1 eq.121
  23.4 0.1 eq.125
  23.6 2.4 %reshape_reshape_squeeze.3.q_ref = bf16[512,576]{1,0:T(8,128)(2,1)} reshape(bf16[1,64,4608]{2,1,0:T(8,128)(2,1)} %param.14) | data formatting | bytes 1179648 | tf_op jit(solution)/shard_map/reshape;reshape;squeeze | solution.py:144
  25.9 0.2 reduce-window.18
  26.1 0.1 convert_reduce_fusion.1
  26.2 0.1 convert_reduce_fusion.2
  26.3 0.1 fusion.4
  26.4 0.2 copy.51
  26.7 0.1 select_reduce_fusion.2
  26.8 0.1 iota_compare_fusion.6
  26.9 0.2 broadcast_in_dim.44
  27.1 0.6 add_convert_fusion
  27.7 1.4 copy.70
  29.0 0.9 reduce-window.19
  29.9 0.2 slice_reduce_fusion
  30.2 29.2 %all-gather.3.cloned.1.call-done = bf16[3,1024,576]{2,1,0:T(8,128)(2,1)} async-done(((bf16[3,64,576]{2,1,0:T(8,128)(2,1)}), bf16[3,1024,576]{2,1,0:T(8,128)(2,1)}) %all-gather.3.cloned.1.call-update) | async-done | bytes 3538960 | tf_op jit(solution)/shard_map/all_gather | solution.py:130
  59.4 10.1 %shard_map.127 = bf16[512,512]{1,0:T(8,128)(2,1)} custom-call(bf16[512,576]{1,0:T(8,128)(2,1)} %reshape_reshape_squeeze.3.q_ref, bf16[3072,576]{1,0:T(8,128)(2,1)} %bitcast.92, f32[64,3072]{1,0:T(8,128)} %bitcast.82), custom_call_target="tpu_custom_call" | custom-call | flops 3422552064 | bytes 5439488 | tf_op jit(solution)/shard_map/pallas_call | solution.py:58
  69.5 0.0 copy-done.8
  69.5 1.4 fusion.2
  70.9 0.0 copy-start.3
  70.9 0.0 copy-start.5
  70.9 2.3 %all-to-all-done = bf16[32,512,64]{1,2,0:T(8,128)(2,1)S(1)} async-done(((bf16[32,512,64]{1,2,0:T(8,128)(2,1)}), bf16[32,512,64]{1,2,0:T(8,128)(2,1)S(1)}, u32[]{:S(2)}, u32[]{:S(2)}) %all-to-all-start) | async-done | bytes 2097184 | tf_op jit(solution)/shard_map/all_to_all | solution.py:158
  73.2 0.6 constant_dynamic-slice_fusion
  73.8 1.9 collective-permute-start
  75.8 0.9 fusion.12
  76.6 0.8 reshape.206
  77.4 0.8 copy.63
  78.2 0.0 collective-permute-done
  78.2 2.6 %fusion.5 = f32[64,32,64]{0,2,1:T(8,128)} fusion(bf16[32,512,64]{1,2,0:T(8,128)(2,1)S(1)} %all-to-all-done, bf16[64,512]{1,0:T(8,128)(2,1)} %collective-permute-done), kind=kOutput, calls=%fused_computation.22 | convolution fusion | flops 134217728 | bytes 2686976 | tf_op jit(solution)/shard_map/tr,jrc->tjc/dot_general | solution.py:170
  80.8 2.6 %collective-permute-start.1 = (f32[64,32,64]{0,2,1:T(8,128)}, f32[64,32,64]{0,2,1:T(8,128)}, u32[]{:S(2)}, u32[]{:S(2)}) collective-permute-start(f32[64,32,64]{0,2,1:T(8,128)} %fusion.5), channel_id=1, source_target_pairs={{0,32},{32,0},{64,96},{96,64},{128,160},{160,128},{192,224},{224,1... | collective-permute-start | bytes 1572872 | tf_op jit(solution)/shard_map/ppermute | solution.py:175
  83.4 1.2 copy.62
  84.6 0.1 convert_reduce_fusion
  84.7 1.7 fusion.8
  86.4 0.0 collective-permute-done.1
  86.4 0.0 copy-done.2
  86.4 0.0 copy-start.11
  86.5 1.6 multiply_reduce_fusion
  88.0 0.3 copy.55
  88.4 0.0 copy-done.11
  88.4 0.1 multiply_convert_fusion
  88.5 0.0 copy-start.4
  88.5 0.7 convolution_convert_fusion
  89.3 56.6 %all_to_all.15 = bf16[32,16,2048]{2,1,0:T(8,128)(2,1)} all-to-all(bf16[32,16,2048]{2,1,0:T(8,128)(2,1)S(1)} %bitcast.76), channel_id=1, replica_groups=mesh['seq'=16,'expert'=32] {'expert'}, dimensions={0} | all-to-all | bytes 4194304 | tf_op jit(solution)/shard_map/all_to_all | solution.py:199
  145.8 0.0 copy-done.4
  145.8 10.6 %shard_map.128 = bf16[512,2048]{1,0:T(8,128)(2,1)} custom-call(bf16[512,2048]{1,0:T(8,128)(2,1)} %bitcast.81, bf16[2048,2112]{1,0:T(8,128)(2,1)} %bitcast.91), custom_call_target="tpu_custom_call" | custom-call | flops 4429185024 | bytes 12845056 | tf_op jit(solution)/shard_map/pallas_call | solution.py:84
  156.4 7.6 %all-to-all-start.2 = ((bf16[32,16,2048]{2,1,0:T(8,128)(2,1)}), bf16[32,16,2048]{2,1,0:T(8,128)(2,1)S(1)}, u32[]{:S(2)}, u32[]{:S(2)}) async-start(bf16[32,16,2048]{2,1,0:T(8,128)(2,1)} %bitcast.80), calls=%async_computation.2 | async-start | bytes 4194304 | tf_op jit(solution)/shard_map/all_to_all | solution.py:206
  164.1 0.1 reshape.205
  164.3 0.1 copy.60
  164.3 1.2 fusion.18
  165.6 0.2 select_reduce_fusion
  165.8 48.0 %all-to-all-done.2 = bf16[32,16,2048]{2,1,0:T(8,128)(2,1)S(1)} async-done(((bf16[32,16,2048]{2,1,0:T(8,128)(2,1)}), bf16[32,16,2048]{2,1,0:T(8,128)(2,1)S(1)}, u32[]{:S(2)}, u32[]{:S(2)}) %all-to-all-start.2) | async-done | bytes 2097184 | tf_op jit(solution)/shard_map/all_to_all | solution.py:206
  213.8 3.0 %fusion.1 = bf16[1,64,2048]{2,1,0:T(8,128)(2,1)} fusion(f32[64,512]{1,0:T(8,128)S(1)} %select_reduce_fusion, bf16[512,2048]{1,0:T(8,128)(2,1)S(1)} %bitcast.75, f32[64,2048]{1,0:T(8,128)} %copy-done.1, bf16[1,64,2048]{2,1,0:T(8,128)(2,1)S(1)} %copy-done.3), kind=kOutput, calls=%fused_computation.3 | convolution fusion | flops 805830656 | bytes 3276800 | tf_op jit(solution)/shard_map/dot_general | solution.py:218
  (32 shorter events, 0.2 us)
Async XLA Ops:
  6.5 62.9 %copy-start = (bf16[8,512,128]{2,1,0:T(8,128)(2,1)S(1)}, bf16[8,512,128]{2,1,0:T(8,128)(2,1)}, u32[]{:S(2)}) copy-start(bf16[8,512,128]{2,1,0:T(8,128)(2,1)} %param.19) | copy-start | bytes 3145732
  6.5 4.8 %copy-start.9 = (bf16[1024,64]{0,1:T(8,128)(2,1)S(1)}, bf16[1024,64]{0,1:T(8,128)(2,1)}, u32[]{:S(2)}) copy-start(bf16[1024,64]{0,1:T(8,128)(2,1)} %param.20) | copy-start | bytes 393220
  6.5 52.8 %all-gather.3.cloned.1.call-start = ((), (), s32[]{:S(2)}) async-start(), calls=%async_computation.3 | async-start | bytes 4177920 | tf_op jit(solution)/shard_map/all_gather | solution.py:130
  8.4 137.5 %all-gather.5.cloned.1.call-start = ((), (), s32[]{:S(2)}) async-start(), calls=%async_computation.4 | async-start | bytes 9469952 | tf_op jit(solution)/shard_map/all_gather | solution.py:201
  13.0 10.2 %copy-start.10 = (s32[1,64,6]{1,0,2:T(1,128)S(1)}, s32[1,64,6]{1,0,2:T(1,128)}, u32[]{:S(2)}) copy-start(s32[1,64,6]{1,0,2:T(1,128)} %param.23) | copy-start | bytes 4612
  13.0 13.0 %copy-start.12 = (s32[1,4]{1,0:T(1,128)S(1)}, s32[1,4]{1,0:T(1,128)}, u32[]{:S(2)}) copy-start(s32[1,4]{1,0:T(1,128)} %param.17) | copy-start | bytes 52
  13.0 13.7 %copy-start.13 = (s32[1,4]{1,0:T(1,128)S(1)}, s32[1,4]{1,0:T(1,128)}, u32[]{:S(2)}) copy-start(s32[1,4]{1,0:T(1,128)} %param.18) | copy-start | bytes 52
  13.0 60.2 %all-to-all-start = ((bf16[32,512,64]{1,2,0:T(8,128)(2,1)}), bf16[32,512,64]{1,2,0:T(8,128)(2,1)S(1)}, u32[]{:S(2)}, u32[]{:S(2)}) async-start(bf16[32,512,64]{1,2,0:T(8,128)(2,1)} %broadcast_in_dim.36), calls=%async_computation | async-start | bytes 4194304 | tf_op jit(solution)/shard_map/all_to_all | solution.py:158
  23.3 5.7 %copy-start.6 = (s32[1,64,6]{2,1,0:T(8,128)}, s32[1,64,6]{2,1,0:T(8,128)S(1)}, u32[]{:S(2)}) copy-start(s32[1,64,6]{2,1,0:T(8,128)S(1)} %copy.56) | copy-start | bytes 4612
  29.9 39.5 %copy-start.8 = (s32[32,3,128]{2,0,1:T(8,128)}, s32[32,3,128]{2,0,1:T(8,128)S(1)}, u32[]{:S(2)}) copy-start(s32[32,3,128]{2,0,1:T(8,128)S(1)} %reduce-window.19) | copy-start | bytes 147460
  70.9 12.5 %copy-start.3 = (bf16[1,64,2048]{2,1,0:T(8,128)(2,1)S(1)}, bf16[1,64,2048]{2,1,0:T(8,128)(2,1)}, u32[]{:S(2)}) copy-start(bf16[1,64,2048]{2,1,0:T(8,128)(2,1)} %param.13) | copy-start | bytes 786436
  70.9 13.7 %copy-start.5 = (bf16[8,8,8,128]{3,2,0,1:T(8,128)(2,1)}, bf16[8,8,8,128]{3,2,0,1:T(8,128)(2,1)S(1)}, u32[]{:S(2)}) copy-start(bf16[8,8,8,128]{3,2,0,1:T(8,128)(2,1)S(1)} %copy.77) | copy-start | bytes 393220
  73.8 4.4 %collective-permute-start = (bf16[64,512]{1,0:T(8,128)(2,1)}, bf16[64,512]{1,0:T(8,128)(2,1)}, u32[]{:S(2)}, u32[]{:S(2)}) collective-permute-start(bf16[64,512]{1,0:T(8,128)(2,1)} %constant_dynamic-slice_fusion), channel_id=1, source_target_pairs={{0,32},{32,0},{64,96},{96,64},{128,160},{160,128},{192,224},{224,1... | collective-permute-start | bytes 196616 | tf_op jit(solution)/shard_map/ppermute | solution.py:169
  80.8 5.6 %collective-permute-start.1 = (f32[64,32,64]{0,2,1:T(8,128)}, f32[64,32,64]{0,2,1:T(8,128)}, u32[]{:S(2)}, u32[]{:S(2)}) collective-permute-start(f32[64,32,64]{0,2,1:T(8,128)} %fusion.5), channel_id=1, source_target_pairs={{0,32},{32,0},{64,96},{96,64},{128,160},{160,128},{192,224},{224,1... | collective-permute-start | bytes 1572872 | tf_op jit(solution)/shard_map/ppermute | solution.py:175
  84.6 1.8 copy-start.2
  86.4 1.9 copy-start.11
  88.4 57.5 %copy-start.1 = (f32[64,2048]{1,0:T(8,128)}, f32[64,2048]{1,0:T(8,128)S(1)}, u32[]{:S(2)}) copy-start(f32[64,2048]{1,0:T(8,128)S(1)} %copy.55) | copy-start | bytes 1572868
  88.5 57.3 %copy-start.4 = (bf16[64,2048]{1,0:T(8,128)(2,1)}, bf16[64,2048]{1,0:T(8,128)(2,1)S(1)}, u32[]{:S(2)}) copy-start(bf16[64,2048]{1,0:T(8,128)(2,1)S(1)} %multiply_convert_fusion) | copy-start | bytes 786436
  156.4 7.8 %copy-start.7 = (s32[1,64,6]{2,1,0:T(8,128)S(1)}, s32[1,64,6]{2,1,0:T(8,128)}, u32[]{:S(2)}) copy-start(s32[1,64,6]{2,1,0:T(8,128)} %copy-done.6) | copy-start | bytes 4612
  156.4 57.4 %all-to-all-start.2 = ((bf16[32,16,2048]{2,1,0:T(8,128)(2,1)}), bf16[32,16,2048]{2,1,0:T(8,128)(2,1)S(1)}, u32[]{:S(2)}, u32[]{:S(2)}) async-start(bf16[32,16,2048]{2,1,0:T(8,128)(2,1)} %bitcast.80), calls=%async_computation.2 | async-start | bytes 4194304 | tf_op jit(solution)/shard_map/all_to_all | solution.py:206
Sparse Core Ops, SparseCore 0:
  9.5 49.8 all-gather.2
  61.5 59.8 all-gather.4

commit v12 on v11

--- a/solution.py
+++ b/solution.py
@@ -140,6 +140,18 @@
     allowed = jnp.concatenate([suffix_allowed[:, None, :], prefix_allowed], axis=1)
     allowed = allowed.reshape(local_tokens, block_count * piece_rows).astype(jnp.float32)
     every_key = key_stack.reshape(block_count * piece_rows, key_width)
+    expert_devices = model_width // out_proj.shape[1]
+    half_rows = out_proj.shape[0] // 2
+    core = lax.axis_index("seq") % 2
+    my_rows = lax.dynamic_slice_in_dim(out_proj, core * half_rows, half_rows, axis=0)
+    my_blocks = lax.all_to_all(
+        jnp.broadcast_to(my_rows[None], (expert_devices,) + my_rows.shape),
+        "expert",
+        split_axis=0,
+        concat_axis=0,
+        tiled=True,
+    )
+    my_blocks, every_key = lax.optimization_barrier((my_blocks, every_key))
     latent_out = attend(
         query_rows.reshape(local_tokens * head_count, key_width),
         every_key,
@@ -151,28 +163,13 @@
         "thl,hlv->thv", latent_out, value_up, preferred_element_type=jnp.float32
     ).astype(jnp.bfloat16)
     value_out = value_out.reshape(local_tokens, head_count * value_up.shape[2])
-    expert_devices = model_width // out_proj.shape[1]
-    half_rows = out_proj.shape[0] // 2
-    core = lax.axis_index("seq") % 2
-    my_rows = lax.dynamic_slice_in_dim(out_proj, core * half_rows, half_rows, axis=0)
-    my_blocks = lax.all_to_all(
-        jnp.broadcast_to(my_rows[None], (expert_devices,) + my_rows.shape),
-        "expert",
-        split_axis=0,
-        concat_axis=0,
-        tiled=True,
-    )
-    my_blocks, value_out = lax.optimization_barrier((my_blocks, value_out))
     pair = [(i, i ^ 1) for i in range(seq_count)]
+    other_blocks = lax.ppermute(my_blocks, "seq", perm=pair)
     my_part = lax.dynamic_slice_in_dim(value_out, core * half_rows, half_rows, axis=1)
     other_part = lax.dynamic_slice_in_dim(value_out, (1 - core) * half_rows, half_rows, axis=1)
-    partner_part = lax.ppermute(other_part, "seq", perm=pair)
-    partner_partial = jnp.einsum(
-        "tr,jrc->tjc", partner_part, my_blocks, preferred_element_type=jnp.float32
-    )
     projected = (
         jnp.einsum("tr,jrc->tjc", my_part, my_blocks, preferred_element_type=jnp.float32)
-        + lax.ppermute(partner_partial, "seq", perm=pair)
+        + jnp.einsum("tr,jrc->tjc", other_part, other_blocks, preferred_element_type=jnp.float32)
     ).reshape(local_tokens, model_width)
     residual = hidden[0].astype(jnp.float32) + projected
     normed = (

time: 224 us -> 235 us (1.049)
  the two profiles are of different devices: /device:TPU:16 before, /device:TPU:400 now
where the time goes in v12:
time: 235 us; the launch traced here: 234 us
  waiting for transfers between devices  98 us (42%)
  blocking collectives  55.5 us (24%)
  Pallas kernels  20.8 us (9%)
  starting transfers between devices  19.8 us (8%)
  between operations  13.7 us (6%)
  local copies, waits for them, and re-layouts  10.7 us (5%)
  matrix products  9.49 us (4%)
  other arithmetic  6.4 us (3%)
    all_to_all x1, blocking collectives, local(): lax.all_to_all(outgoing, 'expert', split_axis=0, concat_axis=0, tiled=True)  55.5 us
    all_to_all x1, waiting for transfers between devices, local(): lax.all_to_all(jnp.broadcast_to(my_rows[None], (expert_devices,) + my_row...  49.7 us
    all_to_all x1, waiting for transfers between devices, local(): lax.all_to_all(produced.reshape(-1, capacity, model_width), 'expert', spl...  48.3 us
    pallas_call x1, Pallas kernels, expert_ffn(): pl.pallas_call(functools.partial(expert_kernel, in_width=in_width), out_s...  10.6 us
    pallas_call x1, Pallas kernels, attend(): pl.pallas_call(functools.partial(attention_kernel, heads=heads, latent_wi...  10.2 us
    all_to_all x1, starting transfers between devices, local(): lax.all_to_all(jnp.broadcast_to(my_rows[None], (expert_devices,) + my_row...  10.2 us
    all_to_all x1, starting transfers between devices, local(): lax.all_to_all(produced.reshape(-1, capacity, model_width), 'expert', spl...  7.69 us
  transfers between devices with their start and end apart: 5, of which 2 were waited for; matrix products, arithmetic and copies ran while one was open for 9% of the time, Pallas kernels for 4%

profile of v12, /device:TPU:400, one launch (start us, length us, event | category | flops | bytes accessed | tf_op | source)
XLA Modules:
  0.0 234.4 jit_solution(13899114952107531687)
XLA Ops:
  6.5 0.0 copy-start
  6.5 0.0 all-gather.3.cloned.1.call-start
  6.5 1.8 pad_maximum_fusion.1
  8.3 0.0 all-gather.3.cloned.1.call-update
  8.4 0.0 all-gather.5.cloned.1.call-start
  8.4 1.1 copy.60
  9.5 1.8 pad_maximum_fusion
  11.3 0.0 all-gather.5.cloned.1.call-update
  11.3 0.0 copy-done.7
  11.4 1.6 broadcast_in_dim.36
  13.0 10.2 %all-to-all-start = ((bf16[32,512,64]{1,2,0:T(8,128)(2,1)}), bf16[32,512,64]{1,2,0:T(8,128)(2,1)S(1)}, u32[]{:S(2)}, u32[]{:S(2)}) async-start(bf16[32,512,64]{1,2,0:T(8,128)(2,1)} %broadcast_in_dim.36), calls=%async_computation | async-start | bytes 4194304 | tf_op jit(solution)/shard_map/all_to_all | solution.py:147
  23.2 0.0 copy-start.11
  23.2 0.0 copy-done.10
  23.2 0.2 reduce-window.18
  23.4 0.1 convert_reduce_fusion.1
  23.4 0.1 convert_reduce_fusion.2
  23.5 49.7 %all-to-all-done = bf16[32,512,64]{1,2,0:T(8,128)(2,1)S(1)} async-done(((bf16[32,512,64]{1,2,0:T(8,128)(2,1)}), bf16[32,512,64]{1,2,0:T(8,128)(2,1)S(1)}, u32[]{:S(2)}, u32[]{:S(2)}) %all-to-all-start) | async-done | bytes 2097184 | tf_op jit(solution)/shard_map/all_to_all | solution.py:147
  73.2 1.9 collective-permute-start
  75.1 0.1 fusion.4
  75.2 0.0 copy-done.8
  75.3 0.1 copy.52
  75.4 0.1 eq.121
  75.5 0.1 eq.125
  75.6 0.0 copy-done.3
  75.6 1.2 copy.58
  76.8 2.4 %reshape_reshape_squeeze.3.q_ref = bf16[512,576]{1,0:T(8,128)(2,1)} reshape(bf16[1,64,4608]{2,1,0:T(8,128)(2,1)} %param.14) | data formatting | bytes 1179648 | tf_op jit(solution)/shard_map/reshape;reshape;squeeze | solution.py:156
  79.2 0.2 copy.48
  79.5 0.0 copy-done.11
  79.5 0.1 select_reduce_fusion.2
  79.6 0.1 iota_compare_fusion.6
  79.6 0.2 broadcast_in_dim.44
  79.8 0.6 add_convert_fusion
  80.5 0.0 copy-done.5
  80.5 1.4 copy.65
  81.8 0.9 reduce-window.19
  82.7 0.2 slice_reduce_fusion
  83.0 0.1 fusion.12
  83.1 0.1 reshape.206
  83.2 0.1 copy.59
  83.3 0.1 convert_reduce_fusion
  83.5 10.2 %shard_map.127 = bf16[512,512]{1,0:T(8,128)(2,1)} custom-call(bf16[512,576]{1,0:T(8,128)(2,1)} %reshape_reshape_squeeze.3.q_ref, bf16[3072,576]{1,0:T(8,128)(2,1)} %bitcast.96, f32[64,3072]{1,0:T(8,128)} %bitcast.86), custom_call_target="tpu_custom_call" | custom-call | flops 3422552064 | bytes 5439488 | tf_op jit(solution)/shard_map/pallas_call | solution.py:58
  93.7 0.0 copy-done
  93.7 1.5 fusion.2
  95.2 0.7 fusion.8
  95.9 0.0 collective-permute-done
  95.9 0.5 copy-done.2
  96.4 2.4 %multiply_reduce_fusion = (f32[64]{0:T(128)S(1)}, f32[64,32,64]{0,2,1:T(8,128)S(1)}) fusion(f32[64,32,64]{0,2,1:T(8,128)S(1)} %bitcast.82, f32[64,2048]{0,1:S(1)} %fusion.8, bf16[512,2048]{0,1:T(8,128)(2,1)} %bitcast.11, bf16[64,1024]{1,0:T(8,128)(2,1)S(1)} %bitcast.88, s32[]{:T(128)S(6)} %select_n.29), kind=kOutput, calls=%fused_computation.6 | convolution fusion | flops 134741952 | bytes 4784388
  98.9 0.3 copy.51
  99.2 0.0 copy-start.1
  99.2 0.0 copy-done.9
  99.2 0.1 multiply_convert_fusion
  99.4 0.0 copy-start.4
  99.4 0.7 copy-done.4
  100.1 0.7 convolution_convert_fusion
  100.8 55.5 %all_to_all.15 = bf16[32,16,2048]{2,1,0:T(8,128)(2,1)} all-to-all(bf16[32,16,2048]{2,1,0:T(8,128)(2,1)S(1)} %bitcast.80), channel_id=1, replica_groups=mesh['seq'=16,'expert'=32] {'expert'}, dimensions={0} | all-to-all | bytes 4194304 | tf_op jit(solution)/shard_map/all_to_all | solution.py:196
  156.3 0.0 copy-done.1
  156.3 10.6 %shard_map.128 = bf16[512,2048]{1,0:T(8,128)(2,1)} custom-call(bf16[512,2048]{1,0:T(8,128)(2,1)} %bitcast.85, bf16[2048,2112]{1,0:T(8,128)(2,1)} %bitcast.95), custom_call_target="tpu_custom_call" | custom-call | flops 4429185024 | bytes 12845056 | tf_op jit(solution)/shard_map/pallas_call | solution.py:84
  166.9 7.7 %all-to-all-start.2 = ((bf16[32,16,2048]{2,1,0:T(8,128)(2,1)}), bf16[32,16,2048]{2,1,0:T(8,128)(2,1)S(1)}, u32[]{:S(2)}, u32[]{:S(2)}) async-start(bf16[32,16,2048]{2,1,0:T(8,128)(2,1)} %bitcast.84), calls=%async_computation.2 | async-start | bytes 4194304 | tf_op jit(solution)/shard_map/all_to_all | solution.py:203
  174.6 0.1 reshape.205
  174.8 0.1 copy.56
  174.9 1.2 fusion.19
  176.2 0.2 select_reduce_fusion
  176.3 48.3 %all-to-all-done.2 = bf16[32,16,2048]{2,1,0:T(8,128)(2,1)S(1)} async-done(((bf16[32,16,2048]{2,1,0:T(8,128)(2,1)}), bf16[32,16,2048]{2,1,0:T(8,128)(2,1)S(1)}, u32[]{:S(2)}, u32[]{:S(2)}) %all-to-all-start.2) | async-done | bytes 2097184 | tf_op jit(solution)/shard_map/all_to_all | solution.py:203
  224.6 3.0 %fusion.1 = bf16[1,64,2048]{2,1,0:T(8,128)(2,1)} fusion(f32[64,512]{1,0:T(8,128)S(1)} %select_reduce_fusion, bf16[512,2048]{1,0:T(8,128)(2,1)S(1)} %bitcast.79, f32[64,2048]{1,0:T(8,128)} %copy-done.1, bf16[1,64,2048]{2,1,0:T(8,128)(2,1)S(1)} %copy-done.3), kind=kOutput, calls=%fused_computation.3 | convolution fusion | flops 805830656 | bytes 3276800 | tf_op jit(solution)/shard_map/dot_general | solution.py:215
  (24 shorter events, 0.2 us)
Async XLA Ops:
  6.5 87.1 %copy-start = (bf16[8,512,128]{2,1,0:T(8,128)(2,1)S(1)}, bf16[8,512,128]{2,1,0:T(8,128)(2,1)}, u32[]{:S(2)}) copy-start(bf16[8,512,128]{2,1,0:T(8,128)(2,1)} %param.19) | copy-start | bytes 3145732
  6.5 4.8 %copy-start.7 = (bf16[1024,64]{0,1:T(8,128)(2,1)S(1)}, bf16[1024,64]{0,1:T(8,128)(2,1)}, u32[]{:S(2)}) copy-start(bf16[1024,64]{0,1:T(8,128)(2,1)} %param.20) | copy-start | bytes 393220
  6.5 66.6 %all-gather.3.cloned.1.call-start = ((), (), s32[]{:S(2)}) async-start(), calls=%async_computation.3 | async-start | bytes 4177920 | tf_op jit(solution)/shard_map/all_gather | solution.py:130
  8.4 147.9 %all-gather.5.cloned.1.call-start = ((), (), s32[]{:S(2)}) async-start(), calls=%async_computation.4 | async-start | bytes 9469952 | tf_op jit(solution)/shard_map/all_gather | solution.py:198
  13.0 10.2 %copy-start.10 = (s32[1,4]{1,0:T(1,128)S(1)}, s32[1,4]{1,0:T(1,128)}, u32[]{:S(2)}) copy-start(s32[1,4]{1,0:T(1,128)} %param.17) | copy-start | bytes 52
  13.0 62.3 %copy-start.8 = (s32[1,64,6]{1,0,2:T(1,128)S(1)}, s32[1,64,6]{1,0,2:T(1,128)}, u32[]{:S(2)}) copy-start(s32[1,64,6]{1,0,2:T(1,128)} %param.23) | copy-start | bytes 4612
  13.0 62.7 %copy-start.3 = (bf16[1,64,2048]{2,1,0:T(8,128)(2,1)S(1)}, bf16[1,64,2048]{2,1,0:T(8,128)(2,1)}, u32[]{:S(2)}) copy-start(bf16[1,64,2048]{2,1,0:T(8,128)(2,1)} %param.13) | copy-start | bytes 786436
  13.0 60.2 %all-to-all-start = ((bf16[32,512,64]{1,2,0:T(8,128)(2,1)}), bf16[32,512,64]{1,2,0:T(8,128)(2,1)S(1)}, u32[]{:S(2)}, u32[]{:S(2)}) async-start(bf16[32,512,64]{1,2,0:T(8,128)(2,1)} %broadcast_in_dim.36), calls=%async_computation | async-start | bytes 4194304 | tf_op jit(solution)/shard_map/all_to_all | solution.py:147
  23.2 56.3 %copy-start.11 = (s32[1,4]{1,0:T(1,128)S(1)}, s32[1,4]{1,0:T(1,128)}, u32[]{:S(2)}) copy-start(s32[1,4]{1,0:T(1,128)} %param.18) | copy-start | bytes 52
  73.2 22.7 %collective-permute-start = (bf16[32,512,64]{1,2,0:T(8,128)(2,1)S(1)}, bf16[32,512,64]{1,2,0:T(8,128)(2,1)}, u32[]{:S(2)}, u32[]{:S(2)}) collective-permute-start(bf16[32,512,64]{1,2,0:T(8,128)(2,1)S(1)} %all-to-all-done), channel_id=1, source_target_pairs={{0,32},{32,0},{64,96},{96,64},{128,160},{160,128},{192,224},{224,1... | collective-permute-start | bytes 6291464 | tf_op jit(solution)/shard_map/ppermute | solution.py:167
  75.4 5.1 %copy-start.5 = (s32[1,64,6]{2,1,0:T(8,128)}, s32[1,64,6]{2,1,0:T(8,128)S(1)}, u32[]{:S(2)}) copy-start(s32[1,64,6]{2,1,0:T(8,128)S(1)} %copy.52) | copy-start | bytes 4612
  95.1 1.3 copy-start.2
  96.4 2.8 %copy-start.9 = (f32[2048]{0:T(1024)S(1)}, f32[2048]{0:T(1024)}, u32[]{:S(2)}) copy-start(f32[2048]{0:T(1024)} %param.21) | copy-start | bytes 24580
  99.2 57.1 %copy-start.1 = (f32[64,2048]{1,0:T(8,128)}, f32[64,2048]{1,0:T(8,128)S(1)}, u32[]{:S(2)}) copy-start(f32[64,2048]{1,0:T(8,128)S(1)} %copy.51) | copy-start | bytes 1572868
  99.4 0.7 copy-start.4
  166.9 7.8 %copy-start.6 = (s32[1,64,6]{2,1,0:T(8,128)S(1)}, s32[1,64,6]{2,1,0:T(8,128)}, u32[]{:S(2)}) copy-start(s32[1,64,6]{2,1,0:T(8,128)} %copy-done.5) | copy-start | bytes 4612
  166.9 57.7 %all-to-all-start.2 = ((bf16[32,16,2048]{2,1,0:T(8,128)(2,1)}), bf16[32,16,2048]{2,1,0:T(8,128)(2,1)S(1)}, u32[]{:S(2)}, u32[]{:S(2)}) async-start(bf16[32,16,2048]{2,1,0:T(8,128)(2,1)} %bitcast.84), calls=%async_computation.2 | async-start | bytes 4194304 | tf_op jit(solution)/shard_map/all_to_all | solution.py:203
Sparse Core Ops, SparseCore 0:
  9.5 42.5 all-gather.2
  54.2 60.0 all-gather.4

commit v13 on v11

--- a/solution.py
+++ b/solution.py
@@ -163,6 +163,7 @@
         tiled=True,
     )
     my_blocks, value_out = lax.optimization_barrier((my_blocks, value_out))
+    my_blocks, expert_in, expert_out = lax.optimization_barrier((my_blocks, expert_in, expert_out))
     pair = [(i, i ^ 1) for i in range(seq_count)]
     my_part = lax.dynamic_slice_in_dim(value_out, core * half_rows, half_rows, axis=1)
     other_part = lax.dynamic_slice_in_dim(value_out, (1 - core) * half_rows, half_rows, axis=1)

time: 224 us -> 235 us (1.049)
  local copies, waits for them, and re-layouts: 11.4 us -> 15.9 us
    all_gather x1, waiting for transfers between devices: 29.2 us -> 32.9 us  [local(): key_stack = lax.all_gather(key_stack, 'seq', axis=1, tiled=True)]
  transfers between devices with their start and end apart: 6 -> 6, of which waited for: 3 -> 3; matrix products, arithmetic and copies ran while one was open for 12% -> 12% of each run, Pallas kernels for 5% -> 4%
where the time goes in v13:
time: 235 us; the launch traced here: 234 us
  waiting for transfers between devices  80.9 us (34%)
  blocking collectives  58.7 us (25%)
  starting transfers between devices  22.4 us (10%)
  Pallas kernels  20.7 us (9%)
  local copies, waits for them, and re-layouts  15.9 us (7%)
  between operations  13.7 us (6%)
  other arithmetic  11.1 us (5%)
  matrix products  10.5 us (4%)
    all_to_all x1, blocking collectives, local(): lax.all_to_all(outgoing, 'expert', split_axis=0, concat_axis=0, tiled=True)  58.7 us
    all_to_all x1, waiting for transfers between devices, local(): lax.all_to_all(produced.reshape(-1, capacity, model_width), 'expert', spl...  47.9 us
    all_gather x1, waiting for transfers between devices, local(): key_stack = lax.all_gather(key_stack, 'seq', axis=1, tiled=True)  32.9 us
    pallas_call x1, Pallas kernels, expert_ffn(): pl.pallas_call(functools.partial(expert_kernel, in_width=in_width), out_s...  10.6 us
    all_to_all x1, starting transfers between devices, local(): lax.all_to_all(jnp.broadcast_to(my_rows[None], (expert_devices,) + my_row...  10.2 us
    pallas_call x1, Pallas kernels, attend(): pl.pallas_call(functools.partial(attention_kernel, heads=heads, latent_wi...  10 us
    all_to_all x1, starting transfers between devices, local(): lax.all_to_all(produced.reshape(-1, capacity, model_width), 'expert', spl...  7.66 us
  transfers between devices with their start and end apart: 6, of which 3 were waited for; matrix products, arithmetic and copies ran while one was open for 12% of the time, Pallas kernels for 4%

profile of v13, /device:TPU:16, one launch (start us, length us, event | category | flops | bytes accessed | tf_op | source)
XLA Modules:
  0.0 233.8 jit_solution(2315931006763625362)
XLA Ops:
  6.5 0.0 all-gather.3.cloned.1.call-start
  6.5 1.8 pad_maximum_fusion.1
  8.3 0.0 all-gather.3.cloned.1.call-update
  8.4 0.8 constant_dynamic-slice_fusion.1
  9.2 1.6 broadcast_in_dim.36
  10.8 10.2 %all-to-all-start = ((bf16[32,512,64]{1,2,0:T(8,128)(2,1)}), bf16[32,512,64]{1,2,0:T(8,128)(2,1)S(1)}, u32[]{:S(2)}, u32[]{:S(2)}) async-start(bf16[32,512,64]{1,2,0:T(8,128)(2,1)} %broadcast_in_dim.36), calls=%async_computation | async-start | bytes 4194304 | tf_op jit(solution)/shard_map/all_to_all | solution.py:158
  21.0 0.0 all-gather.5.cloned.1.call-start
  21.0 2.4 %reshape_reshape_squeeze.3.q_ref = bf16[512,576]{1,0:T(8,128)(2,1)} reshape(bf16[1,64,4608]{2,1,0:T(8,128)(2,1)} %param.14) | data formatting | bytes 1179648 | tf_op jit(solution)/shard_map/reshape;reshape;squeeze | solution.py:144
  23.4 0.2 reduce-window.18
  23.6 0.1 convert_reduce_fusion.1
  23.7 0.1 convert_reduce_fusion.2
  23.8 0.1 fusion.4
  23.9 0.2 copy.51
  24.2 0.1 select_reduce_fusion.2
  24.3 0.1 iota_compare_fusion.6
  24.3 0.2 broadcast_in_dim.44
  24.5 0.6 add_convert_fusion
  25.2 1.4 copy.70
  26.5 32.9 %all-gather.3.cloned.1.call-done = bf16[3,1024,576]{2,1,0:T(8,128)(2,1)} async-done(((bf16[3,64,576]{2,1,0:T(8,128)(2,1)}), bf16[3,1024,576]{2,1,0:T(8,128)(2,1)}) %all-gather.3.cloned.1.call-update) | async-done | bytes 3538960 | tf_op jit(solution)/shard_map/all_gather | solution.py:130
  59.4 10.0 %shard_map.127 = bf16[512,512]{1,0:T(8,128)(2,1)} custom-call(bf16[512,576]{1,0:T(8,128)(2,1)} %reshape_reshape_squeeze.3.q_ref, bf16[3072,576]{1,0:T(8,128)(2,1)} %bitcast.92, f32[64,3072]{1,0:T(8,128)} %bitcast.82), custom_call_target="tpu_custom_call" | custom-call | flops 3422552064 | bytes 5439488 | tf_op jit(solution)/shard_map/pallas_call | solution.py:58
  69.4 0.0 copy-done
  69.4 1.4 fusion.2
  70.9 0.0 copy-start.5
  70.9 0.1 all-to-all-done
  71.0 1.1 copy.64
  72.1 1.8 pad_maximum_fusion
  73.9 0.0 all-gather.5.cloned.1.call-update
  74.0 0.7 copy.56
  74.7 0.9 eq.121
  75.6 0.9 eq.125
  76.5 0.6 fusion.13
  77.1 2.6 %reduce-window.19 = s32[32,3,128]{2,0,1:T(8,128)} reduce-window(s32[32,3,128]{2,0,1:T(8,128)} %fusion.13, s32[]{:T(128)} %constant.20.clone.1), window={size=1x1x128 pad=0_0x0_0x127_0}, to_apply=%region_4.5 | reduce-window | flops 1560576 | bytes 98308 | tf_op jit(solution)/shard_map/reduce-window.1
  79.7 1.0 slice_reduce_fusion
  80.8 0.6 constant_dynamic-slice_fusion
  81.4 2.1 collective-permute-start
  83.5 0.9 fusion.12
  84.4 0.7 reshape.206
  85.1 0.8 copy.63
  85.9 0.0 collective-permute-done
  85.9 2.6 %fusion.5 = f32[64,32,64]{0,2,1:T(8,128)} fusion(bf16[32,512,64]{1,2,0:T(8,128)(2,1)S(1)} %all-to-all-done, bf16[64,512]{1,0:T(8,128)(2,1)} %collective-permute-done), kind=kOutput, calls=%fused_computation.22 | convolution fusion | flops 134217728 | bytes 2686976 | tf_op jit(solution)/shard_map/tr,jrc->tjc/dot_general | solution.py:171
  88.5 0.0 copy-done.5
  88.5 2.4 %collective-permute-start.1 = (f32[64,32,64]{0,2,1:T(8,128)}, f32[64,32,64]{0,2,1:T(8,128)}, u32[]{:S(2)}, u32[]{:S(2)}) collective-permute-start(f32[64,32,64]{0,2,1:T(8,128)} %fusion.5), channel_id=1, source_target_pairs={{0,32},{32,0},{64,96},{96,64},{128,160},{160,128},{192,224},{224,1... | collective-permute-start | bytes 1572872 | tf_op jit(solution)/shard_map/ppermute | solution.py:176
  91.0 1.2 copy.62
  92.1 0.1 convert_reduce_fusion
  92.3 1.6 fusion.8
  93.9 0.0 collective-permute-done.1
  93.9 0.0 copy-done.2
  93.9 0.0 copy-start.8
  94.0 1.6 multiply_reduce_fusion
  95.5 0.3 copy.55
  95.8 0.0 copy-start.1
  95.9 0.1 multiply_convert_fusion
  96.0 0.0 copy-start.4
  96.0 0.7 copy-done.4
  96.7 0.7 convolution_convert_fusion
  97.4 58.7 %all_to_all.15 = bf16[32,16,2048]{2,1,0:T(8,128)(2,1)} all-to-all(bf16[32,16,2048]{2,1,0:T(8,128)(2,1)S(1)} %bitcast.76), channel_id=1, replica_groups=mesh['seq'=16,'expert'=32] {'expert'}, dimensions={0} | all-to-all | bytes 4194304 | tf_op jit(solution)/shard_map/all_to_all | solution.py:200
  156.2 10.6 %shard_map.128 = bf16[512,2048]{1,0:T(8,128)(2,1)} custom-call(bf16[512,2048]{1,0:T(8,128)(2,1)} %bitcast.81, bf16[2048,2112]{1,0:T(8,128)(2,1)} %bitcast.91), custom_call_target="tpu_custom_call" | custom-call | flops 4429185024 | bytes 12845056 | tf_op jit(solution)/shard_map/pallas_call | solution.py:84
  166.8 7.7 %all-to-all-start.2 = ((bf16[32,16,2048]{2,1,0:T(8,128)(2,1)}), bf16[32,16,2048]{2,1,0:T(8,128)(2,1)S(1)}, u32[]{:S(2)}, u32[]{:S(2)}) async-start(bf16[32,16,2048]{2,1,0:T(8,128)(2,1)} %bitcast.80), calls=%async_computation.2 | async-start | bytes 4194304 | tf_op jit(solution)/shard_map/all_to_all | solution.py:207
  174.5 0.1 reshape.205
  174.6 0.1 copy.60
  174.7 1.2 fusion.18
  176.0 0.2 select_reduce_fusion
  176.2 47.9 %all-to-all-done.2 = bf16[32,16,2048]{2,1,0:T(8,128)(2,1)S(1)} async-done(((bf16[32,16,2048]{2,1,0:T(8,128)(2,1)}), bf16[32,16,2048]{2,1,0:T(8,128)(2,1)S(1)}, u32[]{:S(2)}, u32[]{:S(2)}) %all-to-all-start.2) | async-done | bytes 2097184 | tf_op jit(solution)/shard_map/all_to_all | solution.py:207
  224.1 3.0 %fusion.1 = bf16[1,64,2048]{2,1,0:T(8,128)(2,1)} fusion(f32[64,512]{1,0:T(8,128)S(1)} %select_reduce_fusion, bf16[512,2048]{1,0:T(8,128)(2,1)S(1)} %bitcast.75, f32[64,2048]{1,0:T(8,128)} %copy-done.1, bf16[1,64,2048]{2,1,0:T(8,128)(2,1)S(1)} %copy-done.3), kind=kOutput, calls=%fused_computation.3 | convolution fusion | flops 805830656 | bytes 3276800 | tf_op jit(solution)/shard_map/dot_general | solution.py:219
  (26 shorter events, 0.2 us)
Async XLA Ops:
  6.5 62.9 %copy-start = (bf16[8,512,128]{2,1,0:T(8,128)(2,1)S(1)}, bf16[8,512,128]{2,1,0:T(8,128)(2,1)}, u32[]{:S(2)}) copy-start(bf16[8,512,128]{2,1,0:T(8,128)(2,1)} %param.19) | copy-start | bytes 3145732
  6.5 52.8 %all-gather.3.cloned.1.call-start = ((), (), s32[]{:S(2)}) async-start(), calls=%async_computation.3 | async-start | bytes 4177920 | tf_op jit(solution)/shard_map/all_gather | solution.py:130
  10.8 12.6 %copy-start.9 = (s32[1,4]{1,0:T(1,128)S(1)}, s32[1,4]{1,0:T(1,128)}, u32[]{:S(2)}) copy-start(s32[1,4]{1,0:T(1,128)} %param.17) | copy-start | bytes 52
  10.8 13.4 %copy-start.10 = (s32[1,4]{1,0:T(1,128)S(1)}, s32[1,4]{1,0:T(1,128)}, u32[]{:S(2)}) copy-start(s32[1,4]{1,0:T(1,128)} %param.18) | copy-start | bytes 52
  10.8 60.2 %all-to-all-start = ((bf16[32,512,64]{1,2,0:T(8,128)(2,1)}), bf16[32,512,64]{1,2,0:T(8,128)(2,1)S(1)}, u32[]{:S(2)}, u32[]{:S(2)}) async-start(bf16[32,512,64]{1,2,0:T(8,128)(2,1)} %broadcast_in_dim.36), calls=%async_computation | async-start | bytes 4194304 | tf_op jit(solution)/shard_map/all_to_all | solution.py:158
  21.0 135.2 %all-gather.5.cloned.1.call-start = ((), (), s32[]{:S(2)}) async-start(), calls=%async_computation.4 | async-start | bytes 9469952 | tf_op jit(solution)/shard_map/all_gather | solution.py:202
  69.4 4.5 %copy-start.7 = (s32[1,64,6]{1,0,2:T(1,128)S(1)}, s32[1,64,6]{1,0,2:T(1,128)}, u32[]{:S(2)}) copy-start(s32[1,64,6]{1,0,2:T(1,128)} %param.23) | copy-start | bytes 4612
  70.9 17.6 %copy-start.5 = (bf16[8,8,8,128]{3,2,0,1:T(8,128)(2,1)}, bf16[8,8,8,128]{3,2,0,1:T(8,128)(2,1)S(1)}, u32[]{:S(2)}) copy-start(bf16[8,8,8,128]{3,2,0,1:T(8,128)(2,1)S(1)} %copy.77) | copy-start | bytes 393220
  73.9 17.0 %copy-start.3 = (bf16[1,64,2048]{2,1,0:T(8,128)(2,1)S(1)}, bf16[1,64,2048]{2,1,0:T(8,128)(2,1)}, u32[]{:S(2)}) copy-start(bf16[1,64,2048]{2,1,0:T(8,128)(2,1)} %param.13) | copy-start | bytes 786436
  81.4 4.6 %collective-permute-start = (bf16[64,512]{1,0:T(8,128)(2,1)}, bf16[64,512]{1,0:T(8,128)(2,1)}, u32[]{:S(2)}, u32[]{:S(2)}) collective-permute-start(bf16[64,512]{1,0:T(8,128)(2,1)} %constant_dynamic-slice_fusion), channel_id=1, source_target_pairs={{0,32},{32,0},{64,96},{96,64},{128,160},{160,128},{192,224},{224,1... | collective-permute-start | bytes 196616 | tf_op jit(solution)/shard_map/ppermute | solution.py:170
  88.5 5.4 %collective-permute-start.1 = (f32[64,32,64]{0,2,1:T(8,128)}, f32[64,32,64]{0,2,1:T(8,128)}, u32[]{:S(2)}, u32[]{:S(2)}) collective-permute-start(f32[64,32,64]{0,2,1:T(8,128)} %fusion.5), channel_id=1, source_target_pairs={{0,32},{32,0},{64,96},{96,64},{128,160},{160,128},{192,224},{224,1... | collective-permute-start | bytes 1572872 | tf_op jit(solution)/shard_map/ppermute | solution.py:176
  92.1 1.8 copy-start.2
  93.9 1.9 copy-start.8
  95.8 60.3 %copy-start.1 = (f32[64,2048]{1,0:T(8,128)}, f32[64,2048]{1,0:T(8,128)S(1)}, u32[]{:S(2)}) copy-start(f32[64,2048]{1,0:T(8,128)S(1)} %copy.55) | copy-start | bytes 1572868
  96.0 0.7 copy-start.4
  166.8 7.8 %copy-start.6 = (s32[1,64,6]{2,1,0:T(8,128)S(1)}, s32[1,64,6]{2,1,0:T(8,128)}, u32[]{:S(2)}) copy-start(s32[1,64,6]{2,1,0:T(8,128)} %copy.56) | copy-start | bytes 4612
  166.8 57.3 %all-to-all-start.2 = ((bf16[32,16,2048]{2,1,0:T(8,128)(2,1)}), bf16[32,16,2048]{2,1,0:T(8,128)(2,1)S(1)}, u32[]{:S(2)}, u32[]{:S(2)}) async-start(bf16[32,16,2048]{2,1,0:T(8,128)(2,1)} %bitcast.80), calls=%async_computation.2 | async-start | bytes 4194304 | tf_op jit(solution)/shard_map/all_to_all | solution.py:207
Sparse Core Ops, SparseCore 0:
  9.5 49.8 all-gather.2
  74.1 62.3 all-gather.4

commit v14 on v11

--- a/solution.py
+++ b/solution.py
@@ -215,12 +215,14 @@
         jnp.where(cell_index[:, :, None] == cell_ids[None, None, :], gate_values[:, :, None], 0.0),
         axis=1,
     )
-    routed_sum = jnp.dot(
-        combining,
-        returned_rows.astype(jnp.float32),
-        precision=lax.Precision.HIGHEST,
-        preferred_element_type=jnp.float32,
-    )
+    routed_sum = jnp.zeros((local_tokens, model_width), jnp.float32)
+    rest = combining
+    for _ in range(3):
+        part = rest.astype(jnp.bfloat16)
+        rest = rest - part.astype(jnp.float32)
+        routed_sum = routed_sum + jnp.dot(
+            part, returned_rows, preferred_element_type=jnp.float32
+        )
     layer_out = (residual + routed_sum).astype(jnp.bfloat16)
     return layer_out[None]
 

time: 224 us -> 224 us (level)
  no operation moved by 1% of the time
where the time goes in v14:
time: 224 us
  waiting for transfers between devices  79.6 us (36%)
  blocking collectives  56.6 us (25%)
  starting transfers between devices  22.3 us (10%)
  Pallas kernels  20.7 us (9%)
  between operations  13.8 us (6%)
  local copies, waits for them, and re-layouts  12 us (5%)
  matrix products  9.68 us (4%)
  other arithmetic  8.83 us (4%)
    all_to_all x1, blocking collectives, local(): lax.all_to_all(outgoing, 'expert', split_axis=0, concat_axis=0, tiled=True)  56.6 us
    all_to_all x1, waiting for transfers between devices, local(): lax.all_to_all(produced.reshape(-1, capacity, model_width), 'expert', spl...  48.1 us
    all_gather x1, waiting for transfers between devices, local(): key_stack = lax.all_gather(key_stack, 'seq', axis=1, tiled=True)  29.2 us
    pallas_call x1, Pallas kernels, expert_ffn(): pl.pallas_call(functools.partial(expert_kernel, in_width=in_width), out_s...  10.6 us
    all_to_all x1, starting transfers between devices, local(): lax.all_to_all(jnp.broadcast_to(my_rows[None], (expert_devices,) + my_row...  10.2 us
    pallas_call x1, Pallas kernels, attend(): pl.pallas_call(functools.partial(attention_kernel, heads=heads, latent_wi...  10.1 us
    all_to_all x1, starting transfers between devices, local(): lax.all_to_all(produced.reshape(-1, capacity, model_width), 'expert', spl...  7.64 us
  transfers between devices with their start and end apart: 6, of which 3 were waited for; matrix products, arithmetic and copies ran while one was open for 12% of the time, Pallas kernels for 5%

profile of v14, /device:TPU:16, one launch (start us, length us, event | category | flops | bytes accessed | tf_op | source)
XLA Modules:
  0.0 223.5 jit_solution(1050592037683706486)
XLA Ops:
  6.5 0.0 copy-start
  6.5 1.8 pad_maximum_fusion.1
  8.3 0.0 all-gather.3.cloned.1.call-update
  8.4 0.0 all-gather.5.cloned.1.call-start
  8.4 1.1 copy.64
  9.5 1.9 pad_maximum_fusion
  11.3 0.0 all-gather.5.cloned.1.call-update
  11.4 0.0 copy-done.11
  11.4 1.6 broadcast_in_dim.36
  13.0 10.2 %all-to-all-start = ((bf16[32,512,64]{1,2,0:T(8,128)(2,1)}), bf16[32,512,64]{1,2,0:T(8,128)(2,1)S(1)}, u32[]{:S(2)}, u32[]{:S(2)}) async-start(bf16[32,512,64]{1,2,0:T(8,128)(2,1)} %broadcast_in_dim.36), calls=%async_computation | async-start | bytes 4194304 | tf_op jit(solution)/shard_map/all_to_all | solution.py:158
  23.2 0.1 copy.56
  23.3 0.1 eq.125
  23.4 0.1 eq.121
  23.6 0.2 reduce-window.18
  23.8 0.1 convert_reduce_fusion.1
  23.9 0.1 convert_reduce_fusion.2
  23.9 0.1 fusion.5
  24.1 0.2 copy.51
  24.3 0.1 select_reduce_fusion.2
  24.4 0.1 iota_compare_fusion.6
  24.5 0.2 broadcast_in_dim.44
  24.7 0.6 add_convert_fusion
  25.3 1.4 copy.70
  26.7 2.4 %reshape_reshape_squeeze.3.q_ref = bf16[512,576]{1,0:T(8,128)(2,1)} reshape(bf16[1,64,4608]{2,1,0:T(8,128)(2,1)} %param.14) | data formatting | bytes 1179648 | tf_op jit(solution)/shard_map/reshape;reshape;squeeze | solution.py:144
  29.0 0.9 reduce-window.19
  29.9 0.2 slice_reduce_fusion
  30.2 29.2 %all-gather.3.cloned.1.call-done = bf16[3,1024,576]{2,1,0:T(8,128)(2,1)} async-done(((bf16[3,64,576]{2,1,0:T(8,128)(2,1)}), bf16[3,1024,576]{2,1,0:T(8,128)(2,1)}) %all-gather.3.cloned.1.call-update) | async-done | bytes 3538960 | tf_op jit(solution)/shard_map/all_gather | solution.py:130
  59.4 10.1 %shard_map.127 = bf16[512,512]{1,0:T(8,128)(2,1)} custom-call(bf16[512,576]{1,0:T(8,128)(2,1)} %reshape_reshape_squeeze.3.q_ref, bf16[3072,576]{1,0:T(8,128)(2,1)} %bitcast.95, f32[64,3072]{1,0:T(8,128)} %bitcast.85), custom_call_target="tpu_custom_call" | custom-call | flops 3422552064 | bytes 5439488 | tf_op jit(solution)/shard_map/pallas_call | solution.py:58
  69.5 1.4 fusion.3
  70.9 0.0 copy-start.4
  71.0 0.0 copy-start.7
  71.0 2.2 all-to-all-done
  73.2 0.6 constant_dynamic-slice_fusion
  73.8 1.9 collective-permute-start
  75.8 0.9 fusion.17
  76.6 0.8 reshape.206
  77.4 0.8 copy.63
  78.2 0.0 collective-permute-done
  78.2 2.6 %fusion.10 = f32[64,32,64]{0,2,1:T(8,128)} fusion(bf16[32,512,64]{1,2,0:T(8,128)(2,1)S(1)} %all-to-all-done, bf16[64,512]{1,0:T(8,128)(2,1)} %collective-permute-done), kind=kOutput, calls=%fused_computation.29 | convolution fusion | flops 134217728 | bytes 2686976 | tf_op jit(solution)/shard_map/tr,jrc->tjc/dot_general | solution.py:170
  80.8 2.6 %collective-permute-start.1 = (f32[64,32,64]{0,2,1:T(8,128)}, f32[64,32,64]{0,2,1:T(8,128)}, u32[]{:S(2)}, u32[]{:S(2)}) collective-permute-start(f32[64,32,64]{0,2,1:T(8,128)} %fusion.10), channel_id=1, source_target_pairs={{0,32},{32,0},{64,96},{96,64},{128,160},{160,128},{192,224},{224,1... | collective-permute-start | bytes 1572872 | tf_op jit(solution)/shard_map/ppermute | solution.py:175
  83.4 1.2 copy.62
  84.6 0.1 convert_reduce_fusion
  84.7 1.7 fusion.13
  86.4 0.0 collective-permute-done.1
  86.4 0.0 copy-start.5
  86.5 0.0 copy-start.13
  86.5 1.6 multiply_reduce_fusion
  88.1 0.3 copy.55
  88.5 0.1 multiply_convert_fusion
  88.6 0.7 convolution_convert_fusion
  89.3 56.6 %all_to_all.15 = bf16[32,16,2048]{2,1,0:T(8,128)(2,1)} all-to-all(bf16[32,16,2048]{2,1,0:T(8,128)(2,1)S(1)} %bitcast.79), channel_id=1, replica_groups=mesh['seq'=16,'expert'=32] {'expert'}, dimensions={0} | all-to-all | bytes 4194304 | tf_op jit(solution)/shard_map/all_to_all | solution.py:199
  145.9 10.6 %shard_map.128 = bf16[512,2048]{1,0:T(8,128)(2,1)} custom-call(bf16[512,2048]{1,0:T(8,128)(2,1)} %bitcast.84, bf16[2048,2112]{1,0:T(8,128)(2,1)} %bitcast.94), custom_call_target="tpu_custom_call" | custom-call | flops 4429185024 | bytes 12845056 | tf_op jit(solution)/shard_map/pallas_call | solution.py:84
  156.5 7.6 %all-to-all-start.2 = ((bf16[32,16,2048]{2,1,0:T(8,128)(2,1)}), bf16[32,16,2048]{2,1,0:T(8,128)(2,1)S(1)}, u32[]{:S(2)}, u32[]{:S(2)}) async-start(bf16[32,16,2048]{2,1,0:T(8,128)(2,1)} %bitcast.83), calls=%async_computation.2 | async-start | bytes 4194304 | tf_op jit(solution)/shard_map/all_to_all | solution.py:206
  164.1 0.1 reshape.205
  164.3 0.1 copy.60
  164.4 1.1 fusion.23
  165.6 0.2 select_reduce_fusion
  165.8 48.1 %all-to-all-done.2 = bf16[32,16,2048]{2,1,0:T(8,128)(2,1)S(1)} async-done(((bf16[32,16,2048]{2,1,0:T(8,128)(2,1)}), bf16[32,16,2048]{2,1,0:T(8,128)(2,1)S(1)}, u32[]{:S(2)}, u32[]{:S(2)}) %all-to-all-start.2) | async-done | bytes 2097184 | tf_op jit(solution)/shard_map/all_to_all | solution.py:206
  213.9 0.5 fusion.7
  214.4 0.0 copy-start.6
  214.4 0.5 convolution_add_fusion.1
  214.9 0.5 copy-done.2
  215.4 0.1 copy-done.6
  215.5 1.2 fusion.2
  (38 shorter events, 0.2 us)
Async XLA Ops:
  6.5 63.0 %copy-start = (bf16[8,512,128]{2,1,0:T(8,128)(2,1)S(1)}, bf16[8,512,128]{2,1,0:T(8,128)(2,1)}, u32[]{:S(2)}) copy-start(bf16[8,512,128]{2,1,0:T(8,128)(2,1)} %param.19) | copy-start | bytes 3145732
  6.5 4.8 %copy-start.11 = (bf16[1024,64]{0,1:T(8,128)(2,1)S(1)}, bf16[1024,64]{0,1:T(8,128)(2,1)}, u32[]{:S(2)}) copy-start(bf16[1024,64]{0,1:T(8,128)(2,1)} %param.20) | copy-start | bytes 393220
  6.5 52.9 %all-gather.3.cloned.1.call-start = ((), (), s32[]{:S(2)}) async-start(), calls=%async_computation.3 | async-start | bytes 4177920 | tf_op jit(solution)/shard_map/all_gather | solution.py:130
  8.4 137.5 %all-gather.5.cloned.1.call-start = ((), (), s32[]{:S(2)}) async-start(), calls=%async_computation.4 | async-start | bytes 9469952 | tf_op jit(solution)/shard_map/all_gather | solution.py:201
  13.0 10.2 %copy-start.12 = (s32[1,64,6]{1,0,2:T(1,128)S(1)}, s32[1,64,6]{1,0,2:T(1,128)}, u32[]{:S(2)}) copy-start(s32[1,64,6]{1,0,2:T(1,128)} %param.23) | copy-start | bytes 4612
  13.0 10.6 %copy-start.14 = (s32[1,4]{1,0:T(1,128)S(1)}, s32[1,4]{1,0:T(1,128)}, u32[]{:S(2)}) copy-start(s32[1,4]{1,0:T(1,128)} %param.17) | copy-start | bytes 52
  13.0 11.3 %copy-start.15 = (s32[1,4]{1,0:T(1,128)S(1)}, s32[1,4]{1,0:T(1,128)}, u32[]{:S(2)}) copy-start(s32[1,4]{1,0:T(1,128)} %param.18) | copy-start | bytes 52
  13.0 60.2 %all-to-all-start = ((bf16[32,512,64]{1,2,0:T(8,128)(2,1)}), bf16[32,512,64]{1,2,0:T(8,128)(2,1)S(1)}, u32[]{:S(2)}, u32[]{:S(2)}) async-start(bf16[32,512,64]{1,2,0:T(8,128)(2,1)} %broadcast_in_dim.36), calls=%async_computation | async-start | bytes 4194304 | tf_op jit(solution)/shard_map/all_to_all | solution.py:158
  23.3 5.7 %copy-start.8 = (s32[1,64,6]{2,1,0:T(8,128)}, s32[1,64,6]{2,1,0:T(8,128)S(1)}, u32[]{:S(2)}) copy-start(s32[1,64,6]{2,1,0:T(8,128)S(1)} %copy.56) | copy-start | bytes 4612
  29.9 39.6 %copy-start.10 = (s32[32,3,128]{2,0,1:T(8,128)}, s32[32,3,128]{2,0,1:T(8,128)S(1)}, u32[]{:S(2)}) copy-start(s32[32,3,128]{2,0,1:T(8,128)S(1)} %reduce-window.19) | copy-start | bytes 147460
  70.9 12.5 %copy-start.4 = (bf16[1,64,2048]{2,1,0:T(8,128)(2,1)S(1)}, bf16[1,64,2048]{2,1,0:T(8,128)(2,1)}, u32[]{:S(2)}) copy-start(bf16[1,64,2048]{2,1,0:T(8,128)(2,1)} %param.13) | copy-start | bytes 786436
  71.0 13.6 %copy-start.7 = (bf16[8,8,8,128]{3,2,0,1:T(8,128)(2,1)}, bf16[8,8,8,128]{3,2,0,1:T(8,128)(2,1)S(1)}, u32[]{:S(2)}) copy-start(bf16[8,8,8,128]{3,2,0,1:T(8,128)(2,1)S(1)} %copy.77) | copy-start | bytes 393220
  73.8 4.4 %collective-permute-start = (bf16[64,512]{1,0:T(8,128)(2,1)}, bf16[64,512]{1,0:T(8,128)(2,1)}, u32[]{:S(2)}, u32[]{:S(2)}) collective-permute-start(bf16[64,512]{1,0:T(8,128)(2,1)} %constant_dynamic-slice_fusion), channel_id=1, source_target_pairs={{0,32},{32,0},{64,96},{96,64},{128,160},{160,128},{192,224},{224,1... | collective-permute-start | bytes 196616 | tf_op jit(solution)/shard_map/ppermute | solution.py:169
  80.8 5.6 %collective-permute-start.1 = (f32[64,32,64]{0,2,1:T(8,128)}, f32[64,32,64]{0,2,1:T(8,128)}, u32[]{:S(2)}, u32[]{:S(2)}) collective-permute-start(f32[64,32,64]{0,2,1:T(8,128)} %fusion.10), channel_id=1, source_target_pairs={{0,32},{32,0},{64,96},{96,64},{128,160},{160,128},{192,224},{224,1... | collective-permute-start | bytes 1572872 | tf_op jit(solution)/shard_map/ppermute | solution.py:175
  84.6 1.8 copy-start.3
  86.4 2.0 copy-start.5
  86.5 2.0 copy-start.13
  88.4 57.5 %copy-start.1 = (f32[64,2048]{1,0:T(8,128)}, f32[64,2048]{1,0:T(8,128)S(1)}, u32[]{:S(2)}) copy-start(f32[64,2048]{1,0:T(8,128)S(1)} %copy.55) | copy-start | bytes 1572868
  156.5 7.8 %copy-start.9 = (s32[1,64,6]{2,1,0:T(8,128)S(1)}, s32[1,64,6]{2,1,0:T(8,128)}, u32[]{:S(2)}) copy-start(s32[1,64,6]{2,1,0:T(8,128)} %copy-done.8) | copy-start | bytes 4612
  156.5 57.4 %all-to-all-start.2 = ((bf16[32,16,2048]{2,1,0:T(8,128)(2,1)}), bf16[32,16,2048]{2,1,0:T(8,128)(2,1)S(1)}, u32[]{:S(2)}, u32[]{:S(2)}) async-start(bf16[32,16,2048]{2,1,0:T(8,128)(2,1)} %bitcast.83), calls=%async_computation.2 | async-start | bytes 4194304 | tf_op jit(solution)/shard_map/all_to_all | solution.py:206
  214.4 1.0 copy-start.2
  214.4 1.1 copy-start.6
Sparse Core Ops, SparseCore 0:
  9.5 49.8 all-gather.2
  61.6 59.9 all-gather.4
